TPU v7x, 256 devices: a whole 4x4x8 slice. The times are simulated.
256 devices in a mesh: sample: 32 (over x, y, core), slab: 8 (over z).
Axes of the slice: x: 4, y: 4, z: 8, core: 2. Of those that a mesh axis runs over, the one named last changes fastest.
Arguments:
- volume: bfloat16 [4, 32, 32, 4096], P(None, 'sample', 'slab'), may hold values from -6 to 6
- cotangent: bfloat16 [128, 32, 8, 256], P(None, 'sample', 'slab'), may hold values from -0.5 to 0.5
- w_first: bfloat16 [27, 4, 32], replicated, may hold values from -0.625 to 0.625
- b_first: float32 [32], replicated, may hold values from -3 to 3
- w_second: bfloat16 [27, 32, 64], replicated, may hold values from -0.21875 to 0.21875
- b_second: float32 [64], replicated, may hold values from -3 to 3
- w_third: bfloat16 [27, 64, 128], replicated, may hold values from -0.15625 to 0.15625
- b_third: float32 [128], replicated, may hold values from -3 to 3
Outputs:
- features: bfloat16 [128, 32, 8, 256], P(None, 'sample', 'slab')
- kernel_grad_first: float32 [27, 4, 32], replicated
- bias_grad_first: float32 [32], replicated
- kernel_grad_second: float32 [27, 32, 64], replicated
- bias_grad_second: float32 [64], replicated
- kernel_grad_third: float32 [27, 64, 128], replicated
- bias_grad_third: float32 [128], replicated
All inputs are finite; a program needn't handle non-finite values.
Results may differ from a plain program's by a relative error of at most 0.02.
Values may be sent and summed in bfloat16 or wider, within the bound.
No kernel may reach another device: no remote copies, remote signals or barrier semaphores. Data moves between devices by JAX's collectives and lax.ppermute only.
A program may use at most 128 MiB of HBM per device.

v0:
```python
import jax
import jax.numpy as jnp
from jax import lax
from jax.sharding import PartitionSpec as P

SX = 32
CZ = 4


def with_halo(shard, sides, width):
    for axis, dim in sides:
        size, length = (lax.axis_size(axis), shard.shape[dim])
        up = [(i, (i + 1) % size) for i in range(size - 1)]
        down = [(j, i) for i, j in up]
        last = lax.slice_in_dim(shard, length - width, length, axis=dim)
        first = lax.slice_in_dim(shard, 0, width, axis=dim)
        before = lax.ppermute(last, axis, up)
        after = lax.ppermute(first, axis, down)
        shard = jnp.concatenate([before, shard, after], axis=dim)
    return shard


def silu_slope(values):
    sigmoid = jax.nn.sigmoid(values)
    return sigmoid * (1.0 + values * (1.0 - sigmoid))


def put_block(values, update, sample, depth_start):
    return lax.dynamic_update_slice(values, update, (0, sample, depth_start, 0))


def gather_taps(section, row_width):
    depth_len = section.shape[2] - 2
    plane_size = section.shape[3]
    flattened = jnp.pad(section, ((0, 0), (0, 0), (0, 0), (row_width + 1, row_width + 1)))
    column = lax.broadcasted_iota(jnp.int32, (1, 1, 1, plane_size), 3) % row_width
    left_mask = (column >= 1).astype(section.dtype)
    right_mask = (column <= row_width - 2).astype(section.dtype)
    pieces = []
    for tap_index in range(27):
        depth_start = tap_index // 9
        row_step = tap_index // 3 % 3 - 1
        col_step = tap_index % 3 - 1
        offset = row_width + 1 + row_step * row_width + col_step
        shifted = flattened[
            :, :, depth_start : depth_start + depth_len, offset : offset + plane_size
        ]
        if col_step < 0:
            shifted = shifted * left_mask
        elif col_step > 0:
            shifted = shifted * right_mask
        pieces.append(shifted)
    return jnp.concatenate(pieces, axis=0)


def apply_weight(patches, weight):
    flat_weight = weight.reshape(weight.shape[0] * weight.shape[1], weight.shape[2])
    return jnp.einsum("ko,kgzp->ogzp", flat_weight, patches, preferred_element_type=jnp.float32)


def weight_term(patches, grad_block, in_channels):
    summed = jnp.einsum("kgzp,ogzp->ko", patches, grad_block, preferred_element_type=jnp.float32)
    return summed.reshape(27, in_channels, grad_block.shape[0])


def pool_cells(values, row_width):
    channels, samples, depth_len, plane_size = values.shape
    row_count = plane_size // row_width
    grouped = values.reshape(
        channels, samples, depth_len // 2, 2, row_count // 2, 2, row_width // 2, 2
    )
    return grouped.mean(axis=(3, 5, 7)).reshape(channels, samples, depth_len // 2, plane_size // 4)


def spread_cells(values, coarse_width):
    channels, samples, depth_len, plane_size = values.shape
    row_count = plane_size // coarse_width
    grouped = values.reshape(channels, samples, depth_len, 1, row_count, 1, coarse_width, 1)
    grouped = jnp.broadcast_to(
        grouped, (channels, samples, depth_len, 2, row_count, 2, coarse_width, 2)
    )
    return grouped.reshape(channels, samples, 2 * depth_len, 4 * plane_size) * 0.125


def forward_layer(padded, weight, bias_values, row_width, depth_block, pooled_out):
    out_channels = weight.shape[2]
    samples, depth_total, plane_size = (padded.shape[1], padded.shape[2] - 2, padded.shape[3])
    per_sample = depth_total // depth_block
    pre_buffer = jnp.zeros((out_channels, samples, depth_total, plane_size), jnp.bfloat16)
    if pooled_out:
        out_buffer = jnp.zeros(
            (out_channels, samples, depth_total // 2, plane_size // 4), jnp.bfloat16
        )
    else:
        out_buffer = jnp.zeros_like(pre_buffer)

    def forward_block_step(block_index, buffers):
        sample = block_index // per_sample
        depth_start = block_index % per_sample * depth_block
        pre_values = (
            apply_weight(gather_taps(padded, row_width), weight) + bias_values[:, None, None, None]
        ).astype(jnp.bfloat16)
        activated = jax.nn.silu(pre_values.astype(jnp.float32))
        if pooled_out:
            result = put_block(
                buffers[1],
                pool_cells(activated, row_width).astype(jnp.bfloat16),
                sample,
                depth_start // 2,
            )
        else:
            result = put_block(buffers[1], activated.astype(jnp.bfloat16), sample, depth_start)
        return (put_block(buffers[0], pre_values, sample, depth_start), result)

    return lax.fori_loop(0, samples * per_sample, forward_block_step, (pre_buffer, out_buffer))


def weight_grads(padded, delta_values, row_width, depth_block, weight):
    samples, depth_total = (delta_values.shape[1], delta_values.shape[2])
    per_sample = depth_total // depth_block
    in_channels = weight.shape[1]

    def weight_block_step(block_index, summed):
        return summed + weight_term(gather_taps(padded, row_width), delta_values, in_channels)

    return lax.fori_loop(
        0, samples * per_sample, weight_block_step, jnp.zeros(weight.shape, jnp.float32)
    )


def data_grads(padded, flipped, row_width, depth_block):
    out_channels = flipped.shape[2]
    samples, depth_total, plane_size = (padded.shape[1], padded.shape[2] - 2, padded.shape[3])
    per_sample = depth_total // depth_block
    out_buffer = jnp.zeros((out_channels, samples, depth_total, plane_size), jnp.bfloat16)

    def data_block_step(block_index, buffer_now):
        sample = block_index // per_sample
        depth_start = block_index % per_sample * depth_block
        result = apply_weight(gather_taps(padded, row_width), flipped).astype(jnp.bfloat16)
        return put_block(buffer_now, result, sample, depth_start)

    return lax.fori_loop(0, samples * per_sample, data_block_step, out_buffer)


def bias_sum(delta_values):
    return jnp.sum(delta_values, axis=(1, 2, 3), dtype=jnp.float32)


def per_device(volume, cotangent, w_first, b_first, w_second, b_second, w_third, b_third):
    flipped_second = jnp.flip(w_second, 0).transpose(0, 2, 1)
    flipped_third = jnp.flip(w_third, 0).transpose(0, 2, 1)
    volume_padded = with_halo(volume, (("slab", 2),), 1)
    first_pre, first_pooled = forward_layer(volume_padded, w_first, b_first, SX, CZ, True)
    first_padded = with_halo(first_pooled, (("slab", 2),), 1)
    second_pre, second_pooled = forward_layer(
        first_padded, w_second, b_second, SX // 2, CZ // 2, True
    )
    coarse_depth = second_pooled.shape[2]
    third_padded = with_halo(second_pooled, (("slab", 2),), 1)
    third_pre, features = forward_layer(
        third_padded, w_third, b_third, SX // 4, coarse_depth, False
    )
    third_delta = (
        cotangent.astype(jnp.float32) * silu_slope(third_pre.astype(jnp.float32))
    ).astype(jnp.bfloat16)
    kernel_third = weight_grads(third_padded, third_delta, SX // 4, coarse_depth, w_third)
    bias_third = bias_sum(third_delta)
    kernel_third, bias_third = lax.psum((kernel_third, bias_third), ("sample", "slab"))
    delta_window = with_halo(third_delta, (("slab", 2),), 1)
    second_back = data_grads(delta_window, flipped_third, SX // 4, coarse_depth)
    second_delta = (
        spread_cells(second_back.astype(jnp.float32), SX // 4)
        * silu_slope(second_pre.astype(jnp.float32))
    ).astype(jnp.bfloat16)
    kernel_second = weight_grads(first_padded, second_delta, SX // 2, CZ // 2, w_second)
    bias_second = bias_sum(second_delta)
    delta_padded = with_halo(second_delta, (("slab", 2),), 1)
    first_back = data_grads(delta_padded, flipped_second, SX // 2, CZ // 2)
    first_delta = (
        spread_cells(first_back.astype(jnp.float32), SX // 2)
        * silu_slope(first_pre.astype(jnp.float32))
    ).astype(jnp.bfloat16)
    kernel_first = weight_grads(volume_padded, first_delta, SX, CZ, w_first)
    bias_first = bias_sum(first_delta)
    kernel_first, bias_first, kernel_second, bias_second = lax.psum(
        (kernel_first, bias_first, kernel_second, bias_second), ("sample", "slab")
    )
    return (
        features,
        kernel_first,
        bias_first,
        kernel_second,
        bias_second,
        kernel_third,
        bias_third,
    )


def solution(mesh):
    in_specs = (
        P(None, "sample", "slab", None),
        P(None, "sample", "slab", None),
        P(),
        P(),
        P(),
        P(),
        P(),
        P(),
    )
    out_specs = (P(None, "sample", "slab", None), P(), P(), P(), P(), P(), P())
    return jax.shard_map(
        per_device, mesh=mesh, in_specs=in_specs, out_specs=out_specs, check_vma=False
    )
```

profile of v0, /device:TPU:1, one launch (start us, length us, event | category | flops | bytes accessed | tf_op | source)
XLA Modules:
  0.0 395.6 jit_solution(9042423092520511804)
XLA Ops:
  7.2 1.0 copy.58
  8.3 4.4 %collective-permute-start = (bf16[4,1,1,4096]{3,0,2,1:T(4,128)(2,1)S(1)}, bf16[4,1,1,4096]{3,0,2,1:T(4,128)(2,1)S(1)}, u32[]{:S(2)}, u32[]{:S(2)}) collective-permute-start(bf16[4,1,1,4096]{3,0,2,1:T(4,128)(2,1)S(1)} %get-tuple-element.223), channel_id=1, source_target_pairs={{0,1},{1,2},{2,3},{3,4},{4,5},{5,6},{6,7},{8,9},{9,10},{10,11},{11... | collective-permute-start | bytes 98312 | tf_op jit(solution)/shard_map/ppermute | solution.py:17
  12.6 1.3 collective-permute-start.1
  14.0 0.6 fusion.115
  14.6 0.9 reverse_bitcast_fusion.1
  15.5 1.0 reverse_bitcast_fusion
  16.6 1.4 reshape.324
  18.0 0.6 copy-done.3
  18.6 0.6 copy-done.5
  19.4 1.3 slice_multiply_fusion.36
  20.7 1.7 slice_multiply_fusion.37
  22.4 16.2 %concatenate.62 = bf16[108,1,4,4096]{3,0,2,1:T(8,128)(2,1)} concatenate(bf16[4,1,4,4096]{3,0,2,1:T(4,128)(2,1)} %get-tuple-element.212, bf16[4,1,4,4096]{3,0,2,1:T(4,128)(2,1)S(1)} %get-tuple-element.218, bf16[4,1,4,4096]{3,0,2,1:T(4,128)(2,1)S(1)} %get-tuple-element.203, bf16[4,1,4,4096]{3,0,2,1:T(4,128)(2,1)} %get-tuple-element.211, ...), dimensions={0} | concatenate | bytes 7077888 | tf_op jit(solution)/shard_map/while/body/eval_jaxpr/concatenate | solution.py:53
  38.6 4.7 %fusion.10 = (f32[32,4,4096]{2,0,1:T(8,128)S(1)}, f32[32,4,4096]{2,0,1:T(8,128)}) fusion(f32[32]{0:T(128)} %param.11, bf16[108,32]{1,0:T(8,128)(2,1)} %reshape.324, bf16[108,1,4,4096]{3,0,2,1:T(8,128)(2,1)} %concatenate.62), kind=kOutput, calls=%fused_computation.14 | convolution fusion | flops 116916224 | bytes 7740288 | tf_op jit(solution)/shard_map/while/body/eval_jaxpr/ko,kgzp->ogzp/dot_general | solution.py:58
  43.2 4.6 %copy.65 = f32[32,4,4096]{0,2,1:T(8,128)} copy(f32[32,4,4096]{2,0,1:T(8,128)S(1)} %get-tuple-element.225) | data formatting | bytes 4194304 | tf_op jit(solution)/shard_map/while/body/eval_jaxpr/jit(silu)/mul | solution.py:103
  47.9 9.5 %reduce_sum.54 = f32[32,2,64,16]{0,3,2,1:T(8,128)S(1)} reduce(f32[32,2,2,64,2,16,2]{0,6,5,4,3,2,1:T(2,128)} %bitcast.123, f32[]{:T(128)} %constant.224.clone.1), dimensions={2,4,6}, to_apply=%region_0.1 | reduce | flops 458752 | bytes 2359300 | tf_op jit(solution)/shard_map/while/body/eval_jaxpr/reduce_sum | solution.py:72
  57.7 4.2 %collective-permute-start.2 = (bf16[32,1,1,1024]{3,0,2,1:T(8,128)(2,1)S(1)}, bf16[32,1,1,1024]{3,0,2,1:T(8,128)(2,1)S(1)}, u32[]{:S(2)}, u32[]{:S(2)}) collective-permute-start(bf16[32,1,1,1024]{3,0,2,1:T(8,128)(2,1)S(1)} %get-tuple-element.219), channel_id=1, source_target_pairs={{0,1},{1,2},{2,3},{3,4},{4,5},{5,6},{6,7},{8,9},{9,10},{10,11},{11... | collective-permute-start | bytes 196616 | tf_op jit(solution)/shard_map/ppermute | solution.py:17
  61.9 1.8 collective-permute-start.3
  63.7 3.3 collective-permute-done.3
  69.8 1.7 copy-done
  71.5 0.9 multiply_reduce_fusion
  72.6 0.4 reduce_sum.57
  73.1 1.3 collective-permute-start.5
  74.4 5.4 %collective-permute-start.4 = (bf16[64,1,1,256]{0,3,2,1:T(8,128)(2,1)S(1)}, bf16[64,1,1,256]{0,3,2,1:T(8,128)(2,1)S(1)}, u32[]{:S(2)}, u32[]{:S(2)}) collective-permute-start(bf16[64,1,1,256]{0,3,2,1:T(8,128)(2,1)S(1)} %fusion.106), channel_id=1, source_target_pairs={{0,1},{1,2},{2,3},{3,4},{4,5},{5,6},{6,7},{8,9},{9,10},{10,11},{11... | collective-permute-start | bytes 98312 | tf_op jit(solution)/shard_map/ppermute | solution.py:17
  79.8 0.7 copy.75
  80.9 6.6 %copy.74 = bf16[108,4096,4]{1,2,0:T(4,128)(2,1)} copy(bf16[108,4096,4]{1,0,2:T(8,128)(2,1)} %bitcast.125) | data formatting | bytes 7077888 | tf_op jit(solution)/shard_map/while/body/eval_jaxpr/kgzp,ogzp->ko/dot_general | solution.py:62
  87.6 0.8 slice_multiply_fusion.72
  88.5 3.4 concatenate.68
  91.8 0.6 copy.83
  92.5 1.4 convert_reduce_fusion.2
  93.9 1.3 collective-permute-start.7
  95.2 5.2 %collective-permute-start.6 = (bf16[128,1,1,256]{0,3,2,1:T(8,128)(2,1)S(1)}, bf16[128,1,1,256]{0,3,2,1:T(8,128)(2,1)S(1)}, u32[]{:S(2)}, u32[]{:S(2)}) collective-permute-start(bf16[128,1,1,256]{0,3,2,1:T(8,128)(2,1)S(1)} %get-tuple-element.156), channel_id=1, source_target_pairs={{0,1},{1,2},{2,3},{3,4},{4,5},{5,6},{6,7},{8,9},{9,10},{10,11},{11... | collective-permute-start | bytes 196616 | tf_op jit(solution)/shard_map/ppermute | solution.py:17
  100.4 1.3 fusion.107
  101.8 0.7 copy.85
  105.1 0.7 fusion.53
  106.6 4.6 %collective-permute-start.8 = (bf16[64,1,1,1024]{3,0,2,1:T(8,128)(2,1)S(1)}, bf16[64,1,1,1024]{3,0,2,1:T(8,128)(2,1)S(1)}, u32[]{:S(2)}, u32[]{:S(2)}) collective-permute-start(bf16[64,1,1,1024]{3,0,2,1:T(8,128)(2,1)S(1)} %get-tuple-element.165), channel_id=1, source_target_pairs={{0,1},{1,2},{2,3},{3,4},{4,5},{5,6},{6,7},{8,9},{9,10},{10,11},{11... | collective-permute-start | bytes 393224 | tf_op jit(solution)/shard_map/ppermute | solution.py:17
  111.1 1.5 collective-permute-start.9
  112.6 3.8 convolution_bitcast_fusion
  116.5 1.6 collective-permute-done.9
  121.8 1.3 fusion.35
  123.5 7.5 %broadcast_in_dim.14 = f32[32,2,2,64,2,16,2]{0,6,5,4,3,2,1:T(2,128)} broadcast(f32[32,2,64,16]{0,3,2,1:T(8,128)S(1)} %bitcast.130), dimensions={0,1,3,5} | broadcast | bytes 2359296 | tf_op jit(solution)/shard_map/broadcast_in_dim | solution.py:79
  131.0 5.3 %copy.81 = f32[32,4,4096]{2,0,1:T(8,128)S(1)} copy(f32[32,4,4096]{0,2,1:T(8,128)} %bitcast.124) | data formatting | bytes 4194304 | tf_op jit(solution)/shard_map/mul | solution.py:82
  136.4 2.7 convert_reduce_fusion
  139.1 3.9 fusion.41
  143.0 85.7 %all-reduce.5 = (f32[27,4,32]{2,0,1:T(8,128)S(1)}, f32[32]{0:T(128)}, f32[64]{0:T(128)}, f32[128]{0:T(128)}) all-reduce(f32[27,4,32]{2,0,1:T(8,128)S(1)} %fusion.41, f32[32]{0:T(128)S(1)} %get-tuple-element.159, f32[64]{0:T(128)S(1)} %get-tuple-element.157, ...), channel_id=1, replica_groups=mesh['sample'=32,'slab'=8] {'sample','slab'}, use_global_device_ids=true, to_apply=%region_3.4 | all-reduce | flops 3680 | bytes 29440 | tf_op jit(solution)/shard_map/psum | solution.py:186
  228.6 0.7 copy.86
  229.3 155.3 %all-reduce.9.cloned.1.call-done = (f32[27,32,64]{2,1,0:T(8,128)}, f32[27,64,128]{2,1,0:T(8,128)}) async-done(((f32[27,32,64]{2,1,0:T(8,128)}, f32[27,64,128]{2,1,0:T(8,128)}), (f32[27,32,64]{2,1,0:T(8,128)}, f32[27,64,128]{2,1,0:T(8,128)})) %all-reduce.9.cloned.1.call-update) | async-done | bytes 1105936 | tf_op jit(solution)/shard_map/psum | solution.py:186
  384.6 1.8 copy.184
  386.4 2.2 copy.185
  (136 shorter events, 10.9 us)
Async XLA Ops:
  7.2 377.4 %all-reduce.9.cloned.1.call-start = ((), (), s32[]{:S(2)}) async-start(), calls=%async_computation | async-start | bytes 2654208 | tf_op jit(solution)/shard_map/psum | solution.py:186
  8.3 9.7 %collective-permute-start = (bf16[4,1,1,4096]{3,0,2,1:T(4,128)(2,1)S(1)}, bf16[4,1,1,4096]{3,0,2,1:T(4,128)(2,1)S(1)}, u32[]{:S(2)}, u32[]{:S(2)}) collective-permute-start(bf16[4,1,1,4096]{3,0,2,1:T(4,128)(2,1)S(1)} %get-tuple-element.223), channel_id=1, source_target_pairs={{0,1},{1,2},{2,3},{3,4},{4,5},{5,6},{6,7},{8,9},{9,10},{10,11},{11... | collective-permute-start | bytes 98312 | tf_op jit(solution)/shard_map/ppermute | solution.py:17
  12.6 5.3 %collective-permute-start.1 = (bf16[4,1,1,4096]{3,0,2,1:T(4,128)(2,1)S(1)}, bf16[4,1,1,4096]{3,0,2,1:T(4,128)(2,1)S(1)}, u32[]{:S(2)}, u32[]{:S(2)}) collective-permute-start(bf16[4,1,1,4096]{3,0,2,1:T(4,128)(2,1)S(1)} %get-tuple-element.224), channel_id=1, source_target_pairs={{1,0},{2,1},{3,2},{4,3},{5,4},{6,5},{7,6},{9,8},{10,9},{11,10},{12... | collective-permute-start | bytes 98312 | tf_op jit(solution)/shard_map/ppermute | solution.py:18
  18.0 2.7 copy-start.8
  18.0 0.6 copy-start.3
  18.6 0.6 copy-start.5
  19.4 1.3 copy-start.4
  19.4 1.3 copy-start.6
  57.7 6.0 %collective-permute-start.2 = (bf16[32,1,1,1024]{3,0,2,1:T(8,128)(2,1)S(1)}, bf16[32,1,1,1024]{3,0,2,1:T(8,128)(2,1)S(1)}, u32[]{:S(2)}, u32[]{:S(2)}) collective-permute-start(bf16[32,1,1,1024]{3,0,2,1:T(8,128)(2,1)S(1)} %get-tuple-element.219), channel_id=1, source_target_pairs={{0,1},{1,2},{2,3},{3,4},{4,5},{5,6},{6,7},{8,9},{9,10},{10,11},{11... | collective-permute-start | bytes 196616 | tf_op jit(solution)/shard_map/ppermute | solution.py:17
  61.9 5.2 %collective-permute-start.3 = (bf16[32,1,1,1024]{3,0,2,1:T(8,128)(2,1)S(1)}, bf16[32,1,1,1024]{3,0,2,1:T(8,128)(2,1)S(1)}, u32[]{:S(2)}, u32[]{:S(2)}) collective-permute-start(bf16[32,1,1,1024]{3,0,2,1:T(8,128)(2,1)S(1)} %get-tuple-element.220), channel_id=1, source_target_pairs={{1,0},{2,1},{3,2},{4,3},{5,4},{6,5},{7,6},{9,8},{10,9},{11,10},{12... | collective-permute-start | bytes 196616 | tf_op jit(solution)/shard_map/ppermute | solution.py:18
  67.3 4.2 %copy-start.2 = (bf16[27,32,64]{2,1,0:T(8,128)(2,1)S(1)}, bf16[27,32,64]{2,1,0:T(8,128)(2,1)}, u32[]{:S(2)}) copy-start(bf16[27,32,64]{2,1,0:T(8,128)(2,1)} %param.12) | copy-start | bytes 331780
  67.3 4.2 %copy-start.9 = (f32[64]{0:T(128)S(1)}, f32[64]{0:T(128)}, u32[]{:S(2)}) copy-start(f32[64]{0:T(128)} %param.13) | copy-start | bytes 772
  69.8 1.7 copy-start
  71.5 8.3 %copy-start.7 = (bf16[128,1,1,256]{3,0,2,1:T(8,128)(2,1)S(1)}, bf16[128,1,1,256]{3,0,2,1:T(8,128)(2,1)}, u32[]{:S(2)}) copy-start(bf16[128,1,1,256]{3,0,2,1:T(8,128)(2,1)} %param.9) | copy-start | bytes 196612
  73.1 14.4 %collective-permute-start.5 = (bf16[64,1,1,256]{0,3,2,1:T(8,128)(2,1)S(1)}, bf16[64,1,1,256]{0,3,2,1:T(8,128)(2,1)S(1)}, u32[]{:S(2)}, u32[]{:S(2)}) collective-permute-start(bf16[64,1,1,256]{0,3,2,1:T(8,128)(2,1)S(1)} %fusion.106), channel_id=1, source_target_pairs={{1,0},{2,1},{3,2},{4,3},{5,4},{6,5},{7,6},{9,8},{10,9},{11,10},{12... | collective-permute-start | bytes 98312 | tf_op jit(solution)/shard_map/ppermute | solution.py:18
  74.4 13.1 %collective-permute-start.4 = (bf16[64,1,1,256]{0,3,2,1:T(8,128)(2,1)S(1)}, bf16[64,1,1,256]{0,3,2,1:T(8,128)(2,1)S(1)}, u32[]{:S(2)}, u32[]{:S(2)}) collective-permute-start(bf16[64,1,1,256]{0,3,2,1:T(8,128)(2,1)S(1)} %fusion.106), channel_id=1, source_target_pairs={{0,1},{1,2},{2,3},{3,4},{4,5},{5,6},{6,7},{8,9},{9,10},{10,11},{11... | collective-permute-start | bytes 98312 | tf_op jit(solution)/shard_map/ppermute | solution.py:17
  87.6 4.9 %copy-start.10 = (f32[128]{0:T(128)S(1)}, f32[128]{0:T(128)}, u32[]{:S(2)}) copy-start(f32[128]{0:T(128)} %param.15) | copy-start | bytes 1540
  93.9 8.6 %collective-permute-start.7 = (bf16[128,1,1,256]{0,3,2,1:T(8,128)(2,1)S(1)}, bf16[128,1,1,256]{0,3,2,1:T(8,128)(2,1)S(1)}, u32[]{:S(2)}, u32[]{:S(2)}) collective-permute-start(bf16[128,1,1,256]{0,3,2,1:T(8,128)(2,1)S(1)} %get-tuple-element.156), channel_id=1, source_target_pairs={{1,0},{2,1},{3,2},{4,3},{5,4},{6,5},{7,6},{9,8},{10,9},{11,10},{12... | collective-permute-start | bytes 196616 | tf_op jit(solution)/shard_map/ppermute | solution.py:18
  95.2 7.3 %collective-permute-start.6 = (bf16[128,1,1,256]{0,3,2,1:T(8,128)(2,1)S(1)}, bf16[128,1,1,256]{0,3,2,1:T(8,128)(2,1)S(1)}, u32[]{:S(2)}, u32[]{:S(2)}) collective-permute-start(bf16[128,1,1,256]{0,3,2,1:T(8,128)(2,1)S(1)} %get-tuple-element.156), channel_id=1, source_target_pairs={{0,1},{1,2},{2,3},{3,4},{4,5},{5,6},{6,7},{8,9},{9,10},{10,11},{11... | collective-permute-start | bytes 196616 | tf_op jit(solution)/shard_map/ppermute | solution.py:17
  106.6 9.9 %collective-permute-start.8 = (bf16[64,1,1,1024]{3,0,2,1:T(8,128)(2,1)S(1)}, bf16[64,1,1,1024]{3,0,2,1:T(8,128)(2,1)S(1)}, u32[]{:S(2)}, u32[]{:S(2)}) collective-permute-start(bf16[64,1,1,1024]{3,0,2,1:T(8,128)(2,1)S(1)} %get-tuple-element.165), channel_id=1, source_target_pairs={{0,1},{1,2},{2,3},{3,4},{4,5},{5,6},{6,7},{8,9},{9,10},{10,11},{11... | collective-permute-start | bytes 393224 | tf_op jit(solution)/shard_map/ppermute | solution.py:17
  111.1 6.9 %collective-permute-start.9 = (bf16[64,1,1,1024]{3,0,2,1:T(8,128)(2,1)S(1)}, bf16[64,1,1,1024]{3,0,2,1:T(8,128)(2,1)S(1)}, u32[]{:S(2)}, u32[]{:S(2)}) collective-permute-start(bf16[64,1,1,1024]{3,0,2,1:T(8,128)(2,1)S(1)} %get-tuple-element.166), channel_id=1, source_target_pairs={{1,0},{2,1},{3,2},{4,3},{5,4},{6,5},{7,6},{9,8},{10,9},{11,10},{12... | collective-permute-start | bytes 393224 | tf_op jit(solution)/shard_map/ppermute | solution.py:18
  136.3 2.7 copy-start.1
Sparse Core Ops, SparseCore 0:
  116.6 267.9 all-reduce.8
where the time goes:
time: 400 us; the launch traced here: 396 us
  waiting for transfers between devices  160 us (40%)
  blocking collectives  85.7 us (21%)
  local copies, waits for them, and re-layouts  61 us (15%)
  starting transfers between devices  30.9 us (8%)
  other arithmetic  24.5 us (6%)
  matrix products  18 us (4%)
  between operations  15.3 us (4%)
    psum x1, waiting for transfers between devices, per_device(): lax.psum((kernel_first, bias_first, kernel_second, bias_second), ('sample...  155 us
    psum x1, blocking collectives, per_device(): lax.psum((kernel_first, bias_first, kernel_second, bias_second), ('sample...  85.7 us
    ppermute x5, starting transfers between devices, with_halo(): before = lax.ppermute(last, axis, up)  23.7 us
    concatenate x3, local copies, waits for them, and re-layouts, gather_taps(): return jnp.concatenate(pieces, axis=0)  20.2 us
    unnamed x52, local copies, waits for them, and re-layouts  12.9 us
    reduce_sum x2, other arithmetic, pool_cells(): grouped.mean(axis=(3, 5, 7))  9.96 us
    dot_general x3, matrix products, weight_term(): jnp.einsum('kgzp,ogzp->ko', patches, grad_block, preferred_element_type=j...  9.02 us
    dot_general x5, matrix products, apply_weight(): jnp.einsum('ko,kgzp->ogzp', flat_weight, patches, preferred_element_type=...  8.99 us
  transfers between devices with their start and end apart: 11, of which 3 were waited for; matrix products, arithmetic and copies ran while one was open for 11% of the time, Pallas kernels for 0%

commit v1 on v0

--- a/solution.py
+++ b/solution.py
@@ -166,7 +166,6 @@
     ).astype(jnp.bfloat16)
     kernel_third = weight_grads(third_padded, third_delta, SX // 4, coarse_depth, w_third)
     bias_third = bias_sum(third_delta)
-    kernel_third, bias_third = lax.psum((kernel_third, bias_third), ("sample", "slab"))
     delta_window = with_halo(third_delta, (("slab", 2),), 1)
     second_back = data_grads(delta_window, flipped_third, SX // 4, coarse_depth)
     second_delta = (
@@ -183,18 +182,49 @@
     ).astype(jnp.bfloat16)
     kernel_first = weight_grads(volume_padded, first_delta, SX, CZ, w_first)
     bias_first = bias_sum(first_delta)
-    kernel_first, bias_first, kernel_second, bias_second = lax.psum(
-        (kernel_first, bias_first, kernel_second, bias_second), ("sample", "slab")
-    )
-    return (
-        features,
-        kernel_first,
-        bias_first,
-        kernel_second,
-        bias_second,
-        kernel_third,
-        bias_third,
-    )
+    grads = (kernel_first, bias_first, kernel_second, bias_second, kernel_third, bias_third)
+    summed = all_reduce_grads(grads)
+    return (features,) + summed
+
+
+def xor_pairs(axis, mask):
+    return [(i, i ^ mask) for i in range(lax.axis_size(axis))]
+
+
+def all_reduce_grads(grads, halving_steps=3):
+    steps = []
+    for axis in ("sample", "slab"):
+        mask = 1
+        while mask < lax.axis_size(axis):
+            steps.append((axis, mask))
+            mask *= 2
+    sizes = [g.size for g in grads]
+    flat = jnp.concatenate([g.reshape(-1) for g in grads])
+    block = 1024 * (1 << halving_steps)
+    total = -(-flat.shape[0] // block) * block
+    flat = jnp.pad(flat, (0, total - flat.shape[0]))
+    kept = []
+    for axis, mask in steps[:halving_steps]:
+        half = flat.shape[0] // 2
+        upper = (lax.axis_index(axis) & mask) != 0
+        low, high = flat[:half], flat[half:]
+        send = jnp.where(upper, low, high)
+        keep = jnp.where(upper, high, low)
+        flat = keep + lax.ppermute(send, axis, xor_pairs(axis, mask))
+        kept.append((axis, mask, upper))
+    for axis, mask in steps[halving_steps:]:
+        flat = flat + lax.ppermute(flat, axis, xor_pairs(axis, mask))
+    for axis, mask, upper in reversed(kept):
+        other = lax.ppermute(flat, axis, xor_pairs(axis, mask))
+        flat = jnp.where(
+            upper, jnp.concatenate([other, flat]), jnp.concatenate([flat, other])
+        )
+    out = []
+    start = 0
+    for g, size in zip(grads, sizes):
+        out.append(flat[start : start + size].reshape(g.shape))
+        start += size
+    return tuple(out)
 
 
 def solution(mesh):

time: 400 us -> 237 us (0.59)
  waiting for transfers between devices: 160 us -> 40.5 us
  blocking collectives: 85.7 us -> 0 us
  starting transfers between devices: 30.9 us -> 78 us
  between operations: 15.3 us -> 2.13 us
  local copies, waits for them, and re-layouts: 61 us -> 70 us
    psum x1 -> x0, waiting for transfers between devices: 155 us -> none  [per_device(): lax.psum((kernel_first, bias_first, kernel_second, bias_second), ('sample...]
    psum x1 -> x0, blocking collectives: 85.7 us -> none  [per_device(): lax.psum((kernel_first, bias_first, kernel_second, bias_second), ('sample...]
    ppermute x0 -> x11, starting transfers between devices: none -> 47.4 us  [the longest x3 18.9 us: all_reduce_grads(): other = lax.ppermute(flat, axis, xor_pairs(axis, mask))]
    ppermute x0 -> x11, waiting for transfers between devices: none -> 33.5 us  [the longest x5 15.4 us: all_reduce_grads(): flat = flat + lax.ppermute(flat, axis, xor_pairs(axis, mask))]
    concatenate x0 -> x10, local copies, waits for them, and re-layouts: none -> 16.7 us  [the longest x2 11.5 us: all_reduce_grads(): flat = jnp.concatenate([g.reshape(-1) for g in grads])]
    dot_general x1 -> x0, local copies, waits for them, and re-layouts: 6.56 us -> none  [weight_term(): jnp.einsum('kgzp,ogzp->ko', patches, grad_block, preferred_element_type=j...]
    unnamed x52 -> x54, local copies, waits for them, and re-layouts: 12.9 us -> 8.07 us
    dot_general x3, matrix products: 9.02 us -> 4.59 us  [weight_term(): jnp.einsum('kgzp,ogzp->ko', patches, grad_block, preferred_element_type=j...]
  transfers between devices with their start and end apart: 11 -> 21, of which waited for: 3 -> 14; matrix products, arithmetic and copies ran while one was open for 11% -> 6% of each run, Pallas kernels for 0% -> 0%
where the time goes in v1:
time: 237 us; the launch traced here: 232 us
  starting transfers between devices  78 us (33%)
  local copies, waits for them, and re-layouts  70 us (30%)
  waiting for transfers between devices  40.5 us (17%)
  other arithmetic  27.8 us (12%)
  matrix products  14.1 us (6%)
    ppermute x5, starting transfers between devices, with_halo(): before = lax.ppermute(last, axis, up)  23.7 us
    concatenate x2, local copies, waits for them, and re-layouts, gather_taps(): return jnp.concatenate(pieces, axis=0)  19.8 us
    ppermute x3, starting transfers between devices, all_reduce_grads(): other = lax.ppermute(flat, axis, xor_pairs(axis, mask))  18.9 us
    ppermute x5, starting transfers between devices, all_reduce_grads(): flat = flat + lax.ppermute(flat, axis, xor_pairs(axis, mask))  18 us
    ppermute x5, waiting for transfers between devices, all_reduce_grads(): flat = flat + lax.ppermute(flat, axis, xor_pairs(axis, mask))  15.4 us
    concatenate x2, local copies, waits for them, and re-layouts, all_reduce_grads(): flat = jnp.concatenate([g.reshape(-1) for g in grads])  11.5 us
    ppermute x3, waiting for transfers between devices, all_reduce_grads(): flat = keep + lax.ppermute(send, axis, xor_pairs(axis, mask))  11 us
    ppermute x3, starting transfers between devices, all_reduce_grads(): flat = keep + lax.ppermute(send, axis, xor_pairs(axis, mask))  10.5 us
  transfers between devices with their start and end apart: 21, of which 14 were waited for; matrix products, arithmetic and copies ran while one was open for 6% of the time, Pallas kernels for 0%

profile of v1, /device:TPU:1, one launch (start us, length us, event | category | flops | bytes accessed | tf_op | source)
XLA Modules:
  0.0 232.5 jit_solution(973493289761846536)
XLA Ops:
  1.7 4.4 %collective-permute-start = (bf16[4,1,1,4096]{3,0,2,1:T(4,128)(2,1)S(1)}, bf16[4,1,1,4096]{3,0,2,1:T(4,128)(2,1)S(1)}, u32[]{:S(2)}, u32[]{:S(2)}) collective-permute-start(bf16[4,1,1,4096]{3,0,2,1:T(4,128)(2,1)S(1)} %get-tuple-element.217), channel_id=1, source_target_pairs={{0,1},{1,2},{2,3},{3,4},{4,5},{5,6},{6,7},{8,9},{9,10},{10,11},{11... | collective-permute-start | bytes 98312 | tf_op jit(solution)/shard_map/ppermute | solution.py:17
  6.1 1.3 collective-permute-start.1
  10.0 1.4 reshape.352
  14.1 1.7 slice_multiply_fusion.37
  15.8 16.5 %concatenate.112 = bf16[108,1,4,4096]{3,0,2,1:T(8,128)(2,1)} concatenate(bf16[4,1,4,4096]{3,0,2,1:T(4,128)(2,1)} %get-tuple-element.206, bf16[4,1,4,4096]{3,0,2,1:T(4,128)(2,1)S(1)} %get-tuple-element.212, bf16[4,1,4,4096]{3,0,2,1:T(4,128)(2,1)S(1)} %get-tuple-element.197, bf16[4,1,4,4096]{3,0,2,1:T(4,128)(2,1)} %get-tuple-element.205, ...), dimensions={0} | concatenate | bytes 7077888 | tf_op jit(solution)/shard_map/while/body/eval_jaxpr/concatenate | solution.py:53
  32.3 4.7 %fusion.12 = (f32[32,4,4096]{2,0,1:T(8,128)S(1)}, f32[32,4,4096]{2,0,1:T(8,128)}) fusion(f32[32]{0:T(128)} %param.11, bf16[108,32]{1,0:T(8,128)(2,1)} %reshape.352, bf16[108,1,4,4096]{3,0,2,1:T(8,128)(2,1)} %concatenate.112), kind=kOutput, calls=%fused_computation.17 | convolution fusion | flops 116916224 | bytes 7740288 | tf_op jit(solution)/shard_map/while/body/eval_jaxpr/ko,kgzp->ogzp/dot_general | solution.py:58
  37.0 4.7 %copy.57 = f32[32,4,4096]{0,2,1:T(8,128)} copy(f32[32,4,4096]{2,0,1:T(8,128)S(1)} %get-tuple-element.219) | data formatting | bytes 4194304 | tf_op jit(solution)/shard_map/while/body/eval_jaxpr/jit(silu)/mul | solution.py:103
  41.7 9.5 %reduce_sum.54 = f32[32,2,64,16]{0,3,2,1:T(8,128)S(1)} reduce(f32[32,2,2,64,2,16,2]{0,6,5,4,3,2,1:T(2,128)} %bitcast.117, f32[]{:T(128)} %constant.232.clone.1), dimensions={2,4,6}, to_apply=%region_0.1 | reduce | flops 458752 | bytes 2359300 | tf_op jit(solution)/shard_map/while/body/eval_jaxpr/reduce_sum | solution.py:72
  51.6 4.2 %collective-permute-start.2 = (bf16[32,1,1,1024]{3,0,2,1:T(8,128)(2,1)S(1)}, bf16[32,1,1,1024]{3,0,2,1:T(8,128)(2,1)S(1)}, u32[]{:S(2)}, u32[]{:S(2)}) collective-permute-start(bf16[32,1,1,1024]{3,0,2,1:T(8,128)(2,1)S(1)} %get-tuple-element.213), channel_id=1, source_target_pairs={{0,1},{1,2},{2,3},{3,4},{4,5},{5,6},{6,7},{8,9},{9,10},{10,11},{11... | collective-permute-start | bytes 196616 | tf_op jit(solution)/shard_map/ppermute | solution.py:17
  55.8 1.5 collective-permute-start.3
  57.3 3.7 %collective-permute-done.3 = bf16[32,1,1,1024]{3,0,2,1:T(8,128)(2,1)S(1)} collective-permute-done((bf16[32,1,1,1024]{3,0,2,1:T(8,128)(2,1)S(1)}, bf16[32,1,1,1024]{3,0,2,1:T(8,128)(2,1)S(1)}, u32[]{:S(2)}, u32[]{:S(2)}) %collective-permute-start.3) | collective-permute-done | bytes 65568 | tf_op jit(solution)/shard_map/ppermute | solution.py:18
  67.3 5.4 %collective-permute-start.4 = (bf16[64,1,1,256]{0,3,2,1:T(8,128)(2,1)S(1)}, bf16[64,1,1,256]{0,3,2,1:T(8,128)(2,1)S(1)}, u32[]{:S(2)}, u32[]{:S(2)}) collective-permute-start(bf16[64,1,1,256]{0,3,2,1:T(8,128)(2,1)S(1)} %fusion.110), channel_id=1, source_target_pairs={{0,1},{1,2},{2,3},{3,4},{4,5},{5,6},{6,7},{8,9},{9,10},{10,11},{11... | collective-permute-start | bytes 98312 | tf_op jit(solution)/shard_map/ppermute | solution.py:17
  75.2 3.3 %concatenate.118 = bf16[1728,1,1,256]{0,3,2,1:T(8,128)(2,1)S(1)} concatenate(bf16[64,1,1,256]{0,3,2,1:T(8,128)(2,1)S(1)} %get-tuple-element.182, bf16[64,1,1,256]{0,3,2,1:T(8,128)(2,1)} %get-tuple-element.188, bf16[64,1,1,256]{0,3,2,1:T(8,128)(2,1)} %get-tuple-element.173, bf16[64,1,1,256]{0,3,2,1:T(8,128)(2,1)S(1)} %get-tuple-element.181, ...), dimensions={0} | concatenate | bytes 1769472 | tf_op jit(solution)/shard_map/while/body/eval_jaxpr/concatenate | solution.py:53
  78.6 1.9 convert_reduce_fusion.2
  81.8 5.2 %collective-permute-start.6 = (bf16[128,1,1,256]{0,3,2,1:T(8,128)(2,1)S(1)}, bf16[128,1,1,256]{0,3,2,1:T(8,128)(2,1)S(1)}, u32[]{:S(2)}, u32[]{:S(2)}) collective-permute-start(bf16[128,1,1,256]{0,3,2,1:T(8,128)(2,1)S(1)} %get-tuple-element.140), channel_id=1, source_target_pairs={{0,1},{1,2},{2,3},{3,4},{4,5},{5,6},{6,7},{8,9},{9,10},{10,11},{11... | collective-permute-start | bytes 196616 | tf_op jit(solution)/shard_map/ppermute | solution.py:17
  92.3 4.6 %collective-permute-start.8 = (bf16[64,1,1,1024]{3,0,2,1:T(8,128)(2,1)S(1)}, bf16[64,1,1,1024]{3,0,2,1:T(8,128)(2,1)S(1)}, u32[]{:S(2)}, u32[]{:S(2)}) collective-permute-start(bf16[64,1,1,1024]{3,0,2,1:T(8,128)(2,1)S(1)} %get-tuple-element.150), channel_id=1, source_target_pairs={{0,1},{1,2},{2,3},{3,4},{4,5},{5,6},{6,7},{8,9},{9,10},{10,11},{11... | collective-permute-start | bytes 393224 | tf_op jit(solution)/shard_map/ppermute | solution.py:17
  96.9 1.5 collective-permute-start.9
  98.4 3.1 %fusion.18 = f32[864,64]{1,0:T(8,128)S(1)} fusion(bf16[64,2,1024]{2,0,1:T(8,128)(2,1)S(1)} %get-tuple-element.147, bf16[864,1,2,1024]{3,0,2,1:T(8,128)(2,1)} %copy-done.10), kind=kOutput, calls=%fused_computation.23 | convolution fusion | flops 226492416 | bytes 4022272 | tf_op jit(solution)/shard_map/while/body/eval_jaxpr/kgzp,ogzp->ko/dot_general | solution.py:62
  101.6 2.2 collective-permute-done.9
  107.6 1.3 fusion.40
  109.3 7.6 %broadcast_in_dim.14 = f32[32,2,2,64,2,16,2]{0,6,5,4,3,2,1:T(2,128)} broadcast(f32[32,2,64,16]{0,3,2,1:T(8,128)S(1)} %bitcast.123), dimensions={0,1,3,5} | broadcast | bytes 2359296 | tf_op jit(solution)/shard_map/broadcast_in_dim | solution.py:79
  116.9 5.1 %copy.72 = f32[32,4,4096]{2,0,1:T(8,128)S(1)} copy(f32[32,4,4096]{0,2,1:T(8,128)} %bitcast.118) | data formatting | bytes 4194304 | tf_op jit(solution)/shard_map/mul | solution.py:82
  122.0 2.7 %convert_reduce_fusion = (f32[32]{0:T(128)S(1)}, bf16[32,4,4096]{2,0,1:T(8,128)(2,1)S(1)}) fusion(f32[32,4,4096]{2,0,1:T(8,128)S(1)} %copy.72, f32[32,4,4096]{2,0,1:T(8,128)} %get-tuple-element.220), kind=kLoop, calls=%fused_computation.14 | loop fusion | flops 5767136 | bytes 5243008 | tf_op jit(solution)/shard_map/reduce_sum | solution.py:147
  125.8 5.7 %concatenate.126 = f32[280032]{0:T(1024)S(1)} concatenate(f32[3456]{0:T(1024)S(1)} %reshape.362, f32[32]{0:T(128)S(1)} %get-tuple-element.148, f32[55296]{0:T(1024)S(1)} %reshape.363, f32[64]{0:T(128)S(1)} %get-tuple-element.146, f32[221184]{0:T(1024)S(1)} %convolution_bitcast_fusion), dimensions={0} | concatenate | bytes 2240256 | tf_op jit(solution)/shard_map/concatenate | solution.py:202
  131.5 5.8 %concatenate.125 = f32[280160]{0:T(1024)S(1)} concatenate(f32[3456]{0:T(1024)S(1)} %reshape.362, f32[32]{0:T(128)S(1)} %get-tuple-element.148, f32[55296]{0:T(1024)S(1)} %reshape.363, f32[64]{0:T(128)S(1)} %get-tuple-element.146, f32[221184]{0:T(1024)S(1)} %convolution_bitcast_fusion, f32[128]{0:T(128)S(1)} %get-tuple-element.139), dimensions={0} | concatenate | bytes 2241280 | tf_op jit(solution)/shard_map/concatenate | solution.py:202
  137.4 5.9 %collective-permute-start.10 = (f32[143360]{0:T(1024)S(1)}, f32[143360]{0:T(1024)}, u32[]{:S(2)}, u32[]{:S(2)}) collective-permute-start(f32[143360]{0:T(1024)S(1)} %slice_select_fusion), channel_id=1, source_target_pairs={{0,8},{8,0},{16,24},{24,16},{32,40},{40,32},{48,56},{56,48},{64,72... | collective-permute-start | bytes 1720328 | tf_op jit(solution)/shard_map/ppermute | solution.py:213
  143.3 1.7 collective-permute-done.10
  146.3 1.6 collective-permute-start.11
  147.9 6.8 %collective-permute-done.11 = f32[71680]{0:T(1024)S(1)} collective-permute-done((f32[71680]{0:T(1024)S(1)}, f32[71680]{0:T(1024)S(1)}, u32[]{:S(2)}, u32[]{:S(2)}) %collective-permute-start.11) | collective-permute-done | bytes 286752 | tf_op jit(solution)/shard_map/ppermute | solution.py:213
  154.7 3.0 %collective-permute-start.12 = (f32[35840]{0:T(1024)S(1)}, f32[35840]{0:T(1024)S(1)}, u32[]{:S(2)}, u32[]{:S(2)}) collective-permute-start(f32[35840]{0:T(1024)S(1)} %slice_select_fusion.2), channel_id=1, source_target_pairs={{0,32},{8,40},{16,48},{24,56},{32,0},{40,8},{48,16},{56,24},{64,96... | collective-permute-start | bytes 430088 | tf_op jit(solution)/shard_map/ppermute | solution.py:213
  157.7 2.5 %collective-permute-done.12 = f32[35840]{0:T(1024)S(1)} collective-permute-done((f32[35840]{0:T(1024)S(1)}, f32[35840]{0:T(1024)S(1)}, u32[]{:S(2)}, u32[]{:S(2)}) %collective-permute-start.12) | collective-permute-done | bytes 143392 | tf_op jit(solution)/shard_map/ppermute | solution.py:213
  160.3 1.3 collective-permute-start.13
  161.6 2.7 %collective-permute-done.13 = f32[35840]{0:T(1024)S(1)} collective-permute-done((f32[35840]{0:T(1024)S(1)}, f32[35840]{0:T(1024)S(1)}, u32[]{:S(2)}, u32[]{:S(2)}) %collective-permute-start.13) | collective-permute-done | bytes 143392 | tf_op jit(solution)/shard_map/ppermute | solution.py:216
  164.4 2.8 %collective-permute-start.14 = (f32[35840]{0:T(1024)S(1)}, f32[35840]{0:T(1024)S(1)}, u32[]{:S(2)}, u32[]{:S(2)}) collective-permute-start(f32[35840]{0:T(1024)S(1)} %add.439), channel_id=1, source_target_pairs={{0,128},{8,136},{16,144},{24,152},{32,160},{40,168},{48,176},{56,1... | collective-permute-start | bytes 430088 | tf_op jit(solution)/shard_map/ppermute | solution.py:216
  167.2 3.7 %collective-permute-done.14 = f32[35840]{0:T(1024)S(1)} collective-permute-done((f32[35840]{0:T(1024)S(1)}, f32[35840]{0:T(1024)S(1)}, u32[]{:S(2)}, u32[]{:S(2)}) %collective-permute-start.14) | collective-permute-done | bytes 143392 | tf_op jit(solution)/shard_map/ppermute | solution.py:216
  170.9 3.4 %collective-permute-start.15 = (f32[35840]{0:T(1024)S(1)}, f32[35840]{0:T(1024)S(1)}, u32[]{:S(2)}, u32[]{:S(2)}) collective-permute-start(f32[35840]{0:T(1024)S(1)} %add.440), channel_id=1, source_target_pairs={{0,1},{1,0},{2,3},{3,2},{4,5},{5,4},{6,7},{7,6},{8,9},{9,8},{10,11... | collective-permute-start | bytes 430088 | tf_op jit(solution)/shard_map/ppermute | solution.py:216
  174.3 2.5 %collective-permute-done.15 = f32[35840]{0:T(1024)S(1)} collective-permute-done((f32[35840]{0:T(1024)S(1)}, f32[35840]{0:T(1024)S(1)}, u32[]{:S(2)}, u32[]{:S(2)}) %collective-permute-start.15) | collective-permute-done | bytes 143392 | tf_op jit(solution)/shard_map/ppermute | solution.py:216
  176.8 6.0 %collective-permute-start.16 = (f32[35840]{0:T(1024)S(1)}, f32[35840]{0:T(1024)S(1)}, u32[]{:S(2)}, u32[]{:S(2)}) collective-permute-start(f32[35840]{0:T(1024)S(1)} %add.441), channel_id=1, source_target_pairs={{0,2},{1,3},{2,0},{3,1},{4,6},{5,7},{6,4},{7,5},{8,10},{9,11},{10,... | collective-permute-start | bytes 430088 | tf_op jit(solution)/shard_map/ppermute | solution.py:216
  182.8 2.8 %collective-permute-done.16 = f32[35840]{0:T(1024)S(1)} collective-permute-done((f32[35840]{0:T(1024)S(1)}, f32[35840]{0:T(1024)S(1)}, u32[]{:S(2)}, u32[]{:S(2)}) %collective-permute-start.16) | collective-permute-done | bytes 143392 | tf_op jit(solution)/shard_map/ppermute | solution.py:216
  185.7 4.5 %collective-permute-start.17 = (f32[35840]{0:T(1024)S(1)}, f32[35840]{0:T(1024)S(1)}, u32[]{:S(2)}, u32[]{:S(2)}) collective-permute-start(f32[35840]{0:T(1024)S(1)} %add.442), channel_id=1, source_target_pairs={{0,4},{1,5},{2,6},{3,7},{4,0},{5,1},{6,2},{7,3},{8,12},{9,13},{10,... | collective-permute-start | bytes 430088 | tf_op jit(solution)/shard_map/ppermute | solution.py:216
  190.2 3.7 %collective-permute-done.17 = f32[35840]{0:T(1024)S(1)} collective-permute-done((f32[35840]{0:T(1024)S(1)}, f32[35840]{0:T(1024)S(1)}, u32[]{:S(2)}, u32[]{:S(2)}) %collective-permute-start.17) | collective-permute-done | bytes 143392 | tf_op jit(solution)/shard_map/ppermute | solution.py:216
  193.9 3.0 %collective-permute-start.18 = (f32[35840]{0:T(1024)S(1)}, f32[35840]{0:T(1024)S(1)}, u32[]{:S(2)}, u32[]{:S(2)}) collective-permute-start(f32[35840]{0:T(1024)S(1)} %add.443), channel_id=1, source_target_pairs={{0,32},{8,40},{16,48},{24,56},{32,0},{40,8},{48,16},{56,24},{64,96... | collective-permute-start | bytes 430088 | tf_op jit(solution)/shard_map/ppermute | solution.py:218
  196.8 2.5 %collective-permute-done.18 = f32[35840]{0:T(1024)S(1)} collective-permute-done((f32[35840]{0:T(1024)S(1)}, f32[35840]{0:T(1024)S(1)}, u32[]{:S(2)}, u32[]{:S(2)}) %collective-permute-start.18) | collective-permute-done | bytes 143392 | tf_op jit(solution)/shard_map/ppermute | solution.py:218
  199.4 1.4 collective-permute-start.19
  200.8 4.5 %collective-permute-done.19 = f32[71680]{0:T(1024)S(1)} collective-permute-done((f32[71680]{0:T(1024)S(1)}, f32[71680]{0:T(1024)S(1)}, u32[]{:S(2)}, u32[]{:S(2)}) %collective-permute-start.19) | collective-permute-done | bytes 286752 | tf_op jit(solution)/shard_map/ppermute | solution.py:218
  205.3 14.5 %collective-permute-start.20 = (f32[143360]{0:T(1024)S(1)}, f32[143360]{0:T(1024)S(1)}, u32[]{:S(2)}, u32[]{:S(2)}) collective-permute-start(f32[143360]{0:T(1024)S(1)} %maximum_select_fusion.2), channel_id=1, source_target_pairs={{0,8},{8,0},{16,24},{24,16},{32,40},{40,32},{48,56},{56,48},{64,72... | collective-permute-start | bytes 1720328 | tf_op jit(solution)/shard_map/ppermute | solution.py:218
  223.6 1.3 maximum_select_fusion.1
  229.9 1.5 copy.81
  (189 shorter events, 37.7 us)
Async XLA Ops:
  1.7 9.7 %collective-permute-start = (bf16[4,1,1,4096]{3,0,2,1:T(4,128)(2,1)S(1)}, bf16[4,1,1,4096]{3,0,2,1:T(4,128)(2,1)S(1)}, u32[]{:S(2)}, u32[]{:S(2)}) collective-permute-start(bf16[4,1,1,4096]{3,0,2,1:T(4,128)(2,1)S(1)} %get-tuple-element.217), channel_id=1, source_target_pairs={{0,1},{1,2},{2,3},{3,4},{4,5},{5,6},{6,7},{8,9},{9,10},{10,11},{11... | collective-permute-start | bytes 98312 | tf_op jit(solution)/shard_map/ppermute | solution.py:17
  6.1 5.3 %collective-permute-start.1 = (bf16[4,1,1,4096]{3,0,2,1:T(4,128)(2,1)S(1)}, bf16[4,1,1,4096]{3,0,2,1:T(4,128)(2,1)S(1)}, u32[]{:S(2)}, u32[]{:S(2)}) collective-permute-start(bf16[4,1,1,4096]{3,0,2,1:T(4,128)(2,1)S(1)} %get-tuple-element.218), channel_id=1, source_target_pairs={{1,0},{2,1},{3,2},{4,3},{5,4},{6,5},{7,6},{9,8},{10,9},{11,10},{12... | collective-permute-start | bytes 98312 | tf_op jit(solution)/shard_map/ppermute | solution.py:18
  11.4 2.7 %copy-start.9 = (bf16[4096]{0:T(1024)(128)(2,1)S(1)}, bf16[4096]{0:T(1024)(128)(2,1)}, u32[]{:S(2)}) copy-start(bf16[4096]{0:T(1024)(128)(2,1)} %fusion.119) | copy-start | bytes 24580
  11.4 0.6 copy-start.3
  12.0 0.6 copy-start.5
  12.8 1.3 copy-start.4
  12.8 1.3 copy-start.6
  51.6 5.7 %collective-permute-start.2 = (bf16[32,1,1,1024]{3,0,2,1:T(8,128)(2,1)S(1)}, bf16[32,1,1,1024]{3,0,2,1:T(8,128)(2,1)S(1)}, u32[]{:S(2)}, u32[]{:S(2)}) collective-permute-start(bf16[32,1,1,1024]{3,0,2,1:T(8,128)(2,1)S(1)} %get-tuple-element.213), channel_id=1, source_target_pairs={{0,1},{1,2},{2,3},{3,4},{4,5},{5,6},{6,7},{8,9},{9,10},{10,11},{11... | collective-permute-start | bytes 196616 | tf_op jit(solution)/shard_map/ppermute | solution.py:17
  55.8 5.2 %collective-permute-start.3 = (bf16[32,1,1,1024]{3,0,2,1:T(8,128)(2,1)S(1)}, bf16[32,1,1,1024]{3,0,2,1:T(8,128)(2,1)S(1)}, u32[]{:S(2)}, u32[]{:S(2)}) collective-permute-start(bf16[32,1,1,1024]{3,0,2,1:T(8,128)(2,1)S(1)} %get-tuple-element.214), channel_id=1, source_target_pairs={{1,0},{2,1},{3,2},{4,3},{5,4},{6,5},{7,6},{9,8},{10,9},{11,10},{12... | collective-permute-start | bytes 196616 | tf_op jit(solution)/shard_map/ppermute | solution.py:18
  61.1 2.5 %copy-start.2 = (bf16[27,32,64]{2,1,0:T(8,128)(2,1)S(1)}, bf16[27,32,64]{2,1,0:T(8,128)(2,1)}, u32[]{:S(2)}) copy-start(bf16[27,32,64]{2,1,0:T(8,128)(2,1)} %param.12) | copy-start | bytes 331780
  61.1 2.5 %copy-start.11 = (f32[64]{0:T(128)S(1)}, f32[64]{0:T(128)}, u32[]{:S(2)}) copy-start(f32[64]{0:T(128)} %param.13) | copy-start | bytes 772
  63.6 1.7 copy-start.10
  63.7 9.1 %copy-start.8 = (bf16[128,1,1,256]{3,0,2,1:T(8,128)(2,1)S(1)}, bf16[128,1,1,256]{3,0,2,1:T(8,128)(2,1)}, u32[]{:S(2)}) copy-start(bf16[128,1,1,256]{3,0,2,1:T(8,128)(2,1)} %param.9) | copy-start | bytes 196612
  66.0 7.8 %collective-permute-start.5 = (bf16[64,1,1,256]{0,3,2,1:T(8,128)(2,1)S(1)}, bf16[64,1,1,256]{0,3,2,1:T(8,128)(2,1)S(1)}, u32[]{:S(2)}, u32[]{:S(2)}) collective-permute-start(bf16[64,1,1,256]{0,3,2,1:T(8,128)(2,1)S(1)} %fusion.110), channel_id=1, source_target_pairs={{1,0},{2,1},{3,2},{4,3},{5,4},{6,5},{7,6},{9,8},{10,9},{11,10},{12... | collective-permute-start | bytes 98312 | tf_op jit(solution)/shard_map/ppermute | solution.py:18
  67.3 6.7 %collective-permute-start.4 = (bf16[64,1,1,256]{0,3,2,1:T(8,128)(2,1)S(1)}, bf16[64,1,1,256]{0,3,2,1:T(8,128)(2,1)S(1)}, u32[]{:S(2)}, u32[]{:S(2)}) collective-permute-start(bf16[64,1,1,256]{0,3,2,1:T(8,128)(2,1)S(1)} %fusion.110), channel_id=1, source_target_pairs={{0,1},{1,2},{2,3},{3,4},{4,5},{5,6},{6,7},{8,9},{9,10},{10,11},{11... | collective-permute-start | bytes 98312 | tf_op jit(solution)/shard_map/ppermute | solution.py:17
  73.5 5.1 %copy-start.1 = (bf16[27,64,128]{2,1,0:T(8,128)(2,1)S(1)}, bf16[27,64,128]{2,1,0:T(8,128)(2,1)}, u32[]{:S(2)}) copy-start(bf16[27,64,128]{2,1,0:T(8,128)(2,1)} %param.14) | copy-start | bytes 1327108
  73.5 5.1 %copy-start.12 = (f32[128]{0:T(128)S(1)}, f32[128]{0:T(128)}, u32[]{:S(2)}) copy-start(f32[128]{0:T(128)} %param.15) | copy-start | bytes 1540
  80.5 6.9 %collective-permute-start.7 = (bf16[128,1,1,256]{0,3,2,1:T(8,128)(2,1)S(1)}, bf16[128,1,1,256]{0,3,2,1:T(8,128)(2,1)S(1)}, u32[]{:S(2)}, u32[]{:S(2)}) collective-permute-start(bf16[128,1,1,256]{0,3,2,1:T(8,128)(2,1)S(1)} %get-tuple-element.140), channel_id=1, source_target_pairs={{1,0},{2,1},{3,2},{4,3},{5,4},{6,5},{7,6},{9,8},{10,9},{11,10},{12... | collective-permute-start | bytes 196616 | tf_op jit(solution)/shard_map/ppermute | solution.py:18
  81.8 6.5 %collective-permute-start.6 = (bf16[128,1,1,256]{0,3,2,1:T(8,128)(2,1)S(1)}, bf16[128,1,1,256]{0,3,2,1:T(8,128)(2,1)S(1)}, u32[]{:S(2)}, u32[]{:S(2)}) collective-permute-start(bf16[128,1,1,256]{0,3,2,1:T(8,128)(2,1)S(1)} %get-tuple-element.140), channel_id=1, source_target_pairs={{0,1},{1,2},{2,3},{3,4},{4,5},{5,6},{6,7},{8,9},{9,10},{10,11},{11... | collective-permute-start | bytes 196616 | tf_op jit(solution)/shard_map/ppermute | solution.py:17
  92.3 9.3 %collective-permute-start.8 = (bf16[64,1,1,1024]{3,0,2,1:T(8,128)(2,1)S(1)}, bf16[64,1,1,1024]{3,0,2,1:T(8,128)(2,1)S(1)}, u32[]{:S(2)}, u32[]{:S(2)}) collective-permute-start(bf16[64,1,1,1024]{3,0,2,1:T(8,128)(2,1)S(1)} %get-tuple-element.150), channel_id=1, source_target_pairs={{0,1},{1,2},{2,3},{3,4},{4,5},{5,6},{6,7},{8,9},{9,10},{10,11},{11... | collective-permute-start | bytes 393224 | tf_op jit(solution)/shard_map/ppermute | solution.py:17
  96.9 6.9 %collective-permute-start.9 = (bf16[64,1,1,1024]{3,0,2,1:T(8,128)(2,1)S(1)}, bf16[64,1,1,1024]{3,0,2,1:T(8,128)(2,1)S(1)}, u32[]{:S(2)}, u32[]{:S(2)}) collective-permute-start(bf16[64,1,1,1024]{3,0,2,1:T(8,128)(2,1)S(1)} %get-tuple-element.156), channel_id=1, source_target_pairs={{1,0},{2,1},{3,2},{4,3},{5,4},{6,5},{7,6},{9,8},{10,9},{11,10},{12... | collective-permute-start | bytes 393224 | tf_op jit(solution)/shard_map/ppermute | solution.py:18
  122.0 2.7 %copy-start = (bf16[108,1,4,4096]{3,0,2,1:T(8,128)(2,1)S(1)}, bf16[108,1,4,4096]{3,0,2,1:T(8,128)(2,1)}, u32[]{:S(2)}) copy-start(bf16[108,1,4,4096]{3,0,2,1:T(8,128)(2,1)} %concatenate.112) | copy-start | bytes 10616836
  137.4 7.6 %collective-permute-start.10 = (f32[143360]{0:T(1024)S(1)}, f32[143360]{0:T(1024)}, u32[]{:S(2)}, u32[]{:S(2)}) collective-permute-start(f32[143360]{0:T(1024)S(1)} %slice_select_fusion), channel_id=1, source_target_pairs={{0,8},{8,0},{16,24},{24,16},{32,40},{40,32},{48,56},{56,48},{64,72... | collective-permute-start | bytes 1720328 | tf_op jit(solution)/shard_map/ppermute | solution.py:213
  146.2 73.7 %copy-start.7 = (f32[128,256]{0,1:T(8,128)S(1)}, f32[128,256]{0,1:T(8,128)}, u32[]{:S(2)}) copy-start(f32[128,256]{0,1:T(8,128)} %get-tuple-element.223) | copy-start | bytes 393220
  146.3 8.4 %collective-permute-start.11 = (f32[71680]{0:T(1024)S(1)}, f32[71680]{0:T(1024)S(1)}, u32[]{:S(2)}, u32[]{:S(2)}) collective-permute-start(f32[71680]{0:T(1024)S(1)} %slice_select_fusion.1), channel_id=1, source_target_pairs={{0,16},{8,24},{16,0},{24,8},{32,48},{40,56},{48,32},{56,40},{64,80... | collective-permute-start | bytes 860168 | tf_op jit(solution)/shard_map/ppermute | solution.py:213
  154.7 5.5 %collective-permute-start.12 = (f32[35840]{0:T(1024)S(1)}, f32[35840]{0:T(1024)S(1)}, u32[]{:S(2)}, u32[]{:S(2)}) collective-permute-start(f32[35840]{0:T(1024)S(1)} %slice_select_fusion.2), channel_id=1, source_target_pairs={{0,32},{8,40},{16,48},{24,56},{32,0},{40,8},{48,16},{56,24},{64,96... | collective-permute-start | bytes 430088 | tf_op jit(solution)/shard_map/ppermute | solution.py:213
  160.3 4.0 %collective-permute-start.13 = (f32[35840]{0:T(1024)S(1)}, f32[35840]{0:T(1024)S(1)}, u32[]{:S(2)}, u32[]{:S(2)}) collective-permute-start(f32[35840]{0:T(1024)S(1)} %select_add_fusion.2), channel_id=1, source_target_pairs={{0,64},{8,72},{16,80},{24,88},{32,96},{40,104},{48,112},{56,120},{... | collective-permute-start | bytes 430088 | tf_op jit(solution)/shard_map/ppermute | solution.py:216
  164.4 6.5 %collective-permute-start.14 = (f32[35840]{0:T(1024)S(1)}, f32[35840]{0:T(1024)S(1)}, u32[]{:S(2)}, u32[]{:S(2)}) collective-permute-start(f32[35840]{0:T(1024)S(1)} %add.439), channel_id=1, source_target_pairs={{0,128},{8,136},{16,144},{24,152},{32,160},{40,168},{48,176},{56,1... | collective-permute-start | bytes 430088 | tf_op jit(solution)/shard_map/ppermute | solution.py:216
  170.9 5.9 %collective-permute-start.15 = (f32[35840]{0:T(1024)S(1)}, f32[35840]{0:T(1024)S(1)}, u32[]{:S(2)}, u32[]{:S(2)}) collective-permute-start(f32[35840]{0:T(1024)S(1)} %add.440), channel_id=1, source_target_pairs={{0,1},{1,0},{2,3},{3,2},{4,5},{5,4},{6,7},{7,6},{8,9},{9,8},{10,11... | collective-permute-start | bytes 430088 | tf_op jit(solution)/shard_map/ppermute | solution.py:216
  176.8 8.9 %collective-permute-start.16 = (f32[35840]{0:T(1024)S(1)}, f32[35840]{0:T(1024)S(1)}, u32[]{:S(2)}, u32[]{:S(2)}) collective-permute-start(f32[35840]{0:T(1024)S(1)} %add.441), channel_id=1, source_target_pairs={{0,2},{1,3},{2,0},{3,1},{4,6},{5,7},{6,4},{7,5},{8,10},{9,11},{10,... | collective-permute-start | bytes 430088 | tf_op jit(solution)/shard_map/ppermute | solution.py:216
  185.7 8.1 %collective-permute-start.17 = (f32[35840]{0:T(1024)S(1)}, f32[35840]{0:T(1024)S(1)}, u32[]{:S(2)}, u32[]{:S(2)}) collective-permute-start(f32[35840]{0:T(1024)S(1)} %add.442), channel_id=1, source_target_pairs={{0,4},{1,5},{2,6},{3,7},{4,0},{5,1},{6,2},{7,3},{8,12},{9,13},{10,... | collective-permute-start | bytes 430088 | tf_op jit(solution)/shard_map/ppermute | solution.py:216
  193.9 5.5 %collective-permute-start.18 = (f32[35840]{0:T(1024)S(1)}, f32[35840]{0:T(1024)S(1)}, u32[]{:S(2)}, u32[]{:S(2)}) collective-permute-start(f32[35840]{0:T(1024)S(1)} %add.443), channel_id=1, source_target_pairs={{0,32},{8,40},{16,48},{24,56},{32,0},{40,8},{48,16},{56,24},{64,96... | collective-permute-start | bytes 430088 | tf_op jit(solution)/shard_map/ppermute | solution.py:218
  199.4 5.9 %collective-permute-start.19 = (f32[71680]{0:T(1024)S(1)}, f32[71680]{0:T(1024)S(1)}, u32[]{:S(2)}, u32[]{:S(2)}) collective-permute-start(f32[71680]{0:T(1024)S(1)} %maximum_select_fusion.4), channel_id=1, source_target_pairs={{0,16},{8,24},{16,0},{24,8},{32,48},{40,56},{48,32},{56,40},{64,80... | collective-permute-start | bytes 860168 | tf_op jit(solution)/shard_map/ppermute | solution.py:218
  205.3 19.5 %collective-permute-start.20 = (f32[143360]{0:T(1024)S(1)}, f32[143360]{0:T(1024)S(1)}, u32[]{:S(2)}, u32[]{:S(2)}) collective-permute-start(f32[143360]{0:T(1024)S(1)} %maximum_select_fusion.2), channel_id=1, source_target_pairs={{0,8},{8,0},{16,24},{24,16},{32,40},{40,32},{48,56},{56,48},{64,72... | collective-permute-start | bytes 1720328 | tf_op jit(solution)/shard_map/ppermute | solution.py:218

commit v2 on v0

--- a/solution.py
+++ b/solution.py
@@ -166,7 +166,6 @@
     ).astype(jnp.bfloat16)
     kernel_third = weight_grads(third_padded, third_delta, SX // 4, coarse_depth, w_third)
     bias_third = bias_sum(third_delta)
-    kernel_third, bias_third = lax.psum((kernel_third, bias_third), ("sample", "slab"))
     delta_window = with_halo(third_delta, (("slab", 2),), 1)
     second_back = data_grads(delta_window, flipped_third, SX // 4, coarse_depth)
     second_delta = (
@@ -183,9 +182,10 @@
     ).astype(jnp.bfloat16)
     kernel_first = weight_grads(volume_padded, first_delta, SX, CZ, w_first)
     bias_first = bias_sum(first_delta)
-    kernel_first, bias_first, kernel_second, bias_second = lax.psum(
-        (kernel_first, bias_first, kernel_second, bias_second), ("sample", "slab")
-    )
+    weights = all_reduce_rows(
+        (kernel_third, kernel_second, kernel_first, bias_third, bias_second, bias_first)
+    )
+    kernel_third, kernel_second, kernel_first, bias_third, bias_second, bias_first = weights
     return (
         features,
         kernel_first,
@@ -197,6 +197,55 @@
     )
 
 
+def xor_pairs(axis, mask):
+    return [(i, i ^ mask) for i in range(lax.axis_size(axis))]
+
+
+def all_reduce_rows(grads, halving_steps=3, lanes=128):
+    steps = []
+    for axis in ("sample", "slab"):
+        mask = 1
+        while mask < lax.axis_size(axis):
+            steps.append((axis, mask))
+            mask *= 2
+    pieces, offsets = [], []
+    rows = 0
+    for g in grads:
+        count = -(-g.size // lanes)
+        flat = g.reshape(-1)
+        flat = jnp.pad(flat, (0, count * lanes - g.size))
+        pieces.append(flat.reshape(count, lanes))
+        offsets.append(rows)
+        rows += count
+    block = 8 << halving_steps
+    total = -(-rows // block) * block
+    if total > rows:
+        pieces.append(jnp.zeros((total - rows, lanes), jnp.float32))
+    buffer = jnp.concatenate(pieces, axis=0)
+    kept = []
+    for axis, mask in steps[:halving_steps]:
+        half = buffer.shape[0] // 2
+        upper = ((lax.axis_index(axis) // mask) % 2).astype(jnp.int32)
+        send = lax.dynamic_slice_in_dim(buffer, (1 - upper) * half, half, axis=0)
+        keep = lax.dynamic_slice_in_dim(buffer, upper * half, half, axis=0)
+        buffer = keep + lax.ppermute(send, axis, xor_pairs(axis, mask))
+        kept.append((axis, mask, upper))
+    for axis, mask in steps[halving_steps:]:
+        buffer = buffer + lax.ppermute(buffer, axis, xor_pairs(axis, mask))
+    for axis, mask, upper in reversed(kept):
+        other = lax.ppermute(buffer, axis, xor_pairs(axis, mask))
+        pair = jnp.stack([buffer, other])
+        first = lax.dynamic_index_in_dim(pair, upper, axis=0, keepdims=False)
+        second = lax.dynamic_index_in_dim(pair, 1 - upper, axis=0, keepdims=False)
+        buffer = jnp.concatenate([first, second], axis=0)
+    out = []
+    for g, start in zip(grads, offsets):
+        count = -(-g.size // lanes)
+        part = buffer[start : start + count].reshape(-1)[: g.size]
+        out.append(part.reshape(g.shape))
+    return tuple(out)
+
+
 def solution(mesh):
     in_specs = (
         P(None, "sample", "slab", None),

time: 400 us -> 211 us (0.53)
  waiting for transfers between devices: 160 us -> 38 us
  blocking collectives: 85.7 us -> 0 us
  starting transfers between devices: 30.9 us -> 74.9 us
  between operations: 15.3 us -> 2.11 us
  local copies, waits for them, and re-layouts: 61 us -> 52.4 us
  matrix products: 18 us -> 13.4 us
    psum x1 -> x0, waiting for transfers between devices: 155 us -> none  [per_device(): lax.psum((kernel_first, bias_first, kernel_second, bias_second), ('sample...]
    psum x1 -> x0, blocking collectives: 85.7 us -> none  [per_device(): lax.psum((kernel_first, bias_first, kernel_second, bias_second), ('sample...]
    ppermute x0 -> x11, starting transfers between devices: none -> 44.1 us  [the longest x5 19.8 us: all_reduce_rows(): buffer = buffer + lax.ppermute(buffer, axis, xor_pairs(axis, mask))]
    ppermute x0 -> x11, waiting for transfers between devices: none -> 35.9 us  [the longest x5 16 us: all_reduce_rows(): buffer = buffer + lax.ppermute(buffer, axis, xor_pairs(axis, mask))]
    dot_general x1 -> x0, local copies, waits for them, and re-layouts: 6.56 us -> none  [weight_term(): jnp.einsum('kgzp,ogzp->ko', patches, grad_block, preferred_element_type=j...]
    unnamed x52 -> x51, local copies, waits for them, and re-layouts: 12.9 us -> 7.36 us
    ppermute x5, waiting for transfers between devices: 4.94 us -> 0.01 us  [with_halo(): after = lax.ppermute(first, axis, down)]
    dot_general x3, matrix products: 9.02 us -> 4.59 us  [weight_term(): jnp.einsum('kgzp,ogzp->ko', patches, grad_block, preferred_element_type=j...]
  transfers between devices with their start and end apart: 11 -> 21, of which waited for: 3 -> 14; matrix products, arithmetic and copies ran while one was open for 11% -> 4% of each run, Pallas kernels for 0% -> 0%
where the time goes in v2:
time: 211 us; the launch traced here: 207 us
  starting transfers between devices  74.9 us (35%)
  local copies, waits for them, and re-layouts  52.4 us (25%)
  waiting for transfers between devices  38 us (18%)
  other arithmetic  25.7 us (12%)
  matrix products  13.4 us (6%)
  between operations  2.11 us (1%)
    ppermute x5, starting transfers between devices, with_halo(): before = lax.ppermute(last, axis, up)  24.3 us
    concatenate x2, local copies, waits for them, and re-layouts, gather_taps(): return jnp.concatenate(pieces, axis=0)  19.9 us
    ppermute x5, starting transfers between devices, all_reduce_rows(): buffer = buffer + lax.ppermute(buffer, axis, xor_pairs(axis, mask))  19.8 us
    ppermute x3, starting transfers between devices, all_reduce_rows(): other = lax.ppermute(buffer, axis, xor_pairs(axis, mask))  16.3 us
    ppermute x5, waiting for transfers between devices, all_reduce_rows(): buffer = buffer + lax.ppermute(buffer, axis, xor_pairs(axis, mask))  16 us
    ppermute x3, waiting for transfers between devices, all_reduce_rows(): buffer = keep + lax.ppermute(send, axis, xor_pairs(axis, mask))  12.2 us
    reduce_sum x2, other arithmetic, pool_cells(): grouped.mean(axis=(3, 5, 7))  9.96 us
    dot_general x5, matrix products, apply_weight(): jnp.einsum('ko,kgzp->ogzp', flat_weight, patches, preferred_element_type=...  8.8 us
  transfers between devices with their start and end apart: 21, of which 14 were waited for; matrix products, arithmetic and copies ran while one was open for 4% of the time, Pallas kernels for 0%

profile of v2, /device:TPU:1, one launch (start us, length us, event | category | flops | bytes accessed | tf_op | source)
XLA Modules:
  0.0 206.5 jit_solution(10724011970554189238)
XLA Ops:
  0.6 1.0 copy.52
  1.7 1.3 collective-permute-start.1
  3.0 5.0 %collective-permute-start = (bf16[4,1,1,4096]{3,0,2,1:T(4,128)(2,1)S(1)}, bf16[4,1,1,4096]{3,0,2,1:T(4,128)(2,1)S(1)}, u32[]{:S(2)}, u32[]{:S(2)}) collective-permute-start(bf16[4,1,1,4096]{3,0,2,1:T(4,128)(2,1)S(1)} %get-tuple-element.227), channel_id=1, source_target_pairs={{0,1},{1,2},{2,3},{3,4},{4,5},{5,6},{6,7},{8,9},{9,10},{10,11},{11... | collective-permute-start | bytes 98312 | tf_op jit(solution)/shard_map/ppermute | solution.py:17
  8.0 1.0 reverse_bitcast_fusion
  10.0 1.4 reshape.362
  12.8 1.3 slice_multiply_fusion.36
  14.1 1.7 slice_multiply_fusion.37
  15.8 16.5 %concatenate.74 = bf16[108,1,4,4096]{3,0,2,1:T(8,128)(2,1)} concatenate(bf16[4,1,4,4096]{3,0,2,1:T(4,128)(2,1)} %get-tuple-element.216, bf16[4,1,4,4096]{3,0,2,1:T(4,128)(2,1)S(1)} %get-tuple-element.222, bf16[4,1,4,4096]{3,0,2,1:T(4,128)(2,1)S(1)} %get-tuple-element.207, bf16[4,1,4,4096]{3,0,2,1:T(4,128)(2,1)} %get-tuple-element.215, ...), dimensions={0} | concatenate | bytes 7077888 | tf_op jit(solution)/shard_map/while/body/eval_jaxpr/concatenate | solution.py:53
  32.3 4.6 %fusion.12 = (f32[32,4,4096]{2,0,1:T(8,128)S(1)}, f32[32,4,4096]{2,0,1:T(8,128)}) fusion(f32[32]{0:T(128)S(1)} %copy-done.9, bf16[108,32]{1,0:T(8,128)(2,1)} %reshape.362, bf16[108,1,4,4096]{3,0,2,1:T(8,128)(2,1)} %concatenate.74), kind=kOutput, calls=%fused_computation.16 | convolution fusion | flops 116916224 | bytes 7740288 | tf_op jit(solution)/shard_map/while/body/eval_jaxpr/ko,kgzp->ogzp/dot_general | solution.py:58
  37.0 4.7 %copy.59 = f32[32,4,4096]{0,2,1:T(8,128)} copy(f32[32,4,4096]{2,0,1:T(8,128)S(1)} %get-tuple-element.229) | data formatting | bytes 4194304 | tf_op jit(solution)/shard_map/while/body/eval_jaxpr/jit(silu)/mul | solution.py:103
  41.7 9.5 %reduce_sum.54 = f32[32,2,64,16]{0,3,2,1:T(8,128)S(1)} reduce(f32[32,2,2,64,2,16,2]{0,6,5,4,3,2,1:T(2,128)} %bitcast.145, f32[]{:T(128)} %constant.301.clone.1), dimensions={2,4,6}, to_apply=%region_0.1 | reduce | flops 458752 | bytes 2359300 | tf_op jit(solution)/shard_map/while/body/eval_jaxpr/reduce_sum | solution.py:72
  51.5 1.3 collective-permute-start.3
  52.8 4.3 %collective-permute-start.2 = (bf16[32,1,1,1024]{3,0,2,1:T(8,128)(2,1)S(1)}, bf16[32,1,1,1024]{3,0,2,1:T(8,128)(2,1)S(1)}, u32[]{:S(2)}, u32[]{:S(2)}) collective-permute-start(bf16[32,1,1,1024]{3,0,2,1:T(8,128)(2,1)S(1)} %get-tuple-element.223), channel_id=1, source_target_pairs={{0,1},{1,2},{2,3},{3,4},{4,5},{5,6},{6,7},{8,9},{9,10},{10,11},{11... | collective-permute-start | bytes 196616 | tf_op jit(solution)/shard_map/ppermute | solution.py:17
  57.2 1.1 collective-permute-done.2
  63.4 1.3 collective-permute-start.5
  64.7 4.3 %collective-permute-start.4 = (bf16[64,1,1,256]{0,3,2,1:T(8,128)(2,1)S(1)}, bf16[64,1,1,256]{0,3,2,1:T(8,128)(2,1)S(1)}, u32[]{:S(2)}, u32[]{:S(2)}) collective-permute-start(bf16[64,1,1,256]{0,3,2,1:T(8,128)(2,1)S(1)} %fusion.122), channel_id=1, source_target_pairs={{0,1},{1,2},{2,3},{3,4},{4,5},{5,6},{6,7},{8,9},{9,10},{10,11},{11... | collective-permute-start | bytes 98312 | tf_op jit(solution)/shard_map/ppermute | solution.py:17
  70.5 1.0 slice_multiply_fusion.72
  71.5 3.3 %concatenate.80 = bf16[1728,1,1,256]{0,3,2,1:T(8,128)(2,1)S(1)} concatenate(bf16[64,1,1,256]{0,3,2,1:T(8,128)(2,1)S(1)} %get-tuple-element.192, bf16[64,1,1,256]{0,3,2,1:T(8,128)(2,1)} %get-tuple-element.198, bf16[64,1,1,256]{0,3,2,1:T(8,128)(2,1)} %get-tuple-element.183, bf16[64,1,1,256]{0,3,2,1:T(8,128)(2,1)S(1)} %get-tuple-element.191, ...), dimensions={0} | concatenate | bytes 1769472 | tf_op jit(solution)/shard_map/while/body/eval_jaxpr/concatenate | solution.py:53
  74.9 1.3 convert_reduce_fusion.2
  76.2 1.3 collective-permute-start.7
  77.5 5.2 %collective-permute-start.6 = (bf16[128,1,1,256]{0,3,2,1:T(8,128)(2,1)S(1)}, bf16[128,1,1,256]{0,3,2,1:T(8,128)(2,1)S(1)}, u32[]{:S(2)}, u32[]{:S(2)}) collective-permute-start(bf16[128,1,1,256]{0,3,2,1:T(8,128)(2,1)S(1)} %get-tuple-element.149), channel_id=1, source_target_pairs={{0,1},{1,2},{2,3},{3,4},{4,5},{5,6},{6,7},{8,9},{9,10},{10,11},{11... | collective-permute-start | bytes 196616 | tf_op jit(solution)/shard_map/ppermute | solution.py:17
  88.0 1.3 collective-permute-start.9
  89.3 5.4 %collective-permute-start.8 = (bf16[64,1,1,1024]{3,0,2,1:T(8,128)(2,1)S(1)}, bf16[64,1,1,1024]{3,0,2,1:T(8,128)(2,1)S(1)}, u32[]{:S(2)}, u32[]{:S(2)}) collective-permute-start(bf16[64,1,1,1024]{3,0,2,1:T(8,128)(2,1)S(1)} %get-tuple-element.173), channel_id=1, source_target_pairs={{0,1},{1,2},{2,3},{3,4},{4,5},{5,6},{6,7},{8,9},{9,10},{10,11},{11... | collective-permute-start | bytes 393224 | tf_op jit(solution)/shard_map/ppermute | solution.py:17
  94.8 3.1 %fusion.18 = f32[864,64]{1,0:T(8,128)S(1)} fusion(bf16[64,2,1024]{2,0,1:T(8,128)(2,1)S(1)} %get-tuple-element.147, bf16[864,1,2,1024]{3,0,2,1:T(8,128)(2,1)} %copy-done.8), kind=kOutput, calls=%fused_computation.26 | convolution fusion | flops 226492416 | bytes 4022272 | tf_op jit(solution)/shard_map/while/body/eval_jaxpr/kgzp,ogzp->ko/dot_general | solution.py:62
  101.7 1.3 fusion.40
  103.4 7.6 %broadcast_in_dim.16 = f32[32,2,2,64,2,16,2]{0,6,5,4,3,2,1:T(2,128)} broadcast(f32[32,2,64,16]{0,3,2,1:T(8,128)S(1)} %bitcast.151), dimensions={0,1,3,5} | broadcast | bytes 2359296 | tf_op jit(solution)/shard_map/broadcast_in_dim | solution.py:79
  111.0 5.1 %copy.75 = f32[32,4,4096]{2,0,1:T(8,128)S(1)} copy(f32[32,4,4096]{0,2,1:T(8,128)} %bitcast.146) | data formatting | bytes 4194304 | tf_op jit(solution)/shard_map/mul | solution.py:82
  116.2 2.7 %convert_reduce_fusion = (f32[32]{0:T(128)S(1)}, bf16[32,4,4096]{2,0,1:T(8,128)(2,1)S(1)}) fusion(f32[32,4,4096]{2,0,1:T(8,128)S(1)} %copy.75, f32[32,4,4096]{2,0,1:T(8,128)} %get-tuple-element.230), kind=kLoop, calls=%fused_computation.13 | loop fusion | flops 5767136 | bytes 5243008 | tf_op jit(solution)/shard_map/reduce_sum | solution.py:147
  118.8 1.1 fusion.46
  120.5 4.9 %collective-permute-start.10 = (f32[1120,128]{1,0:T(8,128)S(1)}, f32[1120,128]{1,0:T(8,128)S(1)}, u32[]{:S(2)}, u32[]{:S(2)}) collective-permute-start(f32[1120,128]{1,0:T(8,128)S(1)} %constant_dynamic-slice_fusion.2), channel_id=1, source_target_pairs={{0,8},{8,0},{16,24},{24,16},{32,40},{40,32},{48,56},{56,48},{64,72... | collective-permute-start | bytes 1720328 | tf_op jit(solution)/shard_map/ppermute | solution.py:231
  125.4 1.6 collective-permute-done.10
  127.9 7.4 %collective-permute-done.11 = f32[560,128]{1,0:T(8,128)S(1)} collective-permute-done((f32[560,128]{1,0:T(8,128)S(1)}, f32[560,128]{1,0:T(8,128)S(1)}, u32[]{:S(2)}, u32[]{:S(2)}) %collective-permute-start.11) | collective-permute-done | bytes 286752 | tf_op jit(solution)/shard_map/ppermute | solution.py:231
  135.3 2.4 %collective-permute-start.12 = (f32[280,128]{1,0:T(8,128)S(1)}, f32[280,128]{1,0:T(8,128)S(1)}, u32[]{:S(2)}, u32[]{:S(2)}) collective-permute-start(f32[280,128]{1,0:T(8,128)S(1)} %constant_dynamic-slice_fusion), channel_id=1, source_target_pairs={{0,32},{8,40},{16,48},{24,56},{32,0},{40,8},{48,16},{56,24},{64,96... | collective-permute-start | bytes 430088 | tf_op jit(solution)/shard_map/ppermute | solution.py:231
  137.7 3.2 %collective-permute-done.12 = f32[280,128]{1,0:T(8,128)S(1)} collective-permute-done((f32[280,128]{1,0:T(8,128)S(1)}, f32[280,128]{1,0:T(8,128)S(1)}, u32[]{:S(2)}, u32[]{:S(2)}) %collective-permute-start.12) | collective-permute-done | bytes 143392 | tf_op jit(solution)/shard_map/ppermute | solution.py:231
  141.8 3.4 %collective-permute-done.13 = f32[280,128]{1,0:T(8,128)S(1)} collective-permute-done((f32[280,128]{1,0:T(8,128)S(1)}, f32[280,128]{1,0:T(8,128)S(1)}, u32[]{:S(2)}, u32[]{:S(2)}) %collective-permute-start.13) | collective-permute-done | bytes 143392 | tf_op jit(solution)/shard_map/ppermute | solution.py:234
  145.2 2.2 %collective-permute-start.14 = (f32[280,128]{1,0:T(8,128)S(1)}, f32[280,128]{1,0:T(8,128)S(1)}, u32[]{:S(2)}, u32[]{:S(2)}) collective-permute-start(f32[280,128]{1,0:T(8,128)S(1)} %add.505), channel_id=1, source_target_pairs={{0,128},{8,136},{16,144},{24,152},{32,160},{40,168},{48,176},{56,1... | collective-permute-start | bytes 430088 | tf_op jit(solution)/shard_map/ppermute | solution.py:234
  147.4 3.7 %collective-permute-done.14 = f32[280,128]{1,0:T(8,128)S(1)} collective-permute-done((f32[280,128]{1,0:T(8,128)S(1)}, f32[280,128]{1,0:T(8,128)S(1)}, u32[]{:S(2)}, u32[]{:S(2)}) %collective-permute-start.14) | collective-permute-done | bytes 143392 | tf_op jit(solution)/shard_map/ppermute | solution.py:234
  151.1 3.4 %collective-permute-start.15 = (f32[280,128]{1,0:T(8,128)S(1)}, f32[280,128]{1,0:T(8,128)S(1)}, u32[]{:S(2)}, u32[]{:S(2)}) collective-permute-start(f32[280,128]{1,0:T(8,128)S(1)} %add.506), channel_id=1, source_target_pairs={{0,1},{1,0},{2,3},{3,2},{4,5},{5,4},{6,7},{7,6},{8,9},{9,8},{10,11... | collective-permute-start | bytes 430088 | tf_op jit(solution)/shard_map/ppermute | solution.py:234
  154.5 2.5 %collective-permute-done.15 = f32[280,128]{1,0:T(8,128)S(1)} collective-permute-done((f32[280,128]{1,0:T(8,128)S(1)}, f32[280,128]{1,0:T(8,128)S(1)}, u32[]{:S(2)}, u32[]{:S(2)}) %collective-permute-start.15) | collective-permute-done | bytes 143392 | tf_op jit(solution)/shard_map/ppermute | solution.py:234
  157.0 6.4 %collective-permute-start.16 = (f32[280,128]{1,0:T(8,128)S(1)}, f32[280,128]{1,0:T(8,128)S(1)}, u32[]{:S(2)}, u32[]{:S(2)}) collective-permute-start(f32[280,128]{1,0:T(8,128)S(1)} %add.507), channel_id=1, source_target_pairs={{0,2},{1,3},{2,0},{3,1},{4,6},{5,7},{6,4},{7,5},{8,10},{9,11},{10,... | collective-permute-start | bytes 430088 | tf_op jit(solution)/shard_map/ppermute | solution.py:234
  163.4 2.8 %collective-permute-done.16 = f32[280,128]{1,0:T(8,128)S(1)} collective-permute-done((f32[280,128]{1,0:T(8,128)S(1)}, f32[280,128]{1,0:T(8,128)S(1)}, u32[]{:S(2)}, u32[]{:S(2)}) %collective-permute-start.16) | collective-permute-done | bytes 143392 | tf_op jit(solution)/shard_map/ppermute | solution.py:234
  166.2 7.0 %collective-permute-start.17 = (f32[280,128]{1,0:T(8,128)S(1)}, f32[280,128]{1,0:T(8,128)S(1)}, u32[]{:S(2)}, u32[]{:S(2)}) collective-permute-start(f32[280,128]{1,0:T(8,128)S(1)} %add.508), channel_id=1, source_target_pairs={{0,4},{1,5},{2,6},{3,7},{4,0},{5,1},{6,2},{7,3},{8,12},{9,13},{10,... | collective-permute-start | bytes 430088 | tf_op jit(solution)/shard_map/ppermute | solution.py:234
  173.2 3.7 %collective-permute-done.17 = f32[280,128]{1,0:T(8,128)S(1)} collective-permute-done((f32[280,128]{1,0:T(8,128)S(1)}, f32[280,128]{1,0:T(8,128)S(1)}, u32[]{:S(2)}, u32[]{:S(2)}) %collective-permute-start.17) | collective-permute-done | bytes 143392 | tf_op jit(solution)/shard_map/ppermute | solution.py:234
  176.9 3.0 %collective-permute-start.18 = (f32[280,128]{1,0:T(8,128)S(1)}, f32[280,128]{1,0:T(8,128)S(1)}, u32[]{:S(2)}, u32[]{:S(2)}) collective-permute-start(f32[280,128]{1,0:T(8,128)S(1)} %add.509), channel_id=1, source_target_pairs={{0,32},{8,40},{16,48},{24,56},{32,0},{40,8},{48,16},{56,24},{64,96... | collective-permute-start | bytes 430088 | tf_op jit(solution)/shard_map/ppermute | solution.py:236
  179.8 2.6 %collective-permute-done.18 = f32[280,128]{1,0:T(8,128)S(1)} collective-permute-done((f32[280,128]{1,0:T(8,128)S(1)}, f32[280,128]{1,0:T(8,128)S(1)}, u32[]{:S(2)}, u32[]{:S(2)}) %collective-permute-start.18) | collective-permute-done | bytes 143392 | tf_op jit(solution)/shard_map/ppermute | solution.py:236
  182.5 1.3 collective-permute-start.19
  183.9 4.2 %collective-permute-done.19 = f32[560,128]{1,0:T(8,128)S(1)} collective-permute-done((f32[560,128]{1,0:T(8,128)S(1)}, f32[560,128]{1,0:T(8,128)S(1)}, u32[]{:S(2)}, u32[]{:S(2)}) %collective-permute-start.19) | collective-permute-done | bytes 286752 | tf_op jit(solution)/shard_map/ppermute | solution.py:236
  188.3 12.0 %collective-permute-start.20 = (f32[1120,128]{1,0:T(8,128)S(1)}, f32[1120,128]{1,0:T(8,128)S(1)}, u32[]{:S(2)}, u32[]{:S(2)}) collective-permute-start(f32[1120,128]{1,0:T(8,128)S(1)} %get-tuple-element.157), channel_id=1, source_target_pairs={{0,8},{8,0},{16,24},{24,16},{32,40},{40,32},{48,56},{56,48},{64,72... | collective-permute-start | bytes 1720328 | tf_op jit(solution)/shard_map/ppermute | solution.py:236
  (179 shorter events, 26.8 us)
Async XLA Ops:
  1.7 9.7 %collective-permute-start.1 = (bf16[4,1,1,4096]{3,0,2,1:T(4,128)(2,1)S(1)}, bf16[4,1,1,4096]{3,0,2,1:T(4,128)(2,1)S(1)}, u32[]{:S(2)}, u32[]{:S(2)}) collective-permute-start(bf16[4,1,1,4096]{3,0,2,1:T(4,128)(2,1)S(1)} %get-tuple-element.228), channel_id=1, source_target_pairs={{1,0},{2,1},{3,2},{4,3},{5,4},{6,5},{7,6},{9,8},{10,9},{11,10},{12... | collective-permute-start | bytes 98312 | tf_op jit(solution)/shard_map/ppermute | solution.py:18
  3.0 8.4 %collective-permute-start = (bf16[4,1,1,4096]{3,0,2,1:T(4,128)(2,1)S(1)}, bf16[4,1,1,4096]{3,0,2,1:T(4,128)(2,1)S(1)}, u32[]{:S(2)}, u32[]{:S(2)}) collective-permute-start(bf16[4,1,1,4096]{3,0,2,1:T(4,128)(2,1)S(1)} %get-tuple-element.227), channel_id=1, source_target_pairs={{0,1},{1,2},{2,3},{3,4},{4,5},{5,6},{6,7},{8,9},{9,10},{10,11},{11... | collective-permute-start | bytes 98312 | tf_op jit(solution)/shard_map/ppermute | solution.py:17
  11.4 0.6 copy-start.3
  12.0 0.6 copy-start.5
  12.8 1.3 copy-start.4
  12.8 1.3 copy-start.6
  15.8 16.5 %copy-start.9 = (f32[32]{0:T(128)S(1)}, f32[32]{0:T(128)}, u32[]{:S(2)}) copy-start(f32[32]{0:T(128)} %param.11) | copy-start | bytes 388
  51.5 5.7 %collective-permute-start.3 = (bf16[32,1,1,1024]{3,0,2,1:T(8,128)(2,1)S(1)}, bf16[32,1,1,1024]{3,0,2,1:T(8,128)(2,1)S(1)}, u32[]{:S(2)}, u32[]{:S(2)}) collective-permute-start(bf16[32,1,1,1024]{3,0,2,1:T(8,128)(2,1)S(1)} %get-tuple-element.224), channel_id=1, source_target_pairs={{1,0},{2,1},{3,2},{4,3},{5,4},{6,5},{7,6},{9,8},{10,9},{11,10},{12... | collective-permute-start | bytes 196616 | tf_op jit(solution)/shard_map/ppermute | solution.py:18
  52.8 5.5 %collective-permute-start.2 = (bf16[32,1,1,1024]{3,0,2,1:T(8,128)(2,1)S(1)}, bf16[32,1,1,1024]{3,0,2,1:T(8,128)(2,1)S(1)}, u32[]{:S(2)}, u32[]{:S(2)}) collective-permute-start(bf16[32,1,1,1024]{3,0,2,1:T(8,128)(2,1)S(1)} %get-tuple-element.223), channel_id=1, source_target_pairs={{0,1},{1,2},{2,3},{3,4},{4,5},{5,6},{6,7},{8,9},{9,10},{10,11},{11... | collective-permute-start | bytes 196616 | tf_op jit(solution)/shard_map/ppermute | solution.py:17
  58.5 2.5 %copy-start.2 = (bf16[27,32,64]{2,1,0:T(8,128)(2,1)S(1)}, bf16[27,32,64]{2,1,0:T(8,128)(2,1)}, u32[]{:S(2)}) copy-start(bf16[27,32,64]{2,1,0:T(8,128)(2,1)} %param.12) | copy-start | bytes 331780
  58.5 2.5 %copy-start.10 = (f32[64]{0:T(128)S(1)}, f32[64]{0:T(128)}, u32[]{:S(2)}) copy-start(f32[64]{0:T(128)} %param.13) | copy-start | bytes 772
  61.0 1.8 copy-start.8
  61.0 8.0 %copy-start.7 = (bf16[128,1,1,256]{3,0,2,1:T(8,128)(2,1)S(1)}, bf16[128,1,1,256]{3,0,2,1:T(8,128)(2,1)}, u32[]{:S(2)}) copy-start(bf16[128,1,1,256]{3,0,2,1:T(8,128)(2,1)} %param.9) | copy-start | bytes 196612
  63.4 6.8 %collective-permute-start.5 = (bf16[64,1,1,256]{0,3,2,1:T(8,128)(2,1)S(1)}, bf16[64,1,1,256]{0,3,2,1:T(8,128)(2,1)S(1)}, u32[]{:S(2)}, u32[]{:S(2)}) collective-permute-start(bf16[64,1,1,256]{0,3,2,1:T(8,128)(2,1)S(1)} %fusion.122), channel_id=1, source_target_pairs={{1,0},{2,1},{3,2},{4,3},{5,4},{6,5},{7,6},{9,8},{10,9},{11,10},{12... | collective-permute-start | bytes 98312 | tf_op jit(solution)/shard_map/ppermute | solution.py:18
  64.7 5.6 %collective-permute-start.4 = (bf16[64,1,1,256]{0,3,2,1:T(8,128)(2,1)S(1)}, bf16[64,1,1,256]{0,3,2,1:T(8,128)(2,1)S(1)}, u32[]{:S(2)}, u32[]{:S(2)}) collective-permute-start(bf16[64,1,1,256]{0,3,2,1:T(8,128)(2,1)S(1)} %fusion.122), channel_id=1, source_target_pairs={{0,1},{1,2},{2,3},{3,4},{4,5},{5,6},{6,7},{8,9},{9,10},{10,11},{11... | collective-permute-start | bytes 98312 | tf_op jit(solution)/shard_map/ppermute | solution.py:17
  69.8 5.1 %copy-start.1 = (bf16[27,64,128]{2,1,0:T(8,128)(2,1)S(1)}, bf16[27,64,128]{2,1,0:T(8,128)(2,1)}, u32[]{:S(2)}) copy-start(bf16[27,64,128]{2,1,0:T(8,128)(2,1)} %param.14) | copy-start | bytes 1327108
  69.8 5.1 %copy-start.11 = (f32[128]{0:T(128)S(1)}, f32[128]{0:T(128)}, u32[]{:S(2)}) copy-start(f32[128]{0:T(128)} %param.15) | copy-start | bytes 1540
  76.2 7.0 %collective-permute-start.7 = (bf16[128,1,1,256]{0,3,2,1:T(8,128)(2,1)S(1)}, bf16[128,1,1,256]{0,3,2,1:T(8,128)(2,1)S(1)}, u32[]{:S(2)}, u32[]{:S(2)}) collective-permute-start(bf16[128,1,1,256]{0,3,2,1:T(8,128)(2,1)S(1)} %get-tuple-element.149), channel_id=1, source_target_pairs={{1,0},{2,1},{3,2},{4,3},{5,4},{6,5},{7,6},{9,8},{10,9},{11,10},{12... | collective-permute-start | bytes 196616 | tf_op jit(solution)/shard_map/ppermute | solution.py:18
  77.5 6.6 %collective-permute-start.6 = (bf16[128,1,1,256]{0,3,2,1:T(8,128)(2,1)S(1)}, bf16[128,1,1,256]{0,3,2,1:T(8,128)(2,1)S(1)}, u32[]{:S(2)}, u32[]{:S(2)}) collective-permute-start(bf16[128,1,1,256]{0,3,2,1:T(8,128)(2,1)S(1)} %get-tuple-element.149), channel_id=1, source_target_pairs={{0,1},{1,2},{2,3},{3,4},{4,5},{5,6},{6,7},{8,9},{9,10},{10,11},{11... | collective-permute-start | bytes 196616 | tf_op jit(solution)/shard_map/ppermute | solution.py:17
  88.0 9.9 %collective-permute-start.9 = (bf16[64,1,1,1024]{3,0,2,1:T(8,128)(2,1)S(1)}, bf16[64,1,1,1024]{3,0,2,1:T(8,128)(2,1)S(1)}, u32[]{:S(2)}, u32[]{:S(2)}) collective-permute-start(bf16[64,1,1,1024]{3,0,2,1:T(8,128)(2,1)S(1)} %get-tuple-element.174), channel_id=1, source_target_pairs={{1,0},{2,1},{3,2},{4,3},{5,4},{6,5},{7,6},{9,8},{10,9},{11,10},{12... | collective-permute-start | bytes 393224 | tf_op jit(solution)/shard_map/ppermute | solution.py:18
  89.3 8.7 %collective-permute-start.8 = (bf16[64,1,1,1024]{3,0,2,1:T(8,128)(2,1)S(1)}, bf16[64,1,1,1024]{3,0,2,1:T(8,128)(2,1)S(1)}, u32[]{:S(2)}, u32[]{:S(2)}) collective-permute-start(bf16[64,1,1,1024]{3,0,2,1:T(8,128)(2,1)S(1)} %get-tuple-element.173), channel_id=1, source_target_pairs={{0,1},{1,2},{2,3},{3,4},{4,5},{5,6},{6,7},{8,9},{9,10},{10,11},{11... | collective-permute-start | bytes 393224 | tf_op jit(solution)/shard_map/ppermute | solution.py:17
  116.2 2.7 %copy-start = (bf16[108,1,4,4096]{3,0,2,1:T(8,128)(2,1)S(1)}, bf16[108,1,4,4096]{3,0,2,1:T(8,128)(2,1)}, u32[]{:S(2)}) copy-start(bf16[108,1,4,4096]{3,0,2,1:T(8,128)(2,1)} %concatenate.74) | copy-start | bytes 10616836
  120.5 6.5 %collective-permute-start.10 = (f32[1120,128]{1,0:T(8,128)S(1)}, f32[1120,128]{1,0:T(8,128)S(1)}, u32[]{:S(2)}, u32[]{:S(2)}) collective-permute-start(f32[1120,128]{1,0:T(8,128)S(1)} %constant_dynamic-slice_fusion.2), channel_id=1, source_target_pairs={{0,8},{8,0},{16,24},{24,16},{32,40},{40,32},{48,56},{56,48},{64,72... | collective-permute-start | bytes 1720328 | tf_op jit(solution)/shard_map/ppermute | solution.py:231
  127.1 8.1 %collective-permute-start.11 = (f32[560,128]{1,0:T(8,128)S(1)}, f32[560,128]{1,0:T(8,128)S(1)}, u32[]{:S(2)}, u32[]{:S(2)}) collective-permute-start(f32[560,128]{1,0:T(8,128)S(1)} %constant_dynamic-slice_fusion.1), channel_id=1, source_target_pairs={{0,16},{8,24},{16,0},{24,8},{32,48},{40,56},{48,32},{56,40},{64,80... | collective-permute-start | bytes 860168 | tf_op jit(solution)/shard_map/ppermute | solution.py:231
  135.3 5.5 %collective-permute-start.12 = (f32[280,128]{1,0:T(8,128)S(1)}, f32[280,128]{1,0:T(8,128)S(1)}, u32[]{:S(2)}, u32[]{:S(2)}) collective-permute-start(f32[280,128]{1,0:T(8,128)S(1)} %constant_dynamic-slice_fusion), channel_id=1, source_target_pairs={{0,32},{8,40},{16,48},{24,56},{32,0},{40,8},{48,16},{56,24},{64,96... | collective-permute-start | bytes 430088 | tf_op jit(solution)/shard_map/ppermute | solution.py:231
  140.9 4.3 %collective-permute-start.13 = (f32[280,128]{1,0:T(8,128)S(1)}, f32[280,128]{1,0:T(8,128)S(1)}, u32[]{:S(2)}, u32[]{:S(2)}) collective-permute-start(f32[280,128]{1,0:T(8,128)S(1)} %dynamic-slice_add_fusion.2), channel_id=1, source_target_pairs={{0,64},{8,72},{16,80},{24,88},{32,96},{40,104},{48,112},{56,120},{... | collective-permute-start | bytes 430088 | tf_op jit(solution)/shard_map/ppermute | solution.py:234
  145.2 5.9 %collective-permute-start.14 = (f32[280,128]{1,0:T(8,128)S(1)}, f32[280,128]{1,0:T(8,128)S(1)}, u32[]{:S(2)}, u32[]{:S(2)}) collective-permute-start(f32[280,128]{1,0:T(8,128)S(1)} %add.505), channel_id=1, source_target_pairs={{0,128},{8,136},{16,144},{24,152},{32,160},{40,168},{48,176},{56,1... | collective-permute-start | bytes 430088 | tf_op jit(solution)/shard_map/ppermute | solution.py:234
  151.1 5.9 %collective-permute-start.15 = (f32[280,128]{1,0:T(8,128)S(1)}, f32[280,128]{1,0:T(8,128)S(1)}, u32[]{:S(2)}, u32[]{:S(2)}) collective-permute-start(f32[280,128]{1,0:T(8,128)S(1)} %add.506), channel_id=1, source_target_pairs={{0,1},{1,0},{2,3},{3,2},{4,5},{5,4},{6,7},{7,6},{8,9},{9,8},{10,11... | collective-permute-start | bytes 430088 | tf_op jit(solution)/shard_map/ppermute | solution.py:234
  157.0 9.2 %collective-permute-start.16 = (f32[280,128]{1,0:T(8,128)S(1)}, f32[280,128]{1,0:T(8,128)S(1)}, u32[]{:S(2)}, u32[]{:S(2)}) collective-permute-start(f32[280,128]{1,0:T(8,128)S(1)} %add.507), channel_id=1, source_target_pairs={{0,2},{1,3},{2,0},{3,1},{4,6},{5,7},{6,4},{7,5},{8,10},{9,11},{10,... | collective-permute-start | bytes 430088 | tf_op jit(solution)/shard_map/ppermute | solution.py:234
  166.2 10.6 %collective-permute-start.17 = (f32[280,128]{1,0:T(8,128)S(1)}, f32[280,128]{1,0:T(8,128)S(1)}, u32[]{:S(2)}, u32[]{:S(2)}) collective-permute-start(f32[280,128]{1,0:T(8,128)S(1)} %add.508), channel_id=1, source_target_pairs={{0,4},{1,5},{2,6},{3,7},{4,0},{5,1},{6,2},{7,3},{8,12},{9,13},{10,... | collective-permute-start | bytes 430088 | tf_op jit(solution)/shard_map/ppermute | solution.py:234
  176.9 5.5 %collective-permute-start.18 = (f32[280,128]{1,0:T(8,128)S(1)}, f32[280,128]{1,0:T(8,128)S(1)}, u32[]{:S(2)}, u32[]{:S(2)}) collective-permute-start(f32[280,128]{1,0:T(8,128)S(1)} %add.509), channel_id=1, source_target_pairs={{0,32},{8,40},{16,48},{24,56},{32,0},{40,8},{48,16},{56,24},{64,96... | collective-permute-start | bytes 430088 | tf_op jit(solution)/shard_map/ppermute | solution.py:236
  182.5 5.6 %collective-permute-start.19 = (f32[560,128]{1,0:T(8,128)S(1)}, f32[560,128]{1,0:T(8,128)S(1)}, u32[]{:S(2)}, u32[]{:S(2)}) collective-permute-start(f32[560,128]{1,0:T(8,128)S(1)} %get-tuple-element.165), channel_id=1, source_target_pairs={{0,16},{8,24},{16,0},{24,8},{32,48},{40,56},{48,32},{56,40},{64,80... | collective-permute-start | bytes 860168 | tf_op jit(solution)/shard_map/ppermute | solution.py:236
  188.3 13.6 %collective-permute-start.20 = (f32[1120,128]{1,0:T(8,128)S(1)}, f32[1120,128]{1,0:T(8,128)S(1)}, u32[]{:S(2)}, u32[]{:S(2)}) collective-permute-start(f32[1120,128]{1,0:T(8,128)S(1)} %get-tuple-element.157), channel_id=1, source_target_pairs={{0,8},{8,0},{16,24},{24,16},{32,40},{40,32},{48,56},{56,48},{64,72... | collective-permute-start | bytes 1720328 | tf_op jit(solution)/shard_map/ppermute | solution.py:236

commit v3 on v2

--- a/solution.py
+++ b/solution.py
@@ -143,6 +143,51 @@
     return lax.fori_loop(0, samples * per_sample, data_block_step, out_buffer)
 
 
+def parity_split(values, row_width):
+    c, n, z, plane = values.shape
+    rows = plane // row_width
+    grouped = values.reshape(c, n, z, rows // 2, 2, row_width // 2, 2)
+    grouped = grouped.transpose(0, 1, 2, 4, 6, 3, 5)
+    return grouped.reshape(c, n, z, 4, plane // 4)
+
+def parity_taps(split, coarse_width):
+    depth_len = split.shape[2] - 2
+    size = split.shape[4]
+    pad = coarse_width + 1
+    flattened = jnp.pad(split, ((0, 0), (0, 0), (0, 0), (0, 0), (pad, pad)))
+    column = lax.broadcasted_iota(jnp.int32, (1, 1, 1, size), 3) % coarse_width
+    left_mask = (column >= 1).astype(split.dtype)
+    right_mask = (column <= coarse_width - 2).astype(split.dtype)
+    blocks = []
+    for a in range(2):
+        for b in range(2):
+            pieces = []
+            for tap_index in range(27):
+                depth_start = tap_index // 9
+                row_sum = a + tap_index // 3 % 3 - 1
+                col_sum = b + tap_index % 3 - 1
+                source = (row_sum % 2) * 2 + col_sum % 2
+                row_step, col_step = row_sum // 2, col_sum // 2
+                offset = pad + row_step * coarse_width + col_step
+                shifted = flattened[:, :, depth_start : depth_start + depth_len, source, offset : offset + size]
+                if col_step < 0:
+                    shifted = shifted * left_mask
+                elif col_step > 0:
+                    shifted = shifted * right_mask
+                pieces.append(shifted)
+            blocks.append(jnp.concatenate(pieces, axis=0))
+    return jnp.stack(blocks, axis=3)
+
+def parity_pool(values):
+    c, n, z, parities, size = values.shape
+    return values.reshape(c, n, z // 2, 2 * parities, size).mean(axis=3)
+
+def parity_spread(values):
+    c, n, z, size = values.shape
+    grouped = jnp.broadcast_to(values[:, :, :, None, None, :], (c, n, z, 2, 4, size))
+    return grouped.reshape(c, n, 2 * z, 4, size) * 0.125
+
+
 def bias_sum(delta_values):
     return jnp.sum(delta_values, axis=(1, 2, 3), dtype=jnp.float32)
 
@@ -151,7 +196,17 @@
     flipped_second = jnp.flip(w_second, 0).transpose(0, 2, 1)
     flipped_third = jnp.flip(w_third, 0).transpose(0, 2, 1)
     volume_padded = with_halo(volume, (("slab", 2),), 1)
-    first_pre, first_pooled = forward_layer(volume_padded, w_first, b_first, SX, CZ, True)
+    first_patches = parity_taps(parity_split(volume_padded, SX), SX // 2)
+    first_pre = (
+        jnp.einsum(
+            "ko,kgzpq->ogzpq",
+            w_first.reshape(-1, w_first.shape[2]),
+            first_patches,
+            preferred_element_type=jnp.float32,
+        )
+        + b_first[:, None, None, None, None]
+    ).astype(jnp.bfloat16)
+    first_pooled = parity_pool(jax.nn.silu(first_pre.astype(jnp.float32))).astype(jnp.bfloat16)
     first_padded = with_halo(first_pooled, (("slab", 2),), 1)
     second_pre, second_pooled = forward_layer(
         first_padded, w_second, b_second, SX // 2, CZ // 2, True
@@ -177,11 +232,12 @@
     delta_padded = with_halo(second_delta, (("slab", 2),), 1)
     first_back = data_grads(delta_padded, flipped_second, SX // 2, CZ // 2)
     first_delta = (
-        spread_cells(first_back.astype(jnp.float32), SX // 2)
-        * silu_slope(first_pre.astype(jnp.float32))
+        parity_spread(first_back.astype(jnp.float32)) * silu_slope(first_pre.astype(jnp.float32))
     ).astype(jnp.bfloat16)
-    kernel_first = weight_grads(volume_padded, first_delta, SX, CZ, w_first)
-    bias_first = bias_sum(first_delta)
+    kernel_first = jnp.einsum(
+        "kgzpq,ogzpq->ko", first_patches, first_delta, preferred_element_type=jnp.float32
+    ).reshape(w_first.shape)
+    bias_first = jnp.sum(first_delta, axis=(1, 2, 3, 4), dtype=jnp.float32)
     weights = all_reduce_rows(
         (kernel_third, kernel_second, kernel_first, bias_third, bias_second, bias_first)
     )

time: 211 us -> 209 us (level)
  local copies, waits for them, and re-layouts: 52.4 us -> 63.7 us
  other arithmetic: 25.7 us -> 15.8 us
    concatenate x0 -> x5, local copies, waits for them, and re-layouts: none -> 31.6 us  [the longest x4 28.2 us: parity_taps(): blocks.append(jnp.concatenate(pieces, axis=0))]
    concatenate x2 -> x1, local copies, waits for them, and re-layouts: 19.9 us -> 3.42 us  [gather_taps(): return jnp.concatenate(pieces, axis=0)]
    reshape x0 -> x3, local copies, waits for them, and re-layouts: none -> 16.4 us  [the longest x2 15 us: parity_split(): return grouped.reshape(c, n, z, 4, plane // 4)]
    reduce_sum x2 -> x1, other arithmetic: 9.96 us -> 0.43 us  [pool_cells(): grouped.mean(axis=(3, 5, 7))]
    broadcast_in_dim x2 -> x1, local copies, waits for them, and re-layouts: 7.76 us -> 0.16 us  [spread_cells(): jnp.broadcast_to(grouped, (channels, samples, depth_len, 2, row_count, 2,...]
    mul x4 -> x2, local copies, waits for them, and re-layouts: 5.72 us -> 0.27 us  [spread_cells(): grouped.reshape(channels, samples, 2 * depth_len, 4 * plane_size) * 0.125]
    mul x1 -> x0, local copies, waits for them, and re-layouts: 4.71 us -> none  [forward_block_step(): activated = jax.nn.silu(pre_values.astype(jnp.float32))]
    dot_general x5 -> x4, matrix products: 8.8 us -> 4.17 us  [apply_weight(): jnp.einsum('ko,kgzp->ogzp', flat_weight, patches, preferred_element_type=...]
  transfers between devices with their start and end apart: 21 -> 21, of which waited for: 14 -> 13; matrix products, arithmetic and copies ran while one was open for 4% -> 4% of each run, Pallas kernels for 0% -> 0%
where the time goes in v3:
time: 209 us; the launch traced here: 206 us
  starting transfers between devices  75 us (36%)
  local copies, waits for them, and re-layouts  63.7 us (30%)
  waiting for transfers between devices  37.9 us (18%)
  other arithmetic  15.8 us (8%)
  matrix products  11.3 us (5%)
    concatenate x4, local copies, waits for them, and re-layouts, parity_taps(): blocks.append(jnp.concatenate(pieces, axis=0))  28.2 us
    ppermute x5, starting transfers between devices, with_halo(): before = lax.ppermute(last, axis, up)  24.1 us
    ppermute x5, starting transfers between devices, all_reduce_rows(): buffer = buffer + lax.ppermute(buffer, axis, xor_pairs(axis, mask))  19.8 us
    ppermute x3, starting transfers between devices, all_reduce_rows(): other = lax.ppermute(buffer, axis, xor_pairs(axis, mask))  16.4 us
    ppermute x5, waiting for transfers between devices, all_reduce_rows(): buffer = buffer + lax.ppermute(buffer, axis, xor_pairs(axis, mask))  16 us
    reshape x2, local copies, waits for them, and re-layouts, parity_split(): return grouped.reshape(c, n, z, 4, plane // 4)  15 us
    ppermute x3, waiting for transfers between devices, all_reduce_rows(): buffer = keep + lax.ppermute(send, axis, xor_pairs(axis, mask))  12.2 us
    ppermute x3, starting transfers between devices, all_reduce_rows(): buffer = keep + lax.ppermute(send, axis, xor_pairs(axis, mask))  8.19 us
  transfers between devices with their start and end apart: 21, of which 13 were waited for; matrix products, arithmetic and copies ran while one was open for 4% of the time, Pallas kernels for 0%

profile of v3, /device:TPU:1, one launch (start us, length us, event | category | flops | bytes accessed | tf_op | source)
XLA Modules:
  0.0 205.8 jit_solution(878328584335719881)
XLA Ops:
  0.6 1.1 fusion.143
  1.7 1.3 collective-permute-start.1
  3.0 5.0 %collective-permute-start = (bf16[4,1,1,4096]{3,2,1,0:T(2,128)(2,1)S(1)}, bf16[4,1,1,4096]{3,2,1,0:T(2,128)(2,1)S(1)}, u32[]{:S(2)}, u32[]{:S(2)}) collective-permute-start(bf16[4,1,1,4096]{3,2,1,0:T(2,128)(2,1)S(1)} %get-tuple-element.216), channel_id=1, source_target_pairs={{0,1},{1,2},{2,3},{3,4},{4,5},{5,6},{6,7},{8,9},{9,10},{10,11},{11... | collective-permute-start | bytes 98312 | tf_op jit(solution)/shard_map/ppermute | solution.py:17
  8.0 1.0 reverse_bitcast_fusion
  9.1 1.4 reshape.609
  10.5 1.1 pad_maximum_fusion.5
  11.6 3.4 %copy.57 = bf16[4,1,6,4096]{2,3,0,1:T(8,128)(2,1)} copy(bf16[4,1,6,4096]{3,2,1,0:T(8,128)(2,1)S(1)} %pad_maximum_fusion.5) | data formatting | bytes 393216 | tf_op jit(solution)/shard_map/concatenate | solution.py:19
  15.0 13.3 %copy.96 = bf16[4,1,6,2,2,64,16]{6,5,0,2,4,3,1:T(8,128)(2,1)S(1)} copy(bf16[4,1,6,2,2,64,16]{2,4,6,3,5,0,1:T(2,128)(2,1)} %bitcast.277) | data formatting | bytes 393216 | tf_op jit(solution)/shard_map/reshape | solution.py:151
  28.3 1.8 reshape.631
  34.5 9.0 %concatenate.73 = bf16[108,1,4,1024]{3,0,2,1:T(8,128)(2,1)S(1)} concatenate(bf16[4,1,4,1024]{3,0,2,1:T(4,128)(2,1)} %get-tuple-element.177, bf16[4,1,4,1024]{3,0,2,1:T(4,128)(2,1)} %get-tuple-element.176, bf16[4,1,4,1024]{3,0,2,1:T(4,128)(2,1)} %get-tuple-element.165, bf16[4,1,4,1024]{3,0,2,1:T(4,128)(2,1)} %copy-done.4, bf16[4,1,4,1024]{3,0,2,1:T(4,128)(2,1)} %copy-done.3, ...), dimensions={0} | concatenate | bytes 1769472 | tf_op jit(solution)/shard_map/concatenate | solution.py:178
  43.6 17.8 %concatenate.72 = bf16[108,1,4,1024]{3,0,2,1:T(8,128)(2,1)} concatenate(bf16[4,1,4,1024]{3,0,2,1:T(4,128)(2,1)} %get-tuple-element.153, bf16[4,1,4,1024]{3,0,2,1:T(4,128)(2,1)} %get-tuple-element.177, bf16[4,1,4,1024]{3,0,2,1:T(4,128)(2,1)} %get-tuple-element.176, bf16[4,1,4,1024]{3,0,2,1:T(4,128)(2,1)} %copy-done.11, bf16[4,1,4,1024]{3,0,2,1:T(4,128)(2,1)} %copy-done.4, ...), dimensions={0} | concatenate | bytes 1769472 | tf_op jit(solution)/shard_map/concatenate | solution.py:178
  61.4 1.5 maximum_bitcast_fusion
  63.0 2.5 %fusion.11 = (f32[32,4,1024]{2,0,1:T(8,128)S(1)}, bf16[4,4,1024,32]{2,3,1,0:T(8,128)(2,1)}) fusion(f32[32]{0:T(128)S(1)} %copy-done.22, bf16[108,4,4,1024]{3,0,2,1:T(8,128)(2,1)S(1)} %maximum_bitcast_fusion, bf16[108,32]{1,0:T(8,128)(2,1)S(1)} %copy-done.20), kind=kOutput, calls=%fused_computation.15 | convolution fusion | flops 117309440 | bytes 5118848 | tf_op jit(solution)/shard_map/ko,kgzpq->ogzpq/dot_general | solution.py:201
  65.6 1.3 collective-permute-start.3
  66.9 4.2 %collective-permute-start.2 = (bf16[32,1,1,1024]{3,0,2,1:T(8,128)(2,1)S(1)}, bf16[32,1,1,1024]{3,0,2,1:T(8,128)(2,1)S(1)}, u32[]{:S(2)}, u32[]{:S(2)}) collective-permute-start(bf16[32,1,1,1024]{3,0,2,1:T(8,128)(2,1)S(1)} %get-tuple-element.214), channel_id=1, source_target_pairs={{0,1},{1,2},{2,3},{3,4},{4,5},{5,6},{6,7},{8,9},{9,10},{10,11},{11... | collective-permute-start | bytes 196616 | tf_op jit(solution)/shard_map/ppermute | solution.py:17
  71.1 1.3 collective-permute-done.2
  77.5 1.3 collective-permute-start.5
  78.8 4.5 %collective-permute-start.4 = (bf16[64,1,1,256]{0,3,2,1:T(8,128)(2,1)S(1)}, bf16[64,1,1,256]{0,3,2,1:T(8,128)(2,1)S(1)}, u32[]{:S(2)}, u32[]{:S(2)}) collective-permute-start(bf16[64,1,1,256]{0,3,2,1:T(8,128)(2,1)S(1)} %fusion.126), channel_id=1, source_target_pairs={{0,1},{1,2},{2,3},{3,4},{4,5},{5,6},{6,7},{8,9},{9,10},{10,11},{11... | collective-permute-start | bytes 98312 | tf_op jit(solution)/shard_map/ppermute | solution.py:17
  85.6 3.4 %concatenate.81 = bf16[1728,1,1,256]{0,3,2,1:T(8,128)(2,1)S(1)} concatenate(bf16[64,1,1,256]{0,3,2,1:T(8,128)(2,1)S(1)} %get-tuple-element.195, bf16[64,1,1,256]{0,3,2,1:T(8,128)(2,1)} %get-tuple-element.201, bf16[64,1,1,256]{0,3,2,1:T(8,128)(2,1)} %get-tuple-element.186, bf16[64,1,1,256]{0,3,2,1:T(8,128)(2,1)S(1)} %get-tuple-element.194, ...), dimensions={0} | concatenate | bytes 1769472 | tf_op jit(solution)/shard_map/while/body/eval_jaxpr/concatenate | solution.py:53
  89.1 1.3 convert_reduce_fusion.2
  90.4 1.3 collective-permute-start.7
  91.7 5.2 %collective-permute-start.6 = (bf16[128,1,1,256]{0,3,2,1:T(8,128)(2,1)S(1)}, bf16[128,1,1,256]{0,3,2,1:T(8,128)(2,1)S(1)}, u32[]{:S(2)}, u32[]{:S(2)}) collective-permute-start(bf16[128,1,1,256]{0,3,2,1:T(8,128)(2,1)S(1)} %get-tuple-element.129), channel_id=1, source_target_pairs={{0,1},{1,2},{2,3},{3,4},{4,5},{5,6},{6,7},{8,9},{9,10},{10,11},{11... | collective-permute-start | bytes 196616 | tf_op jit(solution)/shard_map/ppermute | solution.py:17
  102.2 1.3 collective-permute-start.9
  103.5 5.2 %collective-permute-start.8 = (bf16[64,1,1,1024]{3,0,2,1:T(8,128)(2,1)S(1)}, bf16[64,1,1,1024]{3,0,2,1:T(8,128)(2,1)S(1)}, u32[]{:S(2)}, u32[]{:S(2)}) collective-permute-start(bf16[64,1,1,1024]{3,0,2,1:T(8,128)(2,1)S(1)} %get-tuple-element.140), channel_id=1, source_target_pairs={{0,1},{1,2},{2,3},{3,4},{4,5},{5,6},{6,7},{8,9},{9,10},{10,11},{11... | collective-permute-start | bytes 393224 | tf_op jit(solution)/shard_map/ppermute | solution.py:17
  108.7 3.1 %fusion.21 = f32[864,64]{1,0:T(8,128)S(1)} fusion(bf16[64,2,1024]{2,0,1:T(8,128)(2,1)S(1)} %get-tuple-element.122, bf16[864,1,2,1024]{3,0,2,1:T(8,128)(2,1)} %copy-done.21), kind=kOutput, calls=%fused_computation.31 | convolution fusion | flops 226492416 | bytes 4022272 | tf_op jit(solution)/shard_map/while/body/eval_jaxpr/kgzp,ogzp->ko/dot_general | solution.py:62
  115.7 1.3 fusion.43
  117.2 1.0 convert_reduce_fusion
  118.1 1.1 fusion.49
  119.8 5.1 %collective-permute-start.10 = (f32[1120,128]{1,0:T(8,128)S(1)}, f32[1120,128]{1,0:T(8,128)S(1)}, u32[]{:S(2)}, u32[]{:S(2)}) collective-permute-start(f32[1120,128]{1,0:T(8,128)S(1)} %constant_dynamic-slice_fusion.2), channel_id=1, source_target_pairs={{0,8},{8,0},{16,24},{24,16},{32,40},{40,32},{48,56},{56,48},{64,72... | collective-permute-start | bytes 1720328 | tf_op jit(solution)/shard_map/ppermute | solution.py:287
  124.9 1.6 collective-permute-done.10
  127.4 7.4 %collective-permute-done.11 = f32[560,128]{1,0:T(8,128)S(1)} collective-permute-done((f32[560,128]{1,0:T(8,128)S(1)}, f32[560,128]{1,0:T(8,128)S(1)}, u32[]{:S(2)}, u32[]{:S(2)}) %collective-permute-start.11) | collective-permute-done | bytes 286752 | tf_op jit(solution)/shard_map/ppermute | solution.py:287
  134.8 2.4 %collective-permute-start.12 = (f32[280,128]{1,0:T(8,128)S(1)}, f32[280,128]{1,0:T(8,128)S(1)}, u32[]{:S(2)}, u32[]{:S(2)}) collective-permute-start(f32[280,128]{1,0:T(8,128)S(1)} %constant_dynamic-slice_fusion), channel_id=1, source_target_pairs={{0,32},{8,40},{16,48},{24,56},{32,0},{40,8},{48,16},{56,24},{64,96... | collective-permute-start | bytes 430088 | tf_op jit(solution)/shard_map/ppermute | solution.py:287
  137.2 3.2 %collective-permute-done.12 = f32[280,128]{1,0:T(8,128)S(1)} collective-permute-done((f32[280,128]{1,0:T(8,128)S(1)}, f32[280,128]{1,0:T(8,128)S(1)}, u32[]{:S(2)}, u32[]{:S(2)}) %collective-permute-start.12) | collective-permute-done | bytes 143392 | tf_op jit(solution)/shard_map/ppermute | solution.py:287
  141.1 3.4 %collective-permute-done.13 = f32[280,128]{1,0:T(8,128)S(1)} collective-permute-done((f32[280,128]{1,0:T(8,128)S(1)}, f32[280,128]{1,0:T(8,128)S(1)}, u32[]{:S(2)}, u32[]{:S(2)}) %collective-permute-start.13) | collective-permute-done | bytes 143392 | tf_op jit(solution)/shard_map/ppermute | solution.py:290
  144.5 2.2 %collective-permute-start.14 = (f32[280,128]{1,0:T(8,128)S(1)}, f32[280,128]{1,0:T(8,128)S(1)}, u32[]{:S(2)}, u32[]{:S(2)}) collective-permute-start(f32[280,128]{1,0:T(8,128)S(1)} %add.478), channel_id=1, source_target_pairs={{0,128},{8,136},{16,144},{24,152},{32,160},{40,168},{48,176},{56,1... | collective-permute-start | bytes 430088 | tf_op jit(solution)/shard_map/ppermute | solution.py:290
  146.7 3.7 %collective-permute-done.14 = f32[280,128]{1,0:T(8,128)S(1)} collective-permute-done((f32[280,128]{1,0:T(8,128)S(1)}, f32[280,128]{1,0:T(8,128)S(1)}, u32[]{:S(2)}, u32[]{:S(2)}) %collective-permute-start.14) | collective-permute-done | bytes 143392 | tf_op jit(solution)/shard_map/ppermute | solution.py:290
  150.4 3.4 %collective-permute-start.15 = (f32[280,128]{1,0:T(8,128)S(1)}, f32[280,128]{1,0:T(8,128)S(1)}, u32[]{:S(2)}, u32[]{:S(2)}) collective-permute-start(f32[280,128]{1,0:T(8,128)S(1)} %add.479), channel_id=1, source_target_pairs={{0,1},{1,0},{2,3},{3,2},{4,5},{5,4},{6,7},{7,6},{8,9},{9,8},{10,11... | collective-permute-start | bytes 430088 | tf_op jit(solution)/shard_map/ppermute | solution.py:290
  153.7 2.5 %collective-permute-done.15 = f32[280,128]{1,0:T(8,128)S(1)} collective-permute-done((f32[280,128]{1,0:T(8,128)S(1)}, f32[280,128]{1,0:T(8,128)S(1)}, u32[]{:S(2)}, u32[]{:S(2)}) %collective-permute-start.15) | collective-permute-done | bytes 143392 | tf_op jit(solution)/shard_map/ppermute | solution.py:290
  156.2 6.4 %collective-permute-start.16 = (f32[280,128]{1,0:T(8,128)S(1)}, f32[280,128]{1,0:T(8,128)S(1)}, u32[]{:S(2)}, u32[]{:S(2)}) collective-permute-start(f32[280,128]{1,0:T(8,128)S(1)} %add.480), channel_id=1, source_target_pairs={{0,2},{1,3},{2,0},{3,1},{4,6},{5,7},{6,4},{7,5},{8,10},{9,11},{10,... | collective-permute-start | bytes 430088 | tf_op jit(solution)/shard_map/ppermute | solution.py:290
  162.6 2.8 %collective-permute-done.16 = f32[280,128]{1,0:T(8,128)S(1)} collective-permute-done((f32[280,128]{1,0:T(8,128)S(1)}, f32[280,128]{1,0:T(8,128)S(1)}, u32[]{:S(2)}, u32[]{:S(2)}) %collective-permute-start.16) | collective-permute-done | bytes 143392 | tf_op jit(solution)/shard_map/ppermute | solution.py:290
  165.5 7.2 %collective-permute-start.17 = (f32[280,128]{1,0:T(8,128)S(1)}, f32[280,128]{1,0:T(8,128)S(1)}, u32[]{:S(2)}, u32[]{:S(2)}) collective-permute-start(f32[280,128]{1,0:T(8,128)S(1)} %add.481), channel_id=1, source_target_pairs={{0,4},{1,5},{2,6},{3,7},{4,0},{5,1},{6,2},{7,3},{8,12},{9,13},{10,... | collective-permute-start | bytes 430088 | tf_op jit(solution)/shard_map/ppermute | solution.py:290
  172.7 3.6 %collective-permute-done.17 = f32[280,128]{1,0:T(8,128)S(1)} collective-permute-done((f32[280,128]{1,0:T(8,128)S(1)}, f32[280,128]{1,0:T(8,128)S(1)}, u32[]{:S(2)}, u32[]{:S(2)}) %collective-permute-start.17) | collective-permute-done | bytes 143392 | tf_op jit(solution)/shard_map/ppermute | solution.py:290
  176.3 3.0 %collective-permute-start.18 = (f32[280,128]{1,0:T(8,128)S(1)}, f32[280,128]{1,0:T(8,128)S(1)}, u32[]{:S(2)}, u32[]{:S(2)}) collective-permute-start(f32[280,128]{1,0:T(8,128)S(1)} %add.482), channel_id=1, source_target_pairs={{0,32},{8,40},{16,48},{24,56},{32,0},{40,8},{48,16},{56,24},{64,96... | collective-permute-start | bytes 430088 | tf_op jit(solution)/shard_map/ppermute | solution.py:292
  179.3 2.5 %collective-permute-done.18 = f32[280,128]{1,0:T(8,128)S(1)} collective-permute-done((f32[280,128]{1,0:T(8,128)S(1)}, f32[280,128]{1,0:T(8,128)S(1)}, u32[]{:S(2)}, u32[]{:S(2)}) %collective-permute-start.18) | collective-permute-done | bytes 143392 | tf_op jit(solution)/shard_map/ppermute | solution.py:292
  182.0 1.4 collective-permute-start.19
  183.4 4.2 %collective-permute-done.19 = f32[560,128]{1,0:T(8,128)S(1)} collective-permute-done((f32[560,128]{1,0:T(8,128)S(1)}, f32[560,128]{1,0:T(8,128)S(1)}, u32[]{:S(2)}, u32[]{:S(2)}) %collective-permute-start.19) | collective-permute-done | bytes 286752 | tf_op jit(solution)/shard_map/ppermute | solution.py:292
  187.7 12.0 %collective-permute-start.20 = (f32[1120,128]{1,0:T(8,128)S(1)}, f32[1120,128]{1,0:T(8,128)S(1)}, u32[]{:S(2)}, u32[]{:S(2)}) collective-permute-start(f32[1120,128]{1,0:T(8,128)S(1)} %get-tuple-element.132), channel_id=1, source_target_pairs={{0,8},{8,0},{16,24},{24,16},{32,40},{40,32},{48,56},{56,48},{64,72... | collective-permute-start | bytes 1720328 | tf_op jit(solution)/shard_map/ppermute | solution.py:292
  204.8 1.0 pad_maximum_fusion
  (207 shorter events, 27.8 us)
Async XLA Ops:
  1.7 8.8 %collective-permute-start.1 = (bf16[4,1,1,4096]{3,2,1,0:T(2,128)(2,1)S(1)}, bf16[4,1,1,4096]{3,2,1,0:T(2,128)(2,1)S(1)}, u32[]{:S(2)}, u32[]{:S(2)}) collective-permute-start(bf16[4,1,1,4096]{3,2,1,0:T(2,128)(2,1)S(1)} %get-tuple-element.217), channel_id=1, source_target_pairs={{1,0},{2,1},{3,2},{4,3},{5,4},{6,5},{7,6},{9,8},{10,9},{11,10},{12... | collective-permute-start | bytes 98312 | tf_op jit(solution)/shard_map/ppermute | solution.py:18
  3.0 7.5 %collective-permute-start = (bf16[4,1,1,4096]{3,2,1,0:T(2,128)(2,1)S(1)}, bf16[4,1,1,4096]{3,2,1,0:T(2,128)(2,1)S(1)}, u32[]{:S(2)}, u32[]{:S(2)}) collective-permute-start(bf16[4,1,1,4096]{3,2,1,0:T(2,128)(2,1)S(1)} %get-tuple-element.216), channel_id=1, source_target_pairs={{0,1},{1,2},{2,3},{3,4},{4,5},{5,6},{6,7},{8,9},{9,10},{10,11},{11... | collective-permute-start | bytes 98312 | tf_op jit(solution)/shard_map/ppermute | solution.py:17
  30.2 4.3 %copy-start.3 = (bf16[4,1,4,1024]{3,0,2,1:T(4,128)(2,1)}, bf16[4,1,4,1024]{3,0,2,1:T(4,128)(2,1)S(1)}, u32[]{:S(2)}) copy-start(bf16[4,1,4,1024]{3,0,2,1:T(4,128)(2,1)S(1)} %get-tuple-element.212) | copy-start | bytes 98308
  30.2 4.3 %copy-start.4 = (bf16[4,1,4,1024]{3,0,2,1:T(4,128)(2,1)}, bf16[4,1,4,1024]{3,0,2,1:T(4,128)(2,1)S(1)}, u32[]{:S(2)}) copy-start(bf16[4,1,4,1024]{3,0,2,1:T(4,128)(2,1)S(1)} %get-tuple-element.213) | copy-start | bytes 98308
  32.1 1.7 copy-start.12
  32.1 1.7 copy-start.13
  32.1 1.7 copy-start.14
  32.1 1.7 copy-start.15
  32.1 1.7 copy-start.16
  32.1 1.7 copy-start.17
  33.0 1.5 copy-start.6
  33.0 1.5 copy-start.7
  33.0 1.5 copy-start.8
  33.0 1.5 copy-start.9
  33.0 1.5 copy-start.10
  33.0 1.5 copy-start.11
  61.4 1.5 copy-start.20
  61.4 1.6 copy-start.22
  63.0 2.5 %copy-start = (bf16[108,4,4,1024]{3,0,2,1:T(8,128)(2,1)}, bf16[108,4,4,1024]{3,0,2,1:T(8,128)(2,1)S(1)}, u32[]{:S(2)}) copy-start(bf16[108,4,4,1024]{3,0,2,1:T(8,128)(2,1)S(1)} %maximum_bitcast_fusion) | copy-start | bytes 10616836
  63.0 8.1 %copy-start.18 = (bf16[27,32,64]{2,1,0:T(8,128)(2,1)S(1)}, bf16[27,32,64]{2,1,0:T(8,128)(2,1)}, u32[]{:S(2)}) copy-start(bf16[27,32,64]{2,1,0:T(8,128)(2,1)} %param.12) | copy-start | bytes 331780
  65.6 5.5 %collective-permute-start.3 = (bf16[32,1,1,1024]{3,0,2,1:T(8,128)(2,1)S(1)}, bf16[32,1,1,1024]{3,0,2,1:T(8,128)(2,1)S(1)}, u32[]{:S(2)}, u32[]{:S(2)}) collective-permute-start(bf16[32,1,1,1024]{3,0,2,1:T(8,128)(2,1)S(1)} %get-tuple-element.215), channel_id=1, source_target_pairs={{1,0},{2,1},{3,2},{4,3},{5,4},{6,5},{7,6},{9,8},{10,9},{11,10},{12... | collective-permute-start | bytes 196616 | tf_op jit(solution)/shard_map/ppermute | solution.py:18
  66.9 5.5 %collective-permute-start.2 = (bf16[32,1,1,1024]{3,0,2,1:T(8,128)(2,1)S(1)}, bf16[32,1,1,1024]{3,0,2,1:T(8,128)(2,1)S(1)}, u32[]{:S(2)}, u32[]{:S(2)}) collective-permute-start(bf16[32,1,1,1024]{3,0,2,1:T(8,128)(2,1)S(1)} %get-tuple-element.214), channel_id=1, source_target_pairs={{0,1},{1,2},{2,3},{3,4},{4,5},{5,6},{6,7},{8,9},{9,10},{10,11},{11... | collective-permute-start | bytes 196616 | tf_op jit(solution)/shard_map/ppermute | solution.py:17
  72.6 2.5 %copy-start.23 = (f32[64]{0:T(128)S(1)}, f32[64]{0:T(128)}, u32[]{:S(2)}) copy-start(f32[64]{0:T(128)} %param.13) | copy-start | bytes 772
  75.1 1.8 copy-start.21
  75.1 8.2 %copy-start.19 = (bf16[128,1,1,256]{3,0,2,1:T(8,128)(2,1)S(1)}, bf16[128,1,1,256]{3,0,2,1:T(8,128)(2,1)}, u32[]{:S(2)}) copy-start(bf16[128,1,1,256]{3,0,2,1:T(8,128)(2,1)} %param.9) | copy-start | bytes 196612
  77.5 6.9 %collective-permute-start.5 = (bf16[64,1,1,256]{0,3,2,1:T(8,128)(2,1)S(1)}, bf16[64,1,1,256]{0,3,2,1:T(8,128)(2,1)S(1)}, u32[]{:S(2)}, u32[]{:S(2)}) collective-permute-start(bf16[64,1,1,256]{0,3,2,1:T(8,128)(2,1)S(1)} %fusion.126), channel_id=1, source_target_pairs={{1,0},{2,1},{3,2},{4,3},{5,4},{6,5},{7,6},{9,8},{10,9},{11,10},{12... | collective-permute-start | bytes 98312 | tf_op jit(solution)/shard_map/ppermute | solution.py:18
  78.8 5.7 %collective-permute-start.4 = (bf16[64,1,1,256]{0,3,2,1:T(8,128)(2,1)S(1)}, bf16[64,1,1,256]{0,3,2,1:T(8,128)(2,1)S(1)}, u32[]{:S(2)}, u32[]{:S(2)}) collective-permute-start(bf16[64,1,1,256]{0,3,2,1:T(8,128)(2,1)S(1)} %fusion.126), channel_id=1, source_target_pairs={{0,1},{1,2},{2,3},{3,4},{4,5},{5,6},{6,7},{8,9},{9,10},{10,11},{11... | collective-permute-start | bytes 98312 | tf_op jit(solution)/shard_map/ppermute | solution.py:17
  84.1 5.0 %copy-start.5 = (bf16[27,64,128]{2,1,0:T(8,128)(2,1)S(1)}, bf16[27,64,128]{2,1,0:T(8,128)(2,1)}, u32[]{:S(2)}) copy-start(bf16[27,64,128]{2,1,0:T(8,128)(2,1)} %param.14) | copy-start | bytes 1327108
  84.1 5.0 %copy-start.24 = (f32[128]{0:T(128)S(1)}, f32[128]{0:T(128)}, u32[]{:S(2)}) copy-start(f32[128]{0:T(128)} %param.15) | copy-start | bytes 1540
  90.4 7.0 %collective-permute-start.7 = (bf16[128,1,1,256]{0,3,2,1:T(8,128)(2,1)S(1)}, bf16[128,1,1,256]{0,3,2,1:T(8,128)(2,1)S(1)}, u32[]{:S(2)}, u32[]{:S(2)}) collective-permute-start(bf16[128,1,1,256]{0,3,2,1:T(8,128)(2,1)S(1)} %get-tuple-element.129), channel_id=1, source_target_pairs={{1,0},{2,1},{3,2},{4,3},{5,4},{6,5},{7,6},{9,8},{10,9},{11,10},{12... | collective-permute-start | bytes 196616 | tf_op jit(solution)/shard_map/ppermute | solution.py:18
  91.7 6.6 %collective-permute-start.6 = (bf16[128,1,1,256]{0,3,2,1:T(8,128)(2,1)S(1)}, bf16[128,1,1,256]{0,3,2,1:T(8,128)(2,1)S(1)}, u32[]{:S(2)}, u32[]{:S(2)}) collective-permute-start(bf16[128,1,1,256]{0,3,2,1:T(8,128)(2,1)S(1)} %get-tuple-element.129), channel_id=1, source_target_pairs={{0,1},{1,2},{2,3},{3,4},{4,5},{5,6},{6,7},{8,9},{9,10},{10,11},{11... | collective-permute-start | bytes 196616 | tf_op jit(solution)/shard_map/ppermute | solution.py:17
  102.2 9.7 %collective-permute-start.9 = (bf16[64,1,1,1024]{3,0,2,1:T(8,128)(2,1)S(1)}, bf16[64,1,1,1024]{3,0,2,1:T(8,128)(2,1)S(1)}, u32[]{:S(2)}, u32[]{:S(2)}) collective-permute-start(bf16[64,1,1,1024]{3,0,2,1:T(8,128)(2,1)S(1)} %get-tuple-element.141), channel_id=1, source_target_pairs={{1,0},{2,1},{3,2},{4,3},{5,4},{6,5},{7,6},{9,8},{10,9},{11,10},{12... | collective-permute-start | bytes 393224 | tf_op jit(solution)/shard_map/ppermute | solution.py:18
  103.5 8.4 %collective-permute-start.8 = (bf16[64,1,1,1024]{3,0,2,1:T(8,128)(2,1)S(1)}, bf16[64,1,1,1024]{3,0,2,1:T(8,128)(2,1)S(1)}, u32[]{:S(2)}, u32[]{:S(2)}) collective-permute-start(bf16[64,1,1,1024]{3,0,2,1:T(8,128)(2,1)S(1)} %get-tuple-element.140), channel_id=1, source_target_pairs={{0,1},{1,2},{2,3},{3,4},{4,5},{5,6},{6,7},{8,9},{9,10},{10,11},{11... | collective-permute-start | bytes 393224 | tf_op jit(solution)/shard_map/ppermute | solution.py:17
  115.7 1.4 copy-start.2
  115.7 2.4 %copy-start.1 = (bf16[108,4,4,1024]{3,0,2,1:T(8,128)(2,1)S(1)}, bf16[108,4,4,1024]{3,0,2,1:T(8,128)(2,1)}, u32[]{:S(2)}) copy-start(bf16[108,4,4,1024]{3,0,2,1:T(8,128)(2,1)} %copy-done) | copy-start | bytes 10616836
  119.8 6.7 %collective-permute-start.10 = (f32[1120,128]{1,0:T(8,128)S(1)}, f32[1120,128]{1,0:T(8,128)S(1)}, u32[]{:S(2)}, u32[]{:S(2)}) collective-permute-start(f32[1120,128]{1,0:T(8,128)S(1)} %constant_dynamic-slice_fusion.2), channel_id=1, source_target_pairs={{0,8},{8,0},{16,24},{24,16},{32,40},{40,32},{48,56},{56,48},{64,72... | collective-permute-start | bytes 1720328 | tf_op jit(solution)/shard_map/ppermute | solution.py:287
  126.6 8.1 %collective-permute-start.11 = (f32[560,128]{1,0:T(8,128)S(1)}, f32[560,128]{1,0:T(8,128)S(1)}, u32[]{:S(2)}, u32[]{:S(2)}) collective-permute-start(f32[560,128]{1,0:T(8,128)S(1)} %constant_dynamic-slice_fusion.1), channel_id=1, source_target_pairs={{0,16},{8,24},{16,0},{24,8},{32,48},{40,56},{48,32},{56,40},{64,80... | collective-permute-start | bytes 860168 | tf_op jit(solution)/shard_map/ppermute | solution.py:287
  134.8 5.5 %collective-permute-start.12 = (f32[280,128]{1,0:T(8,128)S(1)}, f32[280,128]{1,0:T(8,128)S(1)}, u32[]{:S(2)}, u32[]{:S(2)}) collective-permute-start(f32[280,128]{1,0:T(8,128)S(1)} %constant_dynamic-slice_fusion), channel_id=1, source_target_pairs={{0,32},{8,40},{16,48},{24,56},{32,0},{40,8},{48,16},{56,24},{64,96... | collective-permute-start | bytes 430088 | tf_op jit(solution)/shard_map/ppermute | solution.py:287
  140.4 4.0 %collective-permute-start.13 = (f32[280,128]{1,0:T(8,128)S(1)}, f32[280,128]{1,0:T(8,128)S(1)}, u32[]{:S(2)}, u32[]{:S(2)}) collective-permute-start(f32[280,128]{1,0:T(8,128)S(1)} %dynamic-slice_add_fusion.2), channel_id=1, source_target_pairs={{0,64},{8,72},{16,80},{24,88},{32,96},{40,104},{48,112},{56,120},{... | collective-permute-start | bytes 430088 | tf_op jit(solution)/shard_map/ppermute | solution.py:290
  144.5 5.9 %collective-permute-start.14 = (f32[280,128]{1,0:T(8,128)S(1)}, f32[280,128]{1,0:T(8,128)S(1)}, u32[]{:S(2)}, u32[]{:S(2)}) collective-permute-start(f32[280,128]{1,0:T(8,128)S(1)} %add.478), channel_id=1, source_target_pairs={{0,128},{8,136},{16,144},{24,152},{32,160},{40,168},{48,176},{56,1... | collective-permute-start | bytes 430088 | tf_op jit(solution)/shard_map/ppermute | solution.py:290
  150.4 5.9 %collective-permute-start.15 = (f32[280,128]{1,0:T(8,128)S(1)}, f32[280,128]{1,0:T(8,128)S(1)}, u32[]{:S(2)}, u32[]{:S(2)}) collective-permute-start(f32[280,128]{1,0:T(8,128)S(1)} %add.479), channel_id=1, source_target_pairs={{0,1},{1,0},{2,3},{3,2},{4,5},{5,4},{6,7},{7,6},{8,9},{9,8},{10,11... | collective-permute-start | bytes 430088 | tf_op jit(solution)/shard_map/ppermute | solution.py:290
  156.2 9.2 %collective-permute-start.16 = (f32[280,128]{1,0:T(8,128)S(1)}, f32[280,128]{1,0:T(8,128)S(1)}, u32[]{:S(2)}, u32[]{:S(2)}) collective-permute-start(f32[280,128]{1,0:T(8,128)S(1)} %add.480), channel_id=1, source_target_pairs={{0,2},{1,3},{2,0},{3,1},{4,6},{5,7},{6,4},{7,5},{8,10},{9,11},{10,... | collective-permute-start | bytes 430088 | tf_op jit(solution)/shard_map/ppermute | solution.py:290
  165.5 10.8 %collective-permute-start.17 = (f32[280,128]{1,0:T(8,128)S(1)}, f32[280,128]{1,0:T(8,128)S(1)}, u32[]{:S(2)}, u32[]{:S(2)}) collective-permute-start(f32[280,128]{1,0:T(8,128)S(1)} %add.481), channel_id=1, source_target_pairs={{0,4},{1,5},{2,6},{3,7},{4,0},{5,1},{6,2},{7,3},{8,12},{9,13},{10,... | collective-permute-start | bytes 430088 | tf_op jit(solution)/shard_map/ppermute | solution.py:290
  176.3 5.5 %collective-permute-start.18 = (f32[280,128]{1,0:T(8,128)S(1)}, f32[280,128]{1,0:T(8,128)S(1)}, u32[]{:S(2)}, u32[]{:S(2)}) collective-permute-start(f32[280,128]{1,0:T(8,128)S(1)} %add.482), channel_id=1, source_target_pairs={{0,32},{8,40},{16,48},{24,56},{32,0},{40,8},{48,16},{56,24},{64,96... | collective-permute-start | bytes 430088 | tf_op jit(solution)/shard_map/ppermute | solution.py:292
  182.0 5.6 %collective-permute-start.19 = (f32[560,128]{1,0:T(8,128)S(1)}, f32[560,128]{1,0:T(8,128)S(1)}, u32[]{:S(2)}, u32[]{:S(2)}) collective-permute-start(f32[560,128]{1,0:T(8,128)S(1)} %get-tuple-element.136), channel_id=1, source_target_pairs={{0,16},{8,24},{16,0},{24,8},{32,48},{40,56},{48,32},{56,40},{64,80... | collective-permute-start | bytes 860168 | tf_op jit(solution)/shard_map/ppermute | solution.py:292
  187.7 13.6 %collective-permute-start.20 = (f32[1120,128]{1,0:T(8,128)S(1)}, f32[1120,128]{1,0:T(8,128)S(1)}, u32[]{:S(2)}, u32[]{:S(2)}) collective-permute-start(f32[1120,128]{1,0:T(8,128)S(1)} %get-tuple-element.132), channel_id=1, source_target_pairs={{0,8},{8,0},{16,24},{24,16},{32,40},{40,32},{48,56},{56,48},{64,72... | collective-permute-start | bytes 1720328 | tf_op jit(solution)/shard_map/ppermute | solution.py:292

commit v4 on v3

--- a/solution.py
+++ b/solution.py
@@ -1,6 +1,10 @@
+import functools
+
 import jax
 import jax.numpy as jnp
 from jax import lax
+from jax.experimental import pallas as pl
+from jax.experimental.pallas import tpu as pltpu
 from jax.sharding import PartitionSpec as P
 
 SX = 32
@@ -188,6 +192,64 @@
     return grouped.reshape(c, n, 2 * z, 4, size) * 0.125
 
 
+def _parity_kernel(coarse_width, src_ref, w_ref, b_ref, out_ref, shifted_ref):
+    channels, depth, _, size = src_ref.shape
+    lane = lax.broadcasted_iota(jnp.int32, (channels, size), 1)
+    row = lane // coarse_width
+    col = lane % coarse_width
+    rows = size // coarse_width
+    for source_plane in range(depth):
+        cache = {}
+        for a in range(2):
+            for b in range(2):
+                for shift_index in range(9):
+                    row_sum = a + shift_index // 3 - 1
+                    col_sum = b + shift_index % 3 - 1
+                    key = (row_sum % 2, col_sum % 2, row_sum // 2, col_sum // 2)
+                    if key not in cache:
+                        source, row_step, col_step = key[0] * 2 + key[1], key[2], key[3]
+                        values = src_ref[:, source_plane, source, :].astype(jnp.float32)
+                        step = row_step * coarse_width + col_step
+                        if step != 0:
+                            values = pltpu.roll(values, (-step) % size, 1)
+                        valid = (
+                            (row + row_step >= 0) & (row + row_step < rows)
+                            & (col + col_step >= 0) & (col + col_step < coarse_width)
+                        )
+                        cache[key] = jnp.where(valid, values, 0.0).astype(shifted_ref.dtype)
+                    shifted_ref[source_plane, a * 2 + b, shift_index * channels : (shift_index + 1) * channels, :] = cache[key]
+    for z in range(out_ref.shape[1]):
+        for parity in range(4):
+            summed = b_ref[...] + jnp.zeros((out_ref.shape[0], size), jnp.float32)
+            for dz in range(3):
+                summed = summed + jnp.dot(
+                    w_ref[dz], shifted_ref[z + dz, parity], preferred_element_type=jnp.float32
+                )
+            out_ref[:, z, parity, :] = summed.astype(out_ref.dtype)
+
+def parity_conv_forward(split, weight, bias_values, coarse_width):
+    channels, depth, parities, size = split.shape
+    out_channels = weight.shape[2]
+    per_depth = weight.reshape(3, 9 * channels, out_channels).transpose(0, 2, 1)
+    return pl.pallas_call(
+        functools.partial(_parity_kernel, coarse_width),
+        out_shape=(
+            jax.ShapeDtypeStruct((out_channels, depth - 2, parities, size), jnp.bfloat16),
+            jax.ShapeDtypeStruct((depth, parities, 9 * channels, size), jnp.bfloat16),
+        ),
+    )(split, per_depth, bias_values.reshape(out_channels, 1))
+
+def parity_weight_grad(shifted, delta):
+    depth_len = delta.shape[1]
+    per_depth = [
+        jnp.einsum(
+            "zpkq,ozpq->ko", shifted[dz : dz + depth_len], delta, preferred_element_type=jnp.float32
+        )
+        for dz in range(3)
+    ]
+    return jnp.stack(per_depth).reshape(27, shifted.shape[2] // 9, delta.shape[0])
+
+
 def bias_sum(delta_values):
     return jnp.sum(delta_values, axis=(1, 2, 3), dtype=jnp.float32)
 
@@ -196,16 +258,12 @@
     flipped_second = jnp.flip(w_second, 0).transpose(0, 2, 1)
     flipped_third = jnp.flip(w_third, 0).transpose(0, 2, 1)
     volume_padded = with_halo(volume, (("slab", 2),), 1)
-    first_patches = parity_taps(parity_split(volume_padded, SX), SX // 2)
-    first_pre = (
-        jnp.einsum(
-            "ko,kgzpq->ogzpq",
-            w_first.reshape(-1, w_first.shape[2]),
-            first_patches,
-            preferred_element_type=jnp.float32,
-        )
-        + b_first[:, None, None, None, None]
-    ).astype(jnp.bfloat16)
+    first_split = parity_split(volume_padded, SX)
+    first_layer = [
+        parity_conv_forward(first_split[:, s], w_first, b_first, SX // 2)
+        for s in range(first_split.shape[1])
+    ]
+    first_pre = jnp.stack([pre for pre, _ in first_layer], axis=1)
     first_pooled = parity_pool(jax.nn.silu(first_pre.astype(jnp.float32))).astype(jnp.bfloat16)
     first_padded = with_halo(first_pooled, (("slab", 2),), 1)
     second_pre, second_pooled = forward_layer(
@@ -234,9 +292,10 @@
     first_delta = (
         parity_spread(first_back.astype(jnp.float32)) * silu_slope(first_pre.astype(jnp.float32))
     ).astype(jnp.bfloat16)
-    kernel_first = jnp.einsum(
-        "kgzpq,ogzpq->ko", first_patches, first_delta, preferred_element_type=jnp.float32
-    ).reshape(w_first.shape)
+    kernel_first = sum(
+        parity_weight_grad(shifted, first_delta[:, s])
+        for s, (_, shifted) in enumerate(first_layer)
+    )
     bias_first = jnp.sum(first_delta, axis=(1, 2, 3, 4), dtype=jnp.float32)
     weights = all_reduce_rows(
         (kernel_third, kernel_second, kernel_first, bias_third, bias_second, bias_first)

time: 209 us -> 194 us (0.928)
  local copies, waits for them, and re-layouts: 63.7 us -> 41.9 us
  Pallas kernels: 0 us -> 4.56 us
  matrix products: 11.3 us -> 15 us
  other arithmetic: 15.8 us -> 17.9 us
    concatenate x4 -> x0, local copies, waits for them, and re-layouts: 28.2 us -> none  [parity_taps(): blocks.append(jnp.concatenate(pieces, axis=0))]
    reshape x3, local copies, waits for them, and re-layouts: 16.4 us -> 2.82 us  [the longest x2 1.48 us: parity_conv_forward(): per_depth = weight.reshape(3, 9 * channels, out_channels).transpose(0, 2, 1)]
    transpose x0 -> x1, local copies, waits for them, and re-layouts: none -> 13.3 us  [parity_split(): grouped = grouped.transpose(0, 1, 2, 4, 6, 3, 5)]
    pallas_call x0 -> x1, Pallas kernels: none -> 4.56 us  [parity_conv_forward(): pl.pallas_call(functools.partial(_parity_kernel, coarse_width), out_shape...]
    reduce_sum x1 -> x2, other arithmetic: 0.03 us -> 4.25 us  [parity_pool(): return values.reshape(c, n, z // 2, 2 * parities, size).mean(axis=3)]
    another operation x0 -> x2, local copies, waits for them, and re-layouts: none -> 2.57 us  [the longest x1 2.47 us: per_device(): first_split[:, s]]
    dot_general x2 -> x3, matrix products: 3.62 us -> 5.94 us  [parity_weight_grad(): jnp.einsum('zpkq,ozpq->ko', shifted[dz:dz + depth_len], delta, preferred_...]
    unnamed x75 -> x49, local copies, waits for them, and re-layouts: 5.19 us -> 5.53 us
  transfers between devices with their start and end apart: 21 -> 21, of which waited for: 13 -> 13; matrix products, arithmetic and copies ran while one was open for 4% -> 7% of each run, Pallas kernels for 0% -> 0%
where the time goes in v4:
time: 194 us; the launch traced here: 193 us
  starting transfers between devices  74.1 us (38%)
  local copies, waits for them, and re-layouts  41.9 us (22%)
  waiting for transfers between devices  37.3 us (19%)
  other arithmetic  17.9 us (9%)
  matrix products  15 us (8%)
  Pallas kernels  4.56 us (2%)
    ppermute x5, starting transfers between devices, with_halo(): before = lax.ppermute(last, axis, up)  24.3 us
    ppermute x5, starting transfers between devices, all_reduce_rows(): buffer = buffer + lax.ppermute(buffer, axis, xor_pairs(axis, mask))  19 us
    ppermute x3, starting transfers between devices, all_reduce_rows(): other = lax.ppermute(buffer, axis, xor_pairs(axis, mask))  16.5 us
    ppermute x5, waiting for transfers between devices, all_reduce_rows(): buffer = buffer + lax.ppermute(buffer, axis, xor_pairs(axis, mask))  15.9 us
    transpose x1, local copies, waits for them, and re-layouts, parity_split(): grouped = grouped.transpose(0, 1, 2, 4, 6, 3, 5)  13.3 us
    ppermute x3, waiting for transfers between devices, all_reduce_rows(): buffer = keep + lax.ppermute(send, axis, xor_pairs(axis, mask))  11.9 us
    ppermute x3, starting transfers between devices, all_reduce_rows(): buffer = keep + lax.ppermute(send, axis, xor_pairs(axis, mask))  7.83 us
    ppermute x3, waiting for transfers between devices, all_reduce_rows(): other = lax.ppermute(buffer, axis, xor_pairs(axis, mask))  7.51 us
  transfers between devices with their start and end apart: 21, of which 13 were waited for; matrix products, arithmetic and copies ran while one was open for 7% of the time, Pallas kernels for 0%

profile of v4, /device:TPU:1, one launch (start us, length us, event | category | flops | bytes accessed | tf_op | source)
XLA Modules:
  0.0 192.6 jit_solution(14574894933909445496)
XLA Ops:
  1.7 1.3 collective-permute-start.1
  3.0 5.0 %collective-permute-start = (bf16[4,1,1,4096]{3,2,1,0:T(2,128)(2,1)S(1)}, bf16[4,1,1,4096]{3,2,1,0:T(2,128)(2,1)S(1)}, u32[]{:S(2)}, u32[]{:S(2)}) collective-permute-start(bf16[4,1,1,4096]{3,2,1,0:T(2,128)(2,1)S(1)} %get-tuple-element.189), channel_id=1, source_target_pairs={{0,1},{1,2},{2,3},{3,4},{4,5},{5,6},{6,7},{8,9},{9,10},{10,11},{11... | collective-permute-start | bytes 98312 | tf_op jit(solution)/shard_map/ppermute | solution.py:21
  10.1 1.6 copy.98
  13.1 1.3 copy.94.b_ref
  14.8 1.1 pad_maximum_fusion.5
  16.0 3.4 %copy.91 = bf16[4,1,6,4096]{2,3,0,1:T(8,128)(2,1)} copy(bf16[4,1,6,4096]{3,2,1,0:T(8,128)(2,1)S(1)} %pad_maximum_fusion.5) | data formatting | bytes 393216 | tf_op jit(solution)/shard_map/concatenate | solution.py:23
  19.4 13.3 %copy.92 = bf16[4,1,6,2,2,64,16]{6,5,4,3,2,0,1:T(8,128)(2,1)S(1)} copy(bf16[4,1,6,2,2,64,16]{2,4,6,3,5,0,1:T(2,128)(2,1)} %bitcast.155) | data formatting | bytes 393216 | tf_op jit(solution)/shard_map/transpose | solution.py:154
  32.7 2.5 %squeeze_reshape.3.src_ref = bf16[4,6,4,1024]{3,2,1,0:T(4,128)(2,1)} reshape(bf16[4,1,6,2,2,64,16]{6,5,4,3,2,0,1:T(8,128)(2,1)S(1)} %copy.92) | data formatting | bytes 393216 | tf_op jit(solution)/shard_map/squeeze;reshape | solution.py:263
  35.2 4.6 %shard_map.135 = (bf16[32,4,4,1024]{3,2,1,0:T(4,128)(2,1)}, bf16[6,4,36,1024]{3,2,1,0:T(8,128)(2,1)}) custom-call(bf16[4,6,4,1024]{3,2,1,0:T(4,128)(2,1)} %squeeze_reshape.3.src_ref, bf16[3,32,36]{2,1,0:T(8,128)(2,1)} %bitcast.171, f32[32,1]{1,0:T(8,128)} %copy.94.b_ref), custom_call_target="tpu_custom_call" | custom-call | tf_op jit(solution)/shard_map/pallas_call | solution.py:234
  39.8 4.0 %fusion.9 = f32[32,4,1024]{2,1,0:T(4,128)S(1)} fusion(bf16[32,4,4,1024]{3,2,1,0:T(4,128)(2,1)} %get-tuple-element.82), kind=kLoop, calls=%fused_computation.12 | loop fusion | flops 3014656 | bytes 1572864 | tf_op jit(solution)/shard_map/reduce_sum | solution.py:187
  44.1 1.3 collective-permute-start.3
  45.4 4.4 %collective-permute-start.2 = (bf16[32,1,1,1024]{3,0,2,1:T(8,128)(2,1)S(1)}, bf16[32,1,1,1024]{3,0,2,1:T(8,128)(2,1)S(1)}, u32[]{:S(2)}, u32[]{:S(2)}) collective-permute-start(bf16[32,1,1,1024]{3,0,2,1:T(8,128)(2,1)S(1)} %get-tuple-element.187), channel_id=1, source_target_pairs={{0,1},{1,2},{2,3},{3,4},{4,5},{5,6},{6,7},{8,9},{9,10},{10,11},{11... | collective-permute-start | bytes 196616 | tf_op jit(solution)/shard_map/ppermute | solution.py:21
  49.7 1.1 collective-permute-done.2
  53.6 1.6 multiply_reduce_fusion
  56.3 1.3 collective-permute-start.5
  57.6 4.3 %collective-permute-start.4 = (bf16[64,1,1,256]{0,3,2,1:T(8,128)(2,1)S(1)}, bf16[64,1,1,256]{0,3,2,1:T(8,128)(2,1)S(1)}, u32[]{:S(2)}, u32[]{:S(2)}) collective-permute-start(bf16[64,1,1,256]{0,3,2,1:T(8,128)(2,1)S(1)} %fusion.138), channel_id=1, source_target_pairs={{0,1},{1,2},{2,3},{3,4},{4,5},{5,6},{6,7},{8,9},{9,10},{10,11},{11... | collective-permute-start | bytes 98312 | tf_op jit(solution)/shard_map/ppermute | solution.py:21
  61.9 2.0 %fusion.152 = (bf16[4,4,36,1024]{3,2,1,0:T(8,128)(2,1)}, bf16[4,4,36,1024]{3,2,1,0:T(8,128)(2,1)}, bf16[4,4,36,1024]{3,2,1,0:T(8,128)(2,1)}) fusion(bf16[6,4,36,1024]{3,2,1,0:T(8,128)(2,1)S(1)} %copy-done), kind=kLoop, calls=%fused_computation.314 | loop fusion | bytes 7077888 | tf_op jit(solution)/shard_map/slice | solution.py:246
  65.0 3.6 %concatenate.65 = bf16[1728,1,1,256]{0,3,2,1:T(8,128)(2,1)S(1)} concatenate(bf16[64,1,1,256]{0,3,2,1:T(8,128)(2,1)S(1)} %get-tuple-element.180, bf16[64,1,1,256]{0,3,2,1:T(8,128)(2,1)} %get-tuple-element.186, bf16[64,1,1,256]{0,3,2,1:T(8,128)(2,1)S(1)} %get-tuple-element.171, bf16[64,1,1,256]{0,3,2,1:T(8,128)(2,1)S(1)} %get-tuple-element.179, ...), dimensions={0} | concatenate | bytes 1769472 | tf_op jit(solution)/shard_map/while/body/eval_jaxpr/concatenate | solution.py:57
  68.6 1.9 convert_reduce_fusion.2
  70.5 1.3 collective-permute-start.7
  71.8 5.2 %collective-permute-start.6 = (bf16[128,1,1,256]{0,3,2,1:T(8,128)(2,1)S(1)}, bf16[128,1,1,256]{0,3,2,1:T(8,128)(2,1)S(1)}, u32[]{:S(2)}, u32[]{:S(2)}) collective-permute-start(bf16[128,1,1,256]{0,3,2,1:T(8,128)(2,1)S(1)} %get-tuple-element.147), channel_id=1, source_target_pairs={{0,1},{1,2},{2,3},{3,4},{4,5},{5,6},{6,7},{8,9},{9,10},{10,11},{11... | collective-permute-start | bytes 196616 | tf_op jit(solution)/shard_map/ppermute | solution.py:21
  82.4 1.3 collective-permute-start.9
  83.7 5.4 %collective-permute-start.8 = (bf16[64,1,1,1024]{3,0,2,1:T(8,128)(2,1)S(1)}, bf16[64,1,1,1024]{3,0,2,1:T(8,128)(2,1)S(1)}, u32[]{:S(2)}, u32[]{:S(2)}) collective-permute-start(bf16[64,1,1,1024]{3,0,2,1:T(8,128)(2,1)S(1)} %get-tuple-element.161), channel_id=1, source_target_pairs={{0,1},{1,2},{2,3},{3,4},{4,5},{5,6},{6,7},{8,9},{9,10},{10,11},{11... | collective-permute-start | bytes 393224 | tf_op jit(solution)/shard_map/ppermute | solution.py:21
  89.1 3.1 %fusion.25 = f32[864,64]{1,0:T(8,128)S(1)} fusion(bf16[64,2,1024]{2,0,1:T(8,128)(2,1)S(1)} %get-tuple-element.145, bf16[864,1,2,1024]{3,0,2,1:T(8,128)(2,1)} %copy-done.9), kind=kOutput, calls=%fused_computation.33 | convolution fusion | flops 226492416 | bytes 4022272 | tf_op jit(solution)/shard_map/while/body/eval_jaxpr/kgzp,ogzp->ko/dot_general | solution.py:66
  96.8 1.3 fusion.47
  99.1 2.3 %convert_reduce_fusion = (f32[32]{0:T(128)S(1)}, bf16[32,4,4,1024]{3,2,1,0:T(4,128)(2,1)S(1)}) fusion(bf16[32,4,4,1024]{3,2,1,0:T(4,128)(2,1)S(1)} %copy-done.1, f32[32,4,1024]{2,1,0:T(4,128)S(1)} %mul.1071), kind=kLoop, calls=%fused_computation.17 | loop fusion | flops 6291424 | bytes 2621568 | tf_op jit(solution)/shard_map/reduce_sum | solution.py:299
  101.5 2.9 %fusion.71 = f32[1,36,32]{1,2,0:T(8,128)S(1)} fusion(bf16[4,4,36,1024]{3,2,1,0:T(8,128)(2,1)} %get-tuple-element.149, bf16[32,4,4,1024]{3,2,1,0:T(4,128)(2,1)S(1)} %get-tuple-element.143), kind=kOutput, calls=%fused_computation.52 | convolution fusion | flops 37748736 | bytes 2232832 | tf_op jit(solution)/shard_map/zpkq,ozpq->ko/dot_general | solution.py:245
  104.4 1.5 fusion.68
  105.9 1.5 fusion.65
  108.1 4.4 %collective-permute-start.10 = (f32[1120,128]{1,0:T(8,128)S(1)}, f32[1120,128]{1,0:T(8,128)S(1)}, u32[]{:S(2)}, u32[]{:S(2)}) collective-permute-start(f32[1120,128]{1,0:T(8,128)S(1)} %constant_dynamic-slice_fusion.2), channel_id=1, source_target_pairs={{0,8},{8,0},{16,24},{24,16},{32,40},{40,32},{48,56},{56,48},{64,72... | collective-permute-start | bytes 1720328 | tf_op jit(solution)/shard_map/ppermute | solution.py:346
  112.6 1.6 collective-permute-done.10
  115.2 7.2 %collective-permute-done.11 = f32[560,128]{1,0:T(8,128)S(1)} collective-permute-done((f32[560,128]{1,0:T(8,128)S(1)}, f32[560,128]{1,0:T(8,128)S(1)}, u32[]{:S(2)}, u32[]{:S(2)}) %collective-permute-start.11) | collective-permute-done | bytes 286752 | tf_op jit(solution)/shard_map/ppermute | solution.py:346
  122.5 2.5 %collective-permute-start.12 = (f32[280,128]{1,0:T(8,128)S(1)}, f32[280,128]{1,0:T(8,128)S(1)}, u32[]{:S(2)}, u32[]{:S(2)}) collective-permute-start(f32[280,128]{1,0:T(8,128)S(1)} %constant_dynamic-slice_fusion), channel_id=1, source_target_pairs={{0,32},{8,40},{16,48},{24,56},{32,0},{40,8},{48,16},{56,24},{64,96... | collective-permute-start | bytes 430088 | tf_op jit(solution)/shard_map/ppermute | solution.py:346
  125.0 3.0 %collective-permute-done.12 = f32[280,128]{1,0:T(8,128)S(1)} collective-permute-done((f32[280,128]{1,0:T(8,128)S(1)}, f32[280,128]{1,0:T(8,128)S(1)}, u32[]{:S(2)}, u32[]{:S(2)}) %collective-permute-start.12) | collective-permute-done | bytes 143392 | tf_op jit(solution)/shard_map/ppermute | solution.py:346
  128.9 3.2 %collective-permute-done.13 = f32[280,128]{1,0:T(8,128)S(1)} collective-permute-done((f32[280,128]{1,0:T(8,128)S(1)}, f32[280,128]{1,0:T(8,128)S(1)}, u32[]{:S(2)}, u32[]{:S(2)}) %collective-permute-start.13) | collective-permute-done | bytes 143392 | tf_op jit(solution)/shard_map/ppermute | solution.py:349
  132.1 2.3 %collective-permute-start.14 = (f32[280,128]{1,0:T(8,128)S(1)}, f32[280,128]{1,0:T(8,128)S(1)}, u32[]{:S(2)}, u32[]{:S(2)}) collective-permute-start(f32[280,128]{1,0:T(8,128)S(1)} %add.414), channel_id=1, source_target_pairs={{0,128},{8,136},{16,144},{24,152},{32,160},{40,168},{48,176},{56,1... | collective-permute-start | bytes 430088 | tf_op jit(solution)/shard_map/ppermute | solution.py:349
  134.5 3.7 %collective-permute-done.14 = f32[280,128]{1,0:T(8,128)S(1)} collective-permute-done((f32[280,128]{1,0:T(8,128)S(1)}, f32[280,128]{1,0:T(8,128)S(1)}, u32[]{:S(2)}, u32[]{:S(2)}) %collective-permute-start.14) | collective-permute-done | bytes 143392 | tf_op jit(solution)/shard_map/ppermute | solution.py:349
  138.2 3.4 %collective-permute-start.15 = (f32[280,128]{1,0:T(8,128)S(1)}, f32[280,128]{1,0:T(8,128)S(1)}, u32[]{:S(2)}, u32[]{:S(2)}) collective-permute-start(f32[280,128]{1,0:T(8,128)S(1)} %add.415), channel_id=1, source_target_pairs={{0,1},{1,0},{2,3},{3,2},{4,5},{5,4},{6,7},{7,6},{8,9},{9,8},{10,11... | collective-permute-start | bytes 430088 | tf_op jit(solution)/shard_map/ppermute | solution.py:349
  141.5 2.5 %collective-permute-done.15 = f32[280,128]{1,0:T(8,128)S(1)} collective-permute-done((f32[280,128]{1,0:T(8,128)S(1)}, f32[280,128]{1,0:T(8,128)S(1)}, u32[]{:S(2)}, u32[]{:S(2)}) %collective-permute-start.15) | collective-permute-done | bytes 143392 | tf_op jit(solution)/shard_map/ppermute | solution.py:349
  144.0 6.2 %collective-permute-start.16 = (f32[280,128]{1,0:T(8,128)S(1)}, f32[280,128]{1,0:T(8,128)S(1)}, u32[]{:S(2)}, u32[]{:S(2)}) collective-permute-start(f32[280,128]{1,0:T(8,128)S(1)} %add.416), channel_id=1, source_target_pairs={{0,2},{1,3},{2,0},{3,1},{4,6},{5,7},{6,4},{7,5},{8,10},{9,11},{10,... | collective-permute-start | bytes 430088 | tf_op jit(solution)/shard_map/ppermute | solution.py:349
  150.3 2.8 %collective-permute-done.16 = f32[280,128]{1,0:T(8,128)S(1)} collective-permute-done((f32[280,128]{1,0:T(8,128)S(1)}, f32[280,128]{1,0:T(8,128)S(1)}, u32[]{:S(2)}, u32[]{:S(2)}) %collective-permute-start.16) | collective-permute-done | bytes 143392 | tf_op jit(solution)/shard_map/ppermute | solution.py:349
  153.2 6.3 %collective-permute-start.17 = (f32[280,128]{1,0:T(8,128)S(1)}, f32[280,128]{1,0:T(8,128)S(1)}, u32[]{:S(2)}, u32[]{:S(2)}) collective-permute-start(f32[280,128]{1,0:T(8,128)S(1)} %add.417), channel_id=1, source_target_pairs={{0,4},{1,5},{2,6},{3,7},{4,0},{5,1},{6,2},{7,3},{8,12},{9,13},{10,... | collective-permute-start | bytes 430088 | tf_op jit(solution)/shard_map/ppermute | solution.py:349
  159.4 3.6 %collective-permute-done.17 = f32[280,128]{1,0:T(8,128)S(1)} collective-permute-done((f32[280,128]{1,0:T(8,128)S(1)}, f32[280,128]{1,0:T(8,128)S(1)}, u32[]{:S(2)}, u32[]{:S(2)}) %collective-permute-start.17) | collective-permute-done | bytes 143392 | tf_op jit(solution)/shard_map/ppermute | solution.py:349
  163.1 3.0 %collective-permute-start.18 = (f32[280,128]{1,0:T(8,128)S(1)}, f32[280,128]{1,0:T(8,128)S(1)}, u32[]{:S(2)}, u32[]{:S(2)}) collective-permute-start(f32[280,128]{1,0:T(8,128)S(1)} %add.418), channel_id=1, source_target_pairs={{0,32},{8,40},{16,48},{24,56},{32,0},{40,8},{48,16},{56,24},{64,96... | collective-permute-start | bytes 430088 | tf_op jit(solution)/shard_map/ppermute | solution.py:351
  166.1 2.5 %collective-permute-done.18 = f32[280,128]{1,0:T(8,128)S(1)} collective-permute-done((f32[280,128]{1,0:T(8,128)S(1)}, f32[280,128]{1,0:T(8,128)S(1)}, u32[]{:S(2)}, u32[]{:S(2)}) %collective-permute-start.18) | collective-permute-done | bytes 143392 | tf_op jit(solution)/shard_map/ppermute | solution.py:351
  168.7 1.4 collective-permute-start.19
  170.1 4.2 %collective-permute-done.19 = f32[560,128]{1,0:T(8,128)S(1)} collective-permute-done((f32[560,128]{1,0:T(8,128)S(1)}, f32[560,128]{1,0:T(8,128)S(1)}, u32[]{:S(2)}, u32[]{:S(2)}) %collective-permute-start.19) | collective-permute-done | bytes 286752 | tf_op jit(solution)/shard_map/ppermute | solution.py:351
  174.5 12.1 %collective-permute-start.20 = (f32[1120,128]{1,0:T(8,128)S(1)}, f32[1120,128]{1,0:T(8,128)S(1)}, u32[]{:S(2)}, u32[]{:S(2)}) collective-permute-start(f32[1120,128]{1,0:T(8,128)S(1)} %get-tuple-element.153), channel_id=1, source_target_pairs={{0,8},{8,0},{16,24},{24,16},{32,40},{40,32},{48,56},{56,48},{64,72... | collective-permute-start | bytes 1720328 | tf_op jit(solution)/shard_map/ppermute | solution.py:351
  (182 shorter events, 29.1 us)
Async XLA Ops:
  1.7 13.1 %collective-permute-start.1 = (bf16[4,1,1,4096]{3,2,1,0:T(2,128)(2,1)S(1)}, bf16[4,1,1,4096]{3,2,1,0:T(2,128)(2,1)S(1)}, u32[]{:S(2)}, u32[]{:S(2)}) collective-permute-start(bf16[4,1,1,4096]{3,2,1,0:T(2,128)(2,1)S(1)} %get-tuple-element.190), channel_id=1, source_target_pairs={{1,0},{2,1},{3,2},{4,3},{5,4},{6,5},{7,6},{9,8},{10,9},{11,10},{12... | collective-permute-start | bytes 98312 | tf_op jit(solution)/shard_map/ppermute | solution.py:22
  3.0 11.8 %collective-permute-start = (bf16[4,1,1,4096]{3,2,1,0:T(2,128)(2,1)S(1)}, bf16[4,1,1,4096]{3,2,1,0:T(2,128)(2,1)S(1)}, u32[]{:S(2)}, u32[]{:S(2)}) collective-permute-start(bf16[4,1,1,4096]{3,2,1,0:T(2,128)(2,1)S(1)} %get-tuple-element.189), channel_id=1, source_target_pairs={{0,1},{1,2},{2,3},{3,4},{4,5},{5,6},{6,7},{8,9},{9,10},{10,11},{11... | collective-permute-start | bytes 98312 | tf_op jit(solution)/shard_map/ppermute | solution.py:21
  44.1 5.7 %collective-permute-start.3 = (bf16[32,1,1,1024]{3,0,2,1:T(8,128)(2,1)S(1)}, bf16[32,1,1,1024]{3,0,2,1:T(8,128)(2,1)S(1)}, u32[]{:S(2)}, u32[]{:S(2)}) collective-permute-start(bf16[32,1,1,1024]{3,0,2,1:T(8,128)(2,1)S(1)} %get-tuple-element.188), channel_id=1, source_target_pairs={{1,0},{2,1},{3,2},{4,3},{5,4},{6,5},{7,6},{9,8},{10,9},{11,10},{12... | collective-permute-start | bytes 196616 | tf_op jit(solution)/shard_map/ppermute | solution.py:22
  45.4 5.5 %collective-permute-start.2 = (bf16[32,1,1,1024]{3,0,2,1:T(8,128)(2,1)S(1)}, bf16[32,1,1,1024]{3,0,2,1:T(8,128)(2,1)S(1)}, u32[]{:S(2)}, u32[]{:S(2)}) collective-permute-start(bf16[32,1,1,1024]{3,0,2,1:T(8,128)(2,1)S(1)} %get-tuple-element.187), channel_id=1, source_target_pairs={{0,1},{1,2},{2,3},{3,4},{4,5},{5,6},{6,7},{8,9},{9,10},{10,11},{11... | collective-permute-start | bytes 196616 | tf_op jit(solution)/shard_map/ppermute | solution.py:21
  51.0 2.5 %copy-start.7 = (bf16[27,32,64]{2,1,0:T(8,128)(2,1)S(1)}, bf16[27,32,64]{2,1,0:T(8,128)(2,1)}, u32[]{:S(2)}) copy-start(bf16[27,32,64]{2,1,0:T(8,128)(2,1)} %param.12) | copy-start | bytes 331780
  51.1 2.5 %copy-start.10 = (f32[64]{0:T(128)S(1)}, f32[64]{0:T(128)}, u32[]{:S(2)}) copy-start(f32[64]{0:T(128)} %param.13) | copy-start | bytes 772
  53.6 2.1 %copy-start.9 = (bf16[864,1,2,1024]{3,0,2,1:T(8,128)(2,1)}, bf16[864,1,2,1024]{3,0,2,1:T(8,128)(2,1)S(1)}, u32[]{:S(2)}) copy-start(bf16[864,1,2,1024]{3,0,2,1:T(8,128)(2,1)S(1)} %constant_dynamic-update-slice_fusion) | copy-start | bytes 10616836
  53.6 8.3 %copy-start = (bf16[6,4,36,1024]{3,2,1,0:T(8,128)(2,1)S(1)}, bf16[6,4,36,1024]{3,2,1,0:T(8,128)(2,1)}, u32[]{:S(2)}) copy-start(bf16[6,4,36,1024]{3,2,1,0:T(8,128)(2,1)} %get-tuple-element.83) | copy-start | bytes 5308420
  56.3 7.6 %collective-permute-start.5 = (bf16[64,1,1,256]{0,3,2,1:T(8,128)(2,1)S(1)}, bf16[64,1,1,256]{0,3,2,1:T(8,128)(2,1)S(1)}, u32[]{:S(2)}, u32[]{:S(2)}) collective-permute-start(bf16[64,1,1,256]{0,3,2,1:T(8,128)(2,1)S(1)} %fusion.138), channel_id=1, source_target_pairs={{1,0},{2,1},{3,2},{4,3},{5,4},{6,5},{7,6},{9,8},{10,9},{11,10},{12... | collective-permute-start | bytes 98312 | tf_op jit(solution)/shard_map/ppermute | solution.py:22
  57.6 6.3 %collective-permute-start.4 = (bf16[64,1,1,256]{0,3,2,1:T(8,128)(2,1)S(1)}, bf16[64,1,1,256]{0,3,2,1:T(8,128)(2,1)S(1)}, u32[]{:S(2)}, u32[]{:S(2)}) collective-permute-start(bf16[64,1,1,256]{0,3,2,1:T(8,128)(2,1)S(1)} %fusion.138), channel_id=1, source_target_pairs={{0,1},{1,2},{2,3},{3,4},{4,5},{5,6},{6,7},{8,9},{9,10},{10,11},{11... | collective-permute-start | bytes 98312 | tf_op jit(solution)/shard_map/ppermute | solution.py:21
  63.9 4.6 %copy-start.6 = (bf16[27,64,128]{2,1,0:T(8,128)(2,1)S(1)}, bf16[27,64,128]{2,1,0:T(8,128)(2,1)}, u32[]{:S(2)}) copy-start(bf16[27,64,128]{2,1,0:T(8,128)(2,1)} %param.14) | copy-start | bytes 1327108
  63.9 4.6 %copy-start.11 = (f32[128]{0:T(128)S(1)}, f32[128]{0:T(128)}, u32[]{:S(2)}) copy-start(f32[128]{0:T(128)} %param.15) | copy-start | bytes 1540
  70.5 7.0 %collective-permute-start.7 = (bf16[128,1,1,256]{0,3,2,1:T(8,128)(2,1)S(1)}, bf16[128,1,1,256]{0,3,2,1:T(8,128)(2,1)S(1)}, u32[]{:S(2)}, u32[]{:S(2)}) collective-permute-start(bf16[128,1,1,256]{0,3,2,1:T(8,128)(2,1)S(1)} %get-tuple-element.147), channel_id=1, source_target_pairs={{1,0},{2,1},{3,2},{4,3},{5,4},{6,5},{7,6},{9,8},{10,9},{11,10},{12... | collective-permute-start | bytes 196616 | tf_op jit(solution)/shard_map/ppermute | solution.py:22
  71.8 6.6 %collective-permute-start.6 = (bf16[128,1,1,256]{0,3,2,1:T(8,128)(2,1)S(1)}, bf16[128,1,1,256]{0,3,2,1:T(8,128)(2,1)S(1)}, u32[]{:S(2)}, u32[]{:S(2)}) collective-permute-start(bf16[128,1,1,256]{0,3,2,1:T(8,128)(2,1)S(1)} %get-tuple-element.147), channel_id=1, source_target_pairs={{0,1},{1,2},{2,3},{3,4},{4,5},{5,6},{6,7},{8,9},{9,10},{10,11},{11... | collective-permute-start | bytes 196616 | tf_op jit(solution)/shard_map/ppermute | solution.py:21
  78.6 3.4 %copy-start.5 = (f32[64,2,1024]{2,0,1:T(8,128)S(1)}, f32[64,2,1024]{2,0,1:T(8,128)}, u32[]{:S(2)}) copy-start(f32[64,2,1024]{2,0,1:T(8,128)} %get-tuple-element.192) | copy-start | bytes 1572868
  82.4 10.6 %collective-permute-start.9 = (bf16[64,1,1,1024]{3,0,2,1:T(8,128)(2,1)S(1)}, bf16[64,1,1,1024]{3,0,2,1:T(8,128)(2,1)S(1)}, u32[]{:S(2)}, u32[]{:S(2)}) collective-permute-start(bf16[64,1,1,1024]{3,0,2,1:T(8,128)(2,1)S(1)} %get-tuple-element.162), channel_id=1, source_target_pairs={{1,0},{2,1},{3,2},{4,3},{5,4},{6,5},{7,6},{9,8},{10,9},{11,10},{12... | collective-permute-start | bytes 393224 | tf_op jit(solution)/shard_map/ppermute | solution.py:22
  83.7 9.3 %collective-permute-start.8 = (bf16[64,1,1,1024]{3,0,2,1:T(8,128)(2,1)S(1)}, bf16[64,1,1,1024]{3,0,2,1:T(8,128)(2,1)S(1)}, u32[]{:S(2)}, u32[]{:S(2)}) collective-permute-start(bf16[64,1,1,1024]{3,0,2,1:T(8,128)(2,1)S(1)} %get-tuple-element.161), channel_id=1, source_target_pairs={{0,1},{1,2},{2,3},{3,4},{4,5},{5,6},{6,7},{8,9},{9,10},{10,11},{11... | collective-permute-start | bytes 393224 | tf_op jit(solution)/shard_map/ppermute | solution.py:21
  96.7 2.4 %copy-start.1 = (bf16[32,4,4,1024]{3,2,1,0:T(4,128)(2,1)S(1)}, bf16[32,4,4,1024]{3,2,1,0:T(4,128)(2,1)}, u32[]{:S(2)}) copy-start(bf16[32,4,4,1024]{3,2,1,0:T(4,128)(2,1)} %get-tuple-element.82) | copy-start | bytes 3145732
  99.1 5.3 %copy-start.3 = (bf16[4,4,36,1024]{3,2,1,0:T(8,128)(2,1)S(1)}, bf16[4,4,36,1024]{3,2,1,0:T(8,128)(2,1)}, u32[]{:S(2)}) copy-start(bf16[4,4,36,1024]{3,2,1,0:T(8,128)(2,1)} %get-tuple-element.150) | copy-start | bytes 3538948
  101.5 4.4 %copy-start.2 = (bf16[4,4,36,1024]{3,2,1,0:T(8,128)(2,1)S(1)}, bf16[4,4,36,1024]{3,2,1,0:T(8,128)(2,1)}, u32[]{:S(2)}) copy-start(bf16[4,4,36,1024]{3,2,1,0:T(8,128)(2,1)} %get-tuple-element.148) | copy-start | bytes 3538948
  104.4 3.3 %copy-start.4 = (f32[432,128]{1,0:T(8,128)S(1)}, f32[432,128]{1,0:T(8,128)}, u32[]{:S(2)}) copy-start(f32[432,128]{1,0:T(8,128)} %reshape.313) | copy-start | bytes 663556
  108.1 6.1 %collective-permute-start.10 = (f32[1120,128]{1,0:T(8,128)S(1)}, f32[1120,128]{1,0:T(8,128)S(1)}, u32[]{:S(2)}, u32[]{:S(2)}) collective-permute-start(f32[1120,128]{1,0:T(8,128)S(1)} %constant_dynamic-slice_fusion.2), channel_id=1, source_target_pairs={{0,8},{8,0},{16,24},{24,16},{32,40},{40,32},{48,56},{56,48},{64,72... | collective-permute-start | bytes 1720328 | tf_op jit(solution)/shard_map/ppermute | solution.py:346
  114.3 8.1 %collective-permute-start.11 = (f32[560,128]{1,0:T(8,128)S(1)}, f32[560,128]{1,0:T(8,128)S(1)}, u32[]{:S(2)}, u32[]{:S(2)}) collective-permute-start(f32[560,128]{1,0:T(8,128)S(1)} %constant_dynamic-slice_fusion.1), channel_id=1, source_target_pairs={{0,16},{8,24},{16,0},{24,8},{32,48},{40,56},{48,32},{56,40},{64,80... | collective-permute-start | bytes 860168 | tf_op jit(solution)/shard_map/ppermute | solution.py:346
  122.5 64.1 %copy-start.8 = (f32[128,256]{0,1:T(8,128)S(1)}, f32[128,256]{0,1:T(8,128)}, u32[]{:S(2)}) copy-start(f32[128,256]{0,1:T(8,128)} %get-tuple-element.193) | copy-start | bytes 393220
  122.5 5.5 %collective-permute-start.12 = (f32[280,128]{1,0:T(8,128)S(1)}, f32[280,128]{1,0:T(8,128)S(1)}, u32[]{:S(2)}, u32[]{:S(2)}) collective-permute-start(f32[280,128]{1,0:T(8,128)S(1)} %constant_dynamic-slice_fusion), channel_id=1, source_target_pairs={{0,32},{8,40},{16,48},{24,56},{32,0},{40,8},{48,16},{56,24},{64,96... | collective-permute-start | bytes 430088 | tf_op jit(solution)/shard_map/ppermute | solution.py:346
  128.1 4.0 %collective-permute-start.13 = (f32[280,128]{1,0:T(8,128)S(1)}, f32[280,128]{1,0:T(8,128)S(1)}, u32[]{:S(2)}, u32[]{:S(2)}) collective-permute-start(f32[280,128]{1,0:T(8,128)S(1)} %dynamic-slice_add_fusion.2), channel_id=1, source_target_pairs={{0,64},{8,72},{16,80},{24,88},{32,96},{40,104},{48,112},{56,120},{... | collective-permute-start | bytes 430088 | tf_op jit(solution)/shard_map/ppermute | solution.py:349
  132.1 6.0 %collective-permute-start.14 = (f32[280,128]{1,0:T(8,128)S(1)}, f32[280,128]{1,0:T(8,128)S(1)}, u32[]{:S(2)}, u32[]{:S(2)}) collective-permute-start(f32[280,128]{1,0:T(8,128)S(1)} %add.414), channel_id=1, source_target_pairs={{0,128},{8,136},{16,144},{24,152},{32,160},{40,168},{48,176},{56,1... | collective-permute-start | bytes 430088 | tf_op jit(solution)/shard_map/ppermute | solution.py:349
  138.2 5.9 %collective-permute-start.15 = (f32[280,128]{1,0:T(8,128)S(1)}, f32[280,128]{1,0:T(8,128)S(1)}, u32[]{:S(2)}, u32[]{:S(2)}) collective-permute-start(f32[280,128]{1,0:T(8,128)S(1)} %add.415), channel_id=1, source_target_pairs={{0,1},{1,0},{2,3},{3,2},{4,5},{5,4},{6,7},{7,6},{8,9},{9,8},{10,11... | collective-permute-start | bytes 430088 | tf_op jit(solution)/shard_map/ppermute | solution.py:349
  144.0 9.1 %collective-permute-start.16 = (f32[280,128]{1,0:T(8,128)S(1)}, f32[280,128]{1,0:T(8,128)S(1)}, u32[]{:S(2)}, u32[]{:S(2)}) collective-permute-start(f32[280,128]{1,0:T(8,128)S(1)} %add.416), channel_id=1, source_target_pairs={{0,2},{1,3},{2,0},{3,1},{4,6},{5,7},{6,4},{7,5},{8,10},{9,11},{10,... | collective-permute-start | bytes 430088 | tf_op jit(solution)/shard_map/ppermute | solution.py:349
  153.2 9.9 %collective-permute-start.17 = (f32[280,128]{1,0:T(8,128)S(1)}, f32[280,128]{1,0:T(8,128)S(1)}, u32[]{:S(2)}, u32[]{:S(2)}) collective-permute-start(f32[280,128]{1,0:T(8,128)S(1)} %add.417), channel_id=1, source_target_pairs={{0,4},{1,5},{2,6},{3,7},{4,0},{5,1},{6,2},{7,3},{8,12},{9,13},{10,... | collective-permute-start | bytes 430088 | tf_op jit(solution)/shard_map/ppermute | solution.py:349
  163.1 5.5 %collective-permute-start.18 = (f32[280,128]{1,0:T(8,128)S(1)}, f32[280,128]{1,0:T(8,128)S(1)}, u32[]{:S(2)}, u32[]{:S(2)}) collective-permute-start(f32[280,128]{1,0:T(8,128)S(1)} %add.418), channel_id=1, source_target_pairs={{0,32},{8,40},{16,48},{24,56},{32,0},{40,8},{48,16},{56,24},{64,96... | collective-permute-start | bytes 430088 | tf_op jit(solution)/shard_map/ppermute | solution.py:351
  168.7 5.6 %collective-permute-start.19 = (f32[560,128]{1,0:T(8,128)S(1)}, f32[560,128]{1,0:T(8,128)S(1)}, u32[]{:S(2)}, u32[]{:S(2)}) collective-permute-start(f32[560,128]{1,0:T(8,128)S(1)} %get-tuple-element.157), channel_id=1, source_target_pairs={{0,16},{8,24},{16,0},{24,8},{32,48},{40,56},{48,32},{56,40},{64,80... | collective-permute-start | bytes 860168 | tf_op jit(solution)/shard_map/ppermute | solution.py:351
  174.5 13.7 %collective-permute-start.20 = (f32[1120,128]{1,0:T(8,128)S(1)}, f32[1120,128]{1,0:T(8,128)S(1)}, u32[]{:S(2)}, u32[]{:S(2)}) collective-permute-start(f32[1120,128]{1,0:T(8,128)S(1)} %get-tuple-element.153), channel_id=1, source_target_pairs={{0,8},{8,0},{16,24},{24,16},{32,40},{40,32},{48,56},{56,48},{64,72... | collective-permute-start | bytes 1720328 | tf_op jit(solution)/shard_map/ppermute | solution.py:351

commit v5 on v4

--- a/solution.py
+++ b/solution.py
@@ -147,41 +147,6 @@
     return lax.fori_loop(0, samples * per_sample, data_block_step, out_buffer)
 
 
-def parity_split(values, row_width):
-    c, n, z, plane = values.shape
-    rows = plane // row_width
-    grouped = values.reshape(c, n, z, rows // 2, 2, row_width // 2, 2)
-    grouped = grouped.transpose(0, 1, 2, 4, 6, 3, 5)
-    return grouped.reshape(c, n, z, 4, plane // 4)
-
-def parity_taps(split, coarse_width):
-    depth_len = split.shape[2] - 2
-    size = split.shape[4]
-    pad = coarse_width + 1
-    flattened = jnp.pad(split, ((0, 0), (0, 0), (0, 0), (0, 0), (pad, pad)))
-    column = lax.broadcasted_iota(jnp.int32, (1, 1, 1, size), 3) % coarse_width
-    left_mask = (column >= 1).astype(split.dtype)
-    right_mask = (column <= coarse_width - 2).astype(split.dtype)
-    blocks = []
-    for a in range(2):
-        for b in range(2):
-            pieces = []
-            for tap_index in range(27):
-                depth_start = tap_index // 9
-                row_sum = a + tap_index // 3 % 3 - 1
-                col_sum = b + tap_index % 3 - 1
-                source = (row_sum % 2) * 2 + col_sum % 2
-                row_step, col_step = row_sum // 2, col_sum // 2
-                offset = pad + row_step * coarse_width + col_step
-                shifted = flattened[:, :, depth_start : depth_start + depth_len, source, offset : offset + size]
-                if col_step < 0:
-                    shifted = shifted * left_mask
-                elif col_step > 0:
-                    shifted = shifted * right_mask
-                pieces.append(shifted)
-            blocks.append(jnp.concatenate(pieces, axis=0))
-    return jnp.stack(blocks, axis=3)
-
 def parity_pool(values):
     c, n, z, parities, size = values.shape
     return values.reshape(c, n, z // 2, 2 * parities, size).mean(axis=3)
@@ -192,8 +157,22 @@
     return grouped.reshape(c, n, 2 * z, 4, size) * 0.125
 
 
-def _parity_kernel(coarse_width, src_ref, w_ref, b_ref, out_ref, shifted_ref):
-    channels, depth, _, size = src_ref.shape
+def parity_permutation(row_width, chunk=128):
+    lane = jnp.arange(chunk)
+    yy, x = lane // row_width, lane % row_width
+    target = ((yy % 2) * 2 + x % 2) * (chunk // 4) + (yy // 2) * (row_width // 2) + x // 2
+    return (target[:, None] == jnp.arange(chunk)[None, :]).astype(jnp.bfloat16)
+
+def _parity_kernel(coarse_width, channels, src_ref, perm_ref, w_ref, b_ref, out_ref, shifted_ref, sub_ref):
+    rows_total, plane = src_ref.shape
+    depth = rows_total // channels
+    chunk = perm_ref.shape[0]
+    quarter = chunk // 4
+    for g in range(plane // chunk):
+        moved = jnp.dot(src_ref[:, g * chunk : (g + 1) * chunk], perm_ref[...], preferred_element_type=jnp.float32)
+        for s in range(4):
+            sub_ref[s, :, g * quarter : (g + 1) * quarter] = moved[:, s * quarter : (s + 1) * quarter]
+    size = plane // 4
     lane = lax.broadcasted_iota(jnp.int32, (channels, size), 1)
     row = lane // coarse_width
     col = lane % coarse_width
@@ -208,7 +187,7 @@
                     key = (row_sum % 2, col_sum % 2, row_sum // 2, col_sum // 2)
                     if key not in cache:
                         source, row_step, col_step = key[0] * 2 + key[1], key[2], key[3]
-                        values = src_ref[:, source_plane, source, :].astype(jnp.float32)
+                        values = sub_ref[source, source_plane * channels : (source_plane + 1) * channels, :]
                         step = row_step * coarse_width + col_step
                         if step != 0:
                             values = pltpu.roll(values, (-step) % size, 1)
@@ -227,17 +206,20 @@
                 )
             out_ref[:, z, parity, :] = summed.astype(out_ref.dtype)
 
-def parity_conv_forward(split, weight, bias_values, coarse_width):
-    channels, depth, parities, size = split.shape
+def parity_conv_forward(padded, weight, bias_values, row_width):
+    channels, depth, plane = padded.shape
     out_channels = weight.shape[2]
     per_depth = weight.reshape(3, 9 * channels, out_channels).transpose(0, 2, 1)
+    by_plane = padded.transpose(1, 0, 2).reshape(depth * channels, plane)
     return pl.pallas_call(
-        functools.partial(_parity_kernel, coarse_width),
+        functools.partial(_parity_kernel, row_width // 2, channels),
         out_shape=(
-            jax.ShapeDtypeStruct((out_channels, depth - 2, parities, size), jnp.bfloat16),
-            jax.ShapeDtypeStruct((depth, parities, 9 * channels, size), jnp.bfloat16),
+            jax.ShapeDtypeStruct((out_channels, depth - 2, 4, plane // 4), jnp.bfloat16),
+            jax.ShapeDtypeStruct((depth, 4, 9 * channels, plane // 4), jnp.bfloat16),
         ),
-    )(split, per_depth, bias_values.reshape(out_channels, 1))
+        scratch_shapes=[pltpu.VMEM((4, depth * channels, plane // 4), jnp.float32)],
+    )(by_plane, parity_permutation(row_width), per_depth, bias_values.reshape(out_channels, 1))
+
 
 def parity_weight_grad(shifted, delta):
     depth_len = delta.shape[1]
@@ -258,10 +240,9 @@
     flipped_second = jnp.flip(w_second, 0).transpose(0, 2, 1)
     flipped_third = jnp.flip(w_third, 0).transpose(0, 2, 1)
     volume_padded = with_halo(volume, (("slab", 2),), 1)
-    first_split = parity_split(volume_padded, SX)
     first_layer = [
-        parity_conv_forward(first_split[:, s], w_first, b_first, SX // 2)
-        for s in range(first_split.shape[1])
+        parity_conv_forward(volume_padded[:, s], w_first, b_first, SX)
+        for s in range(volume_padded.shape[1])
     ]
     first_pre = jnp.stack([pre for pre, _ in first_layer], axis=1)
     first_pooled = parity_pool(jax.nn.silu(first_pre.astype(jnp.float32))).astype(jnp.bfloat16)

time: 194 us -> 176 us (0.907)
  local copies, waits for them, and re-layouts: 41.9 us -> 23.5 us
    transpose x1, local copies, waits for them, and re-layouts: 13.3 us -> 0.16 us  [parity_conv_forward(): by_plane = padded.transpose(1, 0, 2).reshape(depth * channels, plane)]
    concatenate x1 -> x0, local copies, waits for them, and re-layouts: 3.41 us -> none  [with_halo(): shard = jnp.concatenate([before, shard, after], axis=dim)]
    another operation x1 -> x0, local copies, waits for them, and re-layouts: 2.47 us -> none  [per_device(): first_split[:, s]]
  transfers between devices with their start and end apart: 21 -> 21, of which waited for: 13 -> 13; matrix products, arithmetic and copies ran while one was open for 7% -> 8% of each run, Pallas kernels for 0% -> 0%
where the time goes in v5:
time: 176 us; the launch traced here: 174 us
  starting transfers between devices  73.7 us (42%)
  waiting for transfers between devices  37.3 us (21%)
  local copies, waits for them, and re-layouts  23.5 us (13%)
  other arithmetic  18.6 us (11%)
  matrix products  15 us (9%)
  Pallas kernels  4.42 us (3%)
  between operations  1.86 us (1%)
    ppermute x5, starting transfers between devices, with_halo(): before = lax.ppermute(last, axis, up)  24.1 us
    ppermute x5, starting transfers between devices, all_reduce_rows(): buffer = buffer + lax.ppermute(buffer, axis, xor_pairs(axis, mask))  19.2 us
    ppermute x3, starting transfers between devices, all_reduce_rows(): other = lax.ppermute(buffer, axis, xor_pairs(axis, mask))  16.1 us
    ppermute x5, waiting for transfers between devices, all_reduce_rows(): buffer = buffer + lax.ppermute(buffer, axis, xor_pairs(axis, mask))  15.9 us
    ppermute x3, waiting for transfers between devices, all_reduce_rows(): buffer = keep + lax.ppermute(send, axis, xor_pairs(axis, mask))  11.9 us
    ppermute x3, starting transfers between devices, all_reduce_rows(): buffer = keep + lax.ppermute(send, axis, xor_pairs(axis, mask))  7.79 us
    ppermute x3, waiting for transfers between devices, all_reduce_rows(): other = lax.ppermute(buffer, axis, xor_pairs(axis, mask))  7.55 us
    ppermute x5, starting transfers between devices, with_halo(): after = lax.ppermute(first, axis, down)  6.45 us
  transfers between devices with their start and end apart: 21, of which 13 were waited for; matrix products, arithmetic and copies ran while one was open for 8% of the time, Pallas kernels for 0%

profile of v5, /device:TPU:1, one launch (start us, length us, event | category | flops | bytes accessed | tf_op | source)
XLA Modules:
  0.0 174.5 jit_solution(2047250546994353385)
XLA Ops:
  0.6 1.1 fusion.158
  1.7 1.3 collective-permute-start.1
  3.0 5.0 %collective-permute-start = (bf16[4,1,1,4096]{3,2,1,0:T(2,128)(2,1)S(1)}, bf16[4,1,1,4096]{3,2,1,0:T(2,128)(2,1)S(1)}, u32[]{:S(2)}, u32[]{:S(2)}) collective-permute-start(bf16[4,1,1,4096]{3,2,1,0:T(2,128)(2,1)S(1)} %get-tuple-element.189), channel_id=1, source_target_pairs={{0,1},{1,2},{2,3},{3,4},{4,5},{5,6},{6,7},{8,9},{9,10},{10,11},{11... | collective-permute-start | bytes 98312 | tf_op jit(solution)/shard_map/ppermute | solution.py:21
  8.8 1.0 reverse_bitcast_fusion
  10.8 1.6 copy.94
  13.8 1.3 copy.90.b_ref
  15.5 1.1 maximum_bitcast_fusion
  17.6 4.4 %shard_map.135 = (bf16[32,4,4,1024]{3,2,1,0:T(4,128)(2,1)}, bf16[6,4,36,1024]{3,2,1,0:T(8,128)(2,1)}) custom-call(bf16[24,4096]{1,0:T(8,128)(2,1)} %reshape.381.src_ref, bf16[128,128]{1,0:T(8,128)(2,1)} %fusion.141.perm_ref, bf16[3,32,36]{2,1,0:T(8,128)(2,1)} %bitcast.167, f32[32,1]{1,0:T(8,128)} %copy.90.b_ref), custom_call_target="tpu_custom_call" | custom-call | tf_op jit(solution)/shard_map/pallas_call | solution.py:214
  22.0 4.0 %fusion.9 = f32[32,4,1024]{2,1,0:T(4,128)S(1)} fusion(bf16[32,4,4,1024]{3,2,1,0:T(4,128)(2,1)} %get-tuple-element.82), kind=kLoop, calls=%fused_computation.12 | loop fusion | flops 3014656 | bytes 1572864 | tf_op jit(solution)/shard_map/reduce_sum | solution.py:152
  26.3 1.3 collective-permute-start.3
  27.6 4.2 %collective-permute-start.2 = (bf16[32,1,1,1024]{3,0,2,1:T(8,128)(2,1)S(1)}, bf16[32,1,1,1024]{3,0,2,1:T(8,128)(2,1)S(1)}, u32[]{:S(2)}, u32[]{:S(2)}) collective-permute-start(bf16[32,1,1,1024]{3,0,2,1:T(8,128)(2,1)S(1)} %get-tuple-element.187), channel_id=1, source_target_pairs={{0,1},{1,2},{2,3},{3,4},{4,5},{5,6},{6,7},{8,9},{9,10},{10,11},{11... | collective-permute-start | bytes 196616 | tf_op jit(solution)/shard_map/ppermute | solution.py:21
  31.8 1.3 collective-permute-done.2
  35.8 1.6 multiply_reduce_fusion
  38.5 1.3 collective-permute-start.5
  39.8 4.3 %collective-permute-start.4 = (bf16[64,1,1,256]{0,3,2,1:T(8,128)(2,1)S(1)}, bf16[64,1,1,256]{0,3,2,1:T(8,128)(2,1)S(1)}, u32[]{:S(2)}, u32[]{:S(2)}) collective-permute-start(bf16[64,1,1,256]{0,3,2,1:T(8,128)(2,1)S(1)} %fusion.138), channel_id=1, source_target_pairs={{0,1},{1,2},{2,3},{3,4},{4,5},{5,6},{6,7},{8,9},{9,10},{10,11},{11... | collective-permute-start | bytes 98312 | tf_op jit(solution)/shard_map/ppermute | solution.py:21
  44.2 2.0 %fusion.155 = (bf16[4,4,36,1024]{3,2,1,0:T(8,128)(2,1)}, bf16[4,4,36,1024]{3,2,1,0:T(8,128)(2,1)}, bf16[4,4,36,1024]{3,2,1,0:T(8,128)(2,1)}) fusion(bf16[6,4,36,1024]{3,2,1,0:T(8,128)(2,1)S(1)} %copy-done), kind=kLoop, calls=%fused_computation.334 | loop fusion | bytes 7077888 | tf_op jit(solution)/shard_map/slice | solution.py:228
  47.2 3.6 %concatenate.65 = bf16[1728,1,1,256]{0,3,2,1:T(8,128)(2,1)S(1)} concatenate(bf16[64,1,1,256]{0,3,2,1:T(8,128)(2,1)S(1)} %get-tuple-element.180, bf16[64,1,1,256]{0,3,2,1:T(8,128)(2,1)} %get-tuple-element.186, bf16[64,1,1,256]{0,3,2,1:T(8,128)(2,1)S(1)} %get-tuple-element.171, bf16[64,1,1,256]{0,3,2,1:T(8,128)(2,1)S(1)} %get-tuple-element.179, ...), dimensions={0} | concatenate | bytes 1769472 | tf_op jit(solution)/shard_map/while/body/eval_jaxpr/concatenate | solution.py:57
  50.8 1.9 %convert_reduce_fusion.2 = (f32[128]{0:T(128)S(1)}, bf16[128,1,1,256]{0,3,2,1:T(8,128)(2,1)S(1)}, f32[128,256]{0,1:T(8,128)}) fusion(bf16[128,1,1,256]{0,3,2,1:T(8,128)(2,1)} %copy.94, f32[128]{0:T(128)S(1)} %copy-done.11, bf16[1728,128]{1,0:T(8,128)(2,1)S(1)} %bitcast.163, bf16[1728,1,1,256]{0,3,2,1:T(8,128)(2,1)S(1)} %concatenate.65), kind=kOutput, calls=%fused_computation.248 | convolution fusion | flops 113737600 | bytes 1590272 | tf_op jit(solution)/shard_map/while/body/eval_jaxpr/ko,kgzp->ogzp/dot_general | solution.py:62
  52.7 1.3 collective-permute-start.7
  54.0 5.4 %collective-permute-start.6 = (bf16[128,1,1,256]{0,3,2,1:T(8,128)(2,1)S(1)}, bf16[128,1,1,256]{0,3,2,1:T(8,128)(2,1)S(1)}, u32[]{:S(2)}, u32[]{:S(2)}) collective-permute-start(bf16[128,1,1,256]{0,3,2,1:T(8,128)(2,1)S(1)} %get-tuple-element.147), channel_id=1, source_target_pairs={{0,1},{1,2},{2,3},{3,4},{4,5},{5,6},{6,7},{8,9},{9,10},{10,11},{11... | collective-permute-start | bytes 196616 | tf_op jit(solution)/shard_map/ppermute | solution.py:21
  64.6 1.3 collective-permute-start.9
  65.9 5.2 %collective-permute-start.8 = (bf16[64,1,1,1024]{3,0,2,1:T(8,128)(2,1)S(1)}, bf16[64,1,1,1024]{3,0,2,1:T(8,128)(2,1)S(1)}, u32[]{:S(2)}, u32[]{:S(2)}) collective-permute-start(bf16[64,1,1,1024]{3,0,2,1:T(8,128)(2,1)S(1)} %get-tuple-element.161), channel_id=1, source_target_pairs={{0,1},{1,2},{2,3},{3,4},{4,5},{5,6},{6,7},{8,9},{9,10},{10,11},{11... | collective-permute-start | bytes 393224 | tf_op jit(solution)/shard_map/ppermute | solution.py:21
  71.1 3.1 %fusion.25 = f32[864,64]{1,0:T(8,128)S(1)} fusion(bf16[64,2,1024]{2,0,1:T(8,128)(2,1)S(1)} %get-tuple-element.145, bf16[864,1,2,1024]{3,0,2,1:T(8,128)(2,1)} %copy-done.9), kind=kOutput, calls=%fused_computation.33 | convolution fusion | flops 226492416 | bytes 4022272 | tf_op jit(solution)/shard_map/while/body/eval_jaxpr/kgzp,ogzp->ko/dot_general | solution.py:66
  78.8 1.3 fusion.47
  81.1 2.3 %convert_reduce_fusion = (f32[32]{0:T(128)S(1)}, bf16[32,4,4,1024]{3,2,1,0:T(4,128)(2,1)S(1)}) fusion(bf16[32,4,4,1024]{3,2,1,0:T(4,128)(2,1)S(1)} %copy-done.1, f32[32,4,1024]{2,1,0:T(4,128)S(1)} %mul.1101), kind=kLoop, calls=%fused_computation.17 | loop fusion | flops 6291424 | bytes 2621568 | tf_op jit(solution)/shard_map/reduce_sum | solution.py:280
  83.5 2.9 %fusion.71 = f32[1,36,32]{1,2,0:T(8,128)S(1)} fusion(bf16[4,4,36,1024]{3,2,1,0:T(8,128)(2,1)} %get-tuple-element.149, bf16[32,4,4,1024]{3,2,1,0:T(4,128)(2,1)S(1)} %get-tuple-element.143), kind=kOutput, calls=%fused_computation.52 | convolution fusion | flops 37748736 | bytes 2232832 | tf_op jit(solution)/shard_map/zpkq,ozpq->ko/dot_general | solution.py:227
  86.4 1.5 fusion.68
  87.9 1.5 fusion.65
  90.2 4.4 %collective-permute-start.10 = (f32[1120,128]{1,0:T(8,128)S(1)}, f32[1120,128]{1,0:T(8,128)S(1)}, u32[]{:S(2)}, u32[]{:S(2)}) collective-permute-start(f32[1120,128]{1,0:T(8,128)S(1)} %constant_dynamic-slice_fusion.2), channel_id=1, source_target_pairs={{0,8},{8,0},{16,24},{24,16},{32,40},{40,32},{48,56},{56,48},{64,72... | collective-permute-start | bytes 1720328 | tf_op jit(solution)/shard_map/ppermute | solution.py:327
  94.6 1.6 collective-permute-done.10
  97.2 7.2 %collective-permute-done.11 = f32[560,128]{1,0:T(8,128)S(1)} collective-permute-done((f32[560,128]{1,0:T(8,128)S(1)}, f32[560,128]{1,0:T(8,128)S(1)}, u32[]{:S(2)}, u32[]{:S(2)}) %collective-permute-start.11) | collective-permute-done | bytes 286752 | tf_op jit(solution)/shard_map/ppermute | solution.py:327
  104.5 2.5 %collective-permute-start.12 = (f32[280,128]{1,0:T(8,128)S(1)}, f32[280,128]{1,0:T(8,128)S(1)}, u32[]{:S(2)}, u32[]{:S(2)}) collective-permute-start(f32[280,128]{1,0:T(8,128)S(1)} %constant_dynamic-slice_fusion), channel_id=1, source_target_pairs={{0,32},{8,40},{16,48},{24,56},{32,0},{40,8},{48,16},{56,24},{64,96... | collective-permute-start | bytes 430088 | tf_op jit(solution)/shard_map/ppermute | solution.py:327
  107.0 3.0 %collective-permute-done.12 = f32[280,128]{1,0:T(8,128)S(1)} collective-permute-done((f32[280,128]{1,0:T(8,128)S(1)}, f32[280,128]{1,0:T(8,128)S(1)}, u32[]{:S(2)}, u32[]{:S(2)}) %collective-permute-start.12) | collective-permute-done | bytes 143392 | tf_op jit(solution)/shard_map/ppermute | solution.py:327
  110.8 3.2 %collective-permute-done.13 = f32[280,128]{1,0:T(8,128)S(1)} collective-permute-done((f32[280,128]{1,0:T(8,128)S(1)}, f32[280,128]{1,0:T(8,128)S(1)}, u32[]{:S(2)}, u32[]{:S(2)}) %collective-permute-start.13) | collective-permute-done | bytes 143392 | tf_op jit(solution)/shard_map/ppermute | solution.py:330
  114.1 2.3 %collective-permute-start.14 = (f32[280,128]{1,0:T(8,128)S(1)}, f32[280,128]{1,0:T(8,128)S(1)}, u32[]{:S(2)}, u32[]{:S(2)}) collective-permute-start(f32[280,128]{1,0:T(8,128)S(1)} %add.482), channel_id=1, source_target_pairs={{0,128},{8,136},{16,144},{24,152},{32,160},{40,168},{48,176},{56,1... | collective-permute-start | bytes 430088 | tf_op jit(solution)/shard_map/ppermute | solution.py:330
  116.4 3.7 %collective-permute-done.14 = f32[280,128]{1,0:T(8,128)S(1)} collective-permute-done((f32[280,128]{1,0:T(8,128)S(1)}, f32[280,128]{1,0:T(8,128)S(1)}, u32[]{:S(2)}, u32[]{:S(2)}) %collective-permute-start.14) | collective-permute-done | bytes 143392 | tf_op jit(solution)/shard_map/ppermute | solution.py:330
  120.1 3.4 %collective-permute-start.15 = (f32[280,128]{1,0:T(8,128)S(1)}, f32[280,128]{1,0:T(8,128)S(1)}, u32[]{:S(2)}, u32[]{:S(2)}) collective-permute-start(f32[280,128]{1,0:T(8,128)S(1)} %add.483), channel_id=1, source_target_pairs={{0,1},{1,0},{2,3},{3,2},{4,5},{5,4},{6,7},{7,6},{8,9},{9,8},{10,11... | collective-permute-start | bytes 430088 | tf_op jit(solution)/shard_map/ppermute | solution.py:330
  123.5 2.5 %collective-permute-done.15 = f32[280,128]{1,0:T(8,128)S(1)} collective-permute-done((f32[280,128]{1,0:T(8,128)S(1)}, f32[280,128]{1,0:T(8,128)S(1)}, u32[]{:S(2)}, u32[]{:S(2)}) %collective-permute-start.15) | collective-permute-done | bytes 143392 | tf_op jit(solution)/shard_map/ppermute | solution.py:330
  126.0 6.2 %collective-permute-start.16 = (f32[280,128]{1,0:T(8,128)S(1)}, f32[280,128]{1,0:T(8,128)S(1)}, u32[]{:S(2)}, u32[]{:S(2)}) collective-permute-start(f32[280,128]{1,0:T(8,128)S(1)} %add.484), channel_id=1, source_target_pairs={{0,2},{1,3},{2,0},{3,1},{4,6},{5,7},{6,4},{7,5},{8,10},{9,11},{10,... | collective-permute-start | bytes 430088 | tf_op jit(solution)/shard_map/ppermute | solution.py:330
  132.3 2.8 %collective-permute-done.16 = f32[280,128]{1,0:T(8,128)S(1)} collective-permute-done((f32[280,128]{1,0:T(8,128)S(1)}, f32[280,128]{1,0:T(8,128)S(1)}, u32[]{:S(2)}, u32[]{:S(2)}) %collective-permute-start.16) | collective-permute-done | bytes 143392 | tf_op jit(solution)/shard_map/ppermute | solution.py:330
  135.1 6.5 %collective-permute-start.17 = (f32[280,128]{1,0:T(8,128)S(1)}, f32[280,128]{1,0:T(8,128)S(1)}, u32[]{:S(2)}, u32[]{:S(2)}) collective-permute-start(f32[280,128]{1,0:T(8,128)S(1)} %add.485), channel_id=1, source_target_pairs={{0,4},{1,5},{2,6},{3,7},{4,0},{5,1},{6,2},{7,3},{8,12},{9,13},{10,... | collective-permute-start | bytes 430088 | tf_op jit(solution)/shard_map/ppermute | solution.py:330
  141.6 3.6 %collective-permute-done.17 = f32[280,128]{1,0:T(8,128)S(1)} collective-permute-done((f32[280,128]{1,0:T(8,128)S(1)}, f32[280,128]{1,0:T(8,128)S(1)}, u32[]{:S(2)}, u32[]{:S(2)}) %collective-permute-start.17) | collective-permute-done | bytes 143392 | tf_op jit(solution)/shard_map/ppermute | solution.py:330
  145.3 3.0 %collective-permute-start.18 = (f32[280,128]{1,0:T(8,128)S(1)}, f32[280,128]{1,0:T(8,128)S(1)}, u32[]{:S(2)}, u32[]{:S(2)}) collective-permute-start(f32[280,128]{1,0:T(8,128)S(1)} %add.486), channel_id=1, source_target_pairs={{0,32},{8,40},{16,48},{24,56},{32,0},{40,8},{48,16},{56,24},{64,96... | collective-permute-start | bytes 430088 | tf_op jit(solution)/shard_map/ppermute | solution.py:332
  148.3 2.6 %collective-permute-done.18 = f32[280,128]{1,0:T(8,128)S(1)} collective-permute-done((f32[280,128]{1,0:T(8,128)S(1)}, f32[280,128]{1,0:T(8,128)S(1)}, u32[]{:S(2)}, u32[]{:S(2)}) %collective-permute-start.18) | collective-permute-done | bytes 143392 | tf_op jit(solution)/shard_map/ppermute | solution.py:332
  150.9 1.4 collective-permute-start.19
  152.3 4.2 %collective-permute-done.19 = f32[560,128]{1,0:T(8,128)S(1)} collective-permute-done((f32[560,128]{1,0:T(8,128)S(1)}, f32[560,128]{1,0:T(8,128)S(1)}, u32[]{:S(2)}, u32[]{:S(2)}) %collective-permute-start.19) | collective-permute-done | bytes 286752 | tf_op jit(solution)/shard_map/ppermute | solution.py:332
  156.7 11.7 %collective-permute-start.20 = (f32[1120,128]{1,0:T(8,128)S(1)}, f32[1120,128]{1,0:T(8,128)S(1)}, u32[]{:S(2)}, u32[]{:S(2)}) collective-permute-start(f32[1120,128]{1,0:T(8,128)S(1)} %get-tuple-element.153), channel_id=1, source_target_pairs={{0,8},{8,0},{16,24},{24,16},{32,40},{40,32},{48,56},{56,48},{64,72... | collective-permute-start | bytes 1720328 | tf_op jit(solution)/shard_map/ppermute | solution.py:332
  173.5 1.0 pad_maximum_fusion
  (183 shorter events, 27.4 us)
Async XLA Ops:
  1.7 13.8 %collective-permute-start.1 = (bf16[4,1,1,4096]{3,2,1,0:T(2,128)(2,1)S(1)}, bf16[4,1,1,4096]{3,2,1,0:T(2,128)(2,1)S(1)}, u32[]{:S(2)}, u32[]{:S(2)}) collective-permute-start(bf16[4,1,1,4096]{3,2,1,0:T(2,128)(2,1)S(1)} %get-tuple-element.190), channel_id=1, source_target_pairs={{1,0},{2,1},{3,2},{4,3},{5,4},{6,5},{7,6},{9,8},{10,9},{11,10},{12... | collective-permute-start | bytes 98312 | tf_op jit(solution)/shard_map/ppermute | solution.py:22
  3.0 12.5 %collective-permute-start = (bf16[4,1,1,4096]{3,2,1,0:T(2,128)(2,1)S(1)}, bf16[4,1,1,4096]{3,2,1,0:T(2,128)(2,1)S(1)}, u32[]{:S(2)}, u32[]{:S(2)}) collective-permute-start(bf16[4,1,1,4096]{3,2,1,0:T(2,128)(2,1)S(1)} %get-tuple-element.189), channel_id=1, source_target_pairs={{0,1},{1,2},{2,3},{3,4},{4,5},{5,6},{6,7},{8,9},{9,10},{10,11},{11... | collective-permute-start | bytes 98312 | tf_op jit(solution)/shard_map/ppermute | solution.py:21
  26.3 5.5 %collective-permute-start.3 = (bf16[32,1,1,1024]{3,0,2,1:T(8,128)(2,1)S(1)}, bf16[32,1,1,1024]{3,0,2,1:T(8,128)(2,1)S(1)}, u32[]{:S(2)}, u32[]{:S(2)}) collective-permute-start(bf16[32,1,1,1024]{3,0,2,1:T(8,128)(2,1)S(1)} %get-tuple-element.188), channel_id=1, source_target_pairs={{1,0},{2,1},{3,2},{4,3},{5,4},{6,5},{7,6},{9,8},{10,9},{11,10},{12... | collective-permute-start | bytes 196616 | tf_op jit(solution)/shard_map/ppermute | solution.py:22
  27.6 5.5 %collective-permute-start.2 = (bf16[32,1,1,1024]{3,0,2,1:T(8,128)(2,1)S(1)}, bf16[32,1,1,1024]{3,0,2,1:T(8,128)(2,1)S(1)}, u32[]{:S(2)}, u32[]{:S(2)}) collective-permute-start(bf16[32,1,1,1024]{3,0,2,1:T(8,128)(2,1)S(1)} %get-tuple-element.187), channel_id=1, source_target_pairs={{0,1},{1,2},{2,3},{3,4},{4,5},{5,6},{6,7},{8,9},{9,10},{10,11},{11... | collective-permute-start | bytes 196616 | tf_op jit(solution)/shard_map/ppermute | solution.py:21
  33.3 2.5 %copy-start.7 = (bf16[27,32,64]{2,1,0:T(8,128)(2,1)S(1)}, bf16[27,32,64]{2,1,0:T(8,128)(2,1)}, u32[]{:S(2)}) copy-start(bf16[27,32,64]{2,1,0:T(8,128)(2,1)} %param.12) | copy-start | bytes 331780
  33.3 2.5 %copy-start.10 = (f32[64]{0:T(128)S(1)}, f32[64]{0:T(128)}, u32[]{:S(2)}) copy-start(f32[64]{0:T(128)} %param.13) | copy-start | bytes 772
  35.8 2.1 %copy-start.9 = (bf16[864,1,2,1024]{3,0,2,1:T(8,128)(2,1)}, bf16[864,1,2,1024]{3,0,2,1:T(8,128)(2,1)S(1)}, u32[]{:S(2)}) copy-start(bf16[864,1,2,1024]{3,0,2,1:T(8,128)(2,1)S(1)} %constant_dynamic-update-slice_fusion) | copy-start | bytes 10616836
  35.8 8.3 %copy-start = (bf16[6,4,36,1024]{3,2,1,0:T(8,128)(2,1)S(1)}, bf16[6,4,36,1024]{3,2,1,0:T(8,128)(2,1)}, u32[]{:S(2)}) copy-start(bf16[6,4,36,1024]{3,2,1,0:T(8,128)(2,1)} %get-tuple-element.83) | copy-start | bytes 5308420
  38.5 7.6 %collective-permute-start.5 = (bf16[64,1,1,256]{0,3,2,1:T(8,128)(2,1)S(1)}, bf16[64,1,1,256]{0,3,2,1:T(8,128)(2,1)S(1)}, u32[]{:S(2)}, u32[]{:S(2)}) collective-permute-start(bf16[64,1,1,256]{0,3,2,1:T(8,128)(2,1)S(1)} %fusion.138), channel_id=1, source_target_pairs={{1,0},{2,1},{3,2},{4,3},{5,4},{6,5},{7,6},{9,8},{10,9},{11,10},{12... | collective-permute-start | bytes 98312 | tf_op jit(solution)/shard_map/ppermute | solution.py:22
  39.8 6.3 %collective-permute-start.4 = (bf16[64,1,1,256]{0,3,2,1:T(8,128)(2,1)S(1)}, bf16[64,1,1,256]{0,3,2,1:T(8,128)(2,1)S(1)}, u32[]{:S(2)}, u32[]{:S(2)}) collective-permute-start(bf16[64,1,1,256]{0,3,2,1:T(8,128)(2,1)S(1)} %fusion.138), channel_id=1, source_target_pairs={{0,1},{1,2},{2,3},{3,4},{4,5},{5,6},{6,7},{8,9},{9,10},{10,11},{11... | collective-permute-start | bytes 98312 | tf_op jit(solution)/shard_map/ppermute | solution.py:21
  46.2 4.6 %copy-start.6 = (bf16[27,64,128]{2,1,0:T(8,128)(2,1)S(1)}, bf16[27,64,128]{2,1,0:T(8,128)(2,1)}, u32[]{:S(2)}) copy-start(bf16[27,64,128]{2,1,0:T(8,128)(2,1)} %param.14) | copy-start | bytes 1327108
  46.2 4.6 %copy-start.11 = (f32[128]{0:T(128)S(1)}, f32[128]{0:T(128)}, u32[]{:S(2)}) copy-start(f32[128]{0:T(128)} %param.15) | copy-start | bytes 1540
  52.7 7.2 %collective-permute-start.7 = (bf16[128,1,1,256]{0,3,2,1:T(8,128)(2,1)S(1)}, bf16[128,1,1,256]{0,3,2,1:T(8,128)(2,1)S(1)}, u32[]{:S(2)}, u32[]{:S(2)}) collective-permute-start(bf16[128,1,1,256]{0,3,2,1:T(8,128)(2,1)S(1)} %get-tuple-element.147), channel_id=1, source_target_pairs={{1,0},{2,1},{3,2},{4,3},{5,4},{6,5},{7,6},{9,8},{10,9},{11,10},{12... | collective-permute-start | bytes 196616 | tf_op jit(solution)/shard_map/ppermute | solution.py:22
  54.0 6.6 %collective-permute-start.6 = (bf16[128,1,1,256]{0,3,2,1:T(8,128)(2,1)S(1)}, bf16[128,1,1,256]{0,3,2,1:T(8,128)(2,1)S(1)}, u32[]{:S(2)}, u32[]{:S(2)}) collective-permute-start(bf16[128,1,1,256]{0,3,2,1:T(8,128)(2,1)S(1)} %get-tuple-element.147), channel_id=1, source_target_pairs={{0,1},{1,2},{2,3},{3,4},{4,5},{5,6},{6,7},{8,9},{9,10},{10,11},{11... | collective-permute-start | bytes 196616 | tf_op jit(solution)/shard_map/ppermute | solution.py:21
  60.9 3.4 %copy-start.5 = (f32[64,2,1024]{2,0,1:T(8,128)S(1)}, f32[64,2,1024]{2,0,1:T(8,128)}, u32[]{:S(2)}) copy-start(f32[64,2,1024]{2,0,1:T(8,128)} %get-tuple-element.192) | copy-start | bytes 1572868
  64.6 10.4 %collective-permute-start.9 = (bf16[64,1,1,1024]{3,0,2,1:T(8,128)(2,1)S(1)}, bf16[64,1,1,1024]{3,0,2,1:T(8,128)(2,1)S(1)}, u32[]{:S(2)}, u32[]{:S(2)}) collective-permute-start(bf16[64,1,1,1024]{3,0,2,1:T(8,128)(2,1)S(1)} %get-tuple-element.162), channel_id=1, source_target_pairs={{1,0},{2,1},{3,2},{4,3},{5,4},{6,5},{7,6},{9,8},{10,9},{11,10},{12... | collective-permute-start | bytes 393224 | tf_op jit(solution)/shard_map/ppermute | solution.py:22
  65.9 9.1 %collective-permute-start.8 = (bf16[64,1,1,1024]{3,0,2,1:T(8,128)(2,1)S(1)}, bf16[64,1,1,1024]{3,0,2,1:T(8,128)(2,1)S(1)}, u32[]{:S(2)}, u32[]{:S(2)}) collective-permute-start(bf16[64,1,1,1024]{3,0,2,1:T(8,128)(2,1)S(1)} %get-tuple-element.161), channel_id=1, source_target_pairs={{0,1},{1,2},{2,3},{3,4},{4,5},{5,6},{6,7},{8,9},{9,10},{10,11},{11... | collective-permute-start | bytes 393224 | tf_op jit(solution)/shard_map/ppermute | solution.py:21
  78.8 2.4 %copy-start.1 = (bf16[32,4,4,1024]{3,2,1,0:T(4,128)(2,1)S(1)}, bf16[32,4,4,1024]{3,2,1,0:T(4,128)(2,1)}, u32[]{:S(2)}) copy-start(bf16[32,4,4,1024]{3,2,1,0:T(4,128)(2,1)} %get-tuple-element.82) | copy-start | bytes 3145732
  81.1 5.3 %copy-start.3 = (bf16[4,4,36,1024]{3,2,1,0:T(8,128)(2,1)S(1)}, bf16[4,4,36,1024]{3,2,1,0:T(8,128)(2,1)}, u32[]{:S(2)}) copy-start(bf16[4,4,36,1024]{3,2,1,0:T(8,128)(2,1)} %get-tuple-element.150) | copy-start | bytes 3538948
  83.5 4.4 %copy-start.2 = (bf16[4,4,36,1024]{3,2,1,0:T(8,128)(2,1)S(1)}, bf16[4,4,36,1024]{3,2,1,0:T(8,128)(2,1)}, u32[]{:S(2)}) copy-start(bf16[4,4,36,1024]{3,2,1,0:T(8,128)(2,1)} %get-tuple-element.148) | copy-start | bytes 3538948
  86.4 3.3 %copy-start.4 = (f32[432,128]{1,0:T(8,128)S(1)}, f32[432,128]{1,0:T(8,128)}, u32[]{:S(2)}) copy-start(f32[432,128]{1,0:T(8,128)} %reshape.391) | copy-start | bytes 663556
  90.2 6.0 %collective-permute-start.10 = (f32[1120,128]{1,0:T(8,128)S(1)}, f32[1120,128]{1,0:T(8,128)S(1)}, u32[]{:S(2)}, u32[]{:S(2)}) collective-permute-start(f32[1120,128]{1,0:T(8,128)S(1)} %constant_dynamic-slice_fusion.2), channel_id=1, source_target_pairs={{0,8},{8,0},{16,24},{24,16},{32,40},{40,32},{48,56},{56,48},{64,72... | collective-permute-start | bytes 1720328 | tf_op jit(solution)/shard_map/ppermute | solution.py:327
  96.3 8.1 %collective-permute-start.11 = (f32[560,128]{1,0:T(8,128)S(1)}, f32[560,128]{1,0:T(8,128)S(1)}, u32[]{:S(2)}, u32[]{:S(2)}) collective-permute-start(f32[560,128]{1,0:T(8,128)S(1)} %constant_dynamic-slice_fusion.1), channel_id=1, source_target_pairs={{0,16},{8,24},{16,0},{24,8},{32,48},{40,56},{48,32},{56,40},{64,80... | collective-permute-start | bytes 860168 | tf_op jit(solution)/shard_map/ppermute | solution.py:327
  104.5 64.0 %copy-start.8 = (f32[128,256]{0,1:T(8,128)S(1)}, f32[128,256]{0,1:T(8,128)}, u32[]{:S(2)}) copy-start(f32[128,256]{0,1:T(8,128)} %get-tuple-element.193) | copy-start | bytes 393220
  104.5 5.5 %collective-permute-start.12 = (f32[280,128]{1,0:T(8,128)S(1)}, f32[280,128]{1,0:T(8,128)S(1)}, u32[]{:S(2)}, u32[]{:S(2)}) collective-permute-start(f32[280,128]{1,0:T(8,128)S(1)} %constant_dynamic-slice_fusion), channel_id=1, source_target_pairs={{0,32},{8,40},{16,48},{24,56},{32,0},{40,8},{48,16},{56,24},{64,96... | collective-permute-start | bytes 430088 | tf_op jit(solution)/shard_map/ppermute | solution.py:327
  110.0 4.0 %collective-permute-start.13 = (f32[280,128]{1,0:T(8,128)S(1)}, f32[280,128]{1,0:T(8,128)S(1)}, u32[]{:S(2)}, u32[]{:S(2)}) collective-permute-start(f32[280,128]{1,0:T(8,128)S(1)} %dynamic-slice_add_fusion.2), channel_id=1, source_target_pairs={{0,64},{8,72},{16,80},{24,88},{32,96},{40,104},{48,112},{56,120},{... | collective-permute-start | bytes 430088 | tf_op jit(solution)/shard_map/ppermute | solution.py:330
  114.1 6.0 %collective-permute-start.14 = (f32[280,128]{1,0:T(8,128)S(1)}, f32[280,128]{1,0:T(8,128)S(1)}, u32[]{:S(2)}, u32[]{:S(2)}) collective-permute-start(f32[280,128]{1,0:T(8,128)S(1)} %add.482), channel_id=1, source_target_pairs={{0,128},{8,136},{16,144},{24,152},{32,160},{40,168},{48,176},{56,1... | collective-permute-start | bytes 430088 | tf_op jit(solution)/shard_map/ppermute | solution.py:330
  120.1 5.9 %collective-permute-start.15 = (f32[280,128]{1,0:T(8,128)S(1)}, f32[280,128]{1,0:T(8,128)S(1)}, u32[]{:S(2)}, u32[]{:S(2)}) collective-permute-start(f32[280,128]{1,0:T(8,128)S(1)} %add.483), channel_id=1, source_target_pairs={{0,1},{1,0},{2,3},{3,2},{4,5},{5,4},{6,7},{7,6},{8,9},{9,8},{10,11... | collective-permute-start | bytes 430088 | tf_op jit(solution)/shard_map/ppermute | solution.py:330
  126.0 9.1 %collective-permute-start.16 = (f32[280,128]{1,0:T(8,128)S(1)}, f32[280,128]{1,0:T(8,128)S(1)}, u32[]{:S(2)}, u32[]{:S(2)}) collective-permute-start(f32[280,128]{1,0:T(8,128)S(1)} %add.484), channel_id=1, source_target_pairs={{0,2},{1,3},{2,0},{3,1},{4,6},{5,7},{6,4},{7,5},{8,10},{9,11},{10,... | collective-permute-start | bytes 430088 | tf_op jit(solution)/shard_map/ppermute | solution.py:330
  135.1 10.2 %collective-permute-start.17 = (f32[280,128]{1,0:T(8,128)S(1)}, f32[280,128]{1,0:T(8,128)S(1)}, u32[]{:S(2)}, u32[]{:S(2)}) collective-permute-start(f32[280,128]{1,0:T(8,128)S(1)} %add.485), channel_id=1, source_target_pairs={{0,4},{1,5},{2,6},{3,7},{4,0},{5,1},{6,2},{7,3},{8,12},{9,13},{10,... | collective-permute-start | bytes 430088 | tf_op jit(solution)/shard_map/ppermute | solution.py:330
  145.3 5.5 %collective-permute-start.18 = (f32[280,128]{1,0:T(8,128)S(1)}, f32[280,128]{1,0:T(8,128)S(1)}, u32[]{:S(2)}, u32[]{:S(2)}) collective-permute-start(f32[280,128]{1,0:T(8,128)S(1)} %add.486), channel_id=1, source_target_pairs={{0,32},{8,40},{16,48},{24,56},{32,0},{40,8},{48,16},{56,24},{64,96... | collective-permute-start | bytes 430088 | tf_op jit(solution)/shard_map/ppermute | solution.py:332
  150.9 5.6 %collective-permute-start.19 = (f32[560,128]{1,0:T(8,128)S(1)}, f32[560,128]{1,0:T(8,128)S(1)}, u32[]{:S(2)}, u32[]{:S(2)}) collective-permute-start(f32[560,128]{1,0:T(8,128)S(1)} %get-tuple-element.157), channel_id=1, source_target_pairs={{0,16},{8,24},{16,0},{24,8},{32,48},{40,56},{48,32},{56,40},{64,80... | collective-permute-start | bytes 860168 | tf_op jit(solution)/shard_map/ppermute | solution.py:332
  156.7 13.3 %collective-permute-start.20 = (f32[1120,128]{1,0:T(8,128)S(1)}, f32[1120,128]{1,0:T(8,128)S(1)}, u32[]{:S(2)}, u32[]{:S(2)}) collective-permute-start(f32[1120,128]{1,0:T(8,128)S(1)} %get-tuple-element.153), channel_id=1, source_target_pairs={{0,8},{8,0},{16,24},{24,16},{32,40},{40,32},{48,56},{56,48},{64,72... | collective-permute-start | bytes 1720328 | tf_op jit(solution)/shard_map/ppermute | solution.py:332

commit v6 on v5

--- a/solution.py
+++ b/solution.py
@@ -297,7 +297,7 @@
     return [(i, i ^ mask) for i in range(lax.axis_size(axis))]
 
 
-def all_reduce_rows(grads, halving_steps=3, lanes=128):
+def all_reduce_rows(grads, halving_steps=5, lanes=128):
     steps = []
     for axis in ("sample", "slab"):
         mask = 1

time: 176 us -> 175 us (level)
    ppermute x5 -> x3, waiting for transfers between devices: 15.9 us -> 4.14 us  [all_reduce_rows(): buffer = buffer + lax.ppermute(buffer, axis, xor_pairs(axis, mask))]
    ppermute x3 -> x5, waiting for transfers between devices: 11.9 us -> 17.1 us  [all_reduce_rows(): buffer = keep + lax.ppermute(send, axis, xor_pairs(axis, mask))]
    ppermute x3 -> x5, waiting for transfers between devices: 7.55 us -> 12.4 us  [all_reduce_rows(): other = lax.ppermute(buffer, axis, xor_pairs(axis, mask))]
    ppermute x5 -> x3, starting transfers between devices: 19.2 us -> 14.7 us  [all_reduce_rows(): buffer = buffer + lax.ppermute(buffer, axis, xor_pairs(axis, mask))]
    ppermute x3 -> x5, starting transfers between devices: 7.79 us -> 10.9 us  [all_reduce_rows(): buffer = keep + lax.ppermute(send, axis, xor_pairs(axis, mask))]
    ppermute x3 -> x5, starting transfers between devices: 16.1 us -> 19.2 us  [all_reduce_rows(): other = lax.ppermute(buffer, axis, xor_pairs(axis, mask))]
  transfers between devices with their start and end apart: 21 -> 23, of which waited for: 13 -> 15; matrix products, arithmetic and copies ran while one was open for 8% -> 8% of each run, Pallas kernels for 0% -> 0%
where the time goes in v6:
time: 175 us
  starting transfers between devices  75.4 us (43%)
  waiting for transfers between devices  35.6 us (20%)
  local copies, waits for them, and re-layouts  23.6 us (13%)
  other arithmetic  18.7 us (11%)
  matrix products  15 us (9%)
  Pallas kernels  4.47 us (3%)
  between operations  1.88 us (1%)
    ppermute x5, starting transfers between devices, with_halo(): before = lax.ppermute(last, axis, up)  24.1 us
    ppermute x5, starting transfers between devices, all_reduce_rows(): other = lax.ppermute(buffer, axis, xor_pairs(axis, mask))  19.2 us
    ppermute x5, waiting for transfers between devices, all_reduce_rows(): buffer = keep + lax.ppermute(send, axis, xor_pairs(axis, mask))  17.1 us
    ppermute x3, starting transfers between devices, all_reduce_rows(): buffer = buffer + lax.ppermute(buffer, axis, xor_pairs(axis, mask))  14.7 us
    ppermute x5, waiting for transfers between devices, all_reduce_rows(): other = lax.ppermute(buffer, axis, xor_pairs(axis, mask))  12.4 us
    ppermute x5, starting transfers between devices, all_reduce_rows(): buffer = keep + lax.ppermute(send, axis, xor_pairs(axis, mask))  10.9 us
    ppermute x5, starting transfers between devices, with_halo(): after = lax.ppermute(first, axis, down)  6.45 us
    dot_general x3, matrix products, parity_weight_grad(): jnp.einsum('zpkq,ozpq->ko', shifted[dz:dz + depth_len], delta, preferred_...  5.94 us
  transfers between devices with their start and end apart: 23, of which 15 were waited for; matrix products, arithmetic and copies ran while one was open for 8% of the time, Pallas kernels for 0%

profile of v6, /device:TPU:1, one launch (start us, length us, event | category | flops | bytes accessed | tf_op | source)
XLA Modules:
  0.0 174.6 jit_solution(12150460160997991118)
XLA Ops:
  1.7 1.3 collective-permute-start.1
  3.0 5.0 %collective-permute-start = (bf16[4,1,1,4096]{3,2,1,0:T(2,128)(2,1)S(1)}, bf16[4,1,1,4096]{3,2,1,0:T(2,128)(2,1)S(1)}, u32[]{:S(2)}, u32[]{:S(2)}) collective-permute-start(bf16[4,1,1,4096]{3,2,1,0:T(2,128)(2,1)S(1)} %get-tuple-element.193), channel_id=1, source_target_pairs={{0,1},{1,2},{2,3},{3,4},{4,5},{5,6},{6,7},{8,9},{9,10},{10,11},{11... | collective-permute-start | bytes 98312 | tf_op jit(solution)/shard_map/ppermute | solution.py:21
  10.8 1.6 copy.94
  13.8 1.3 copy.90.b_ref
  15.5 1.1 maximum_bitcast_fusion
  17.6 4.5 %shard_map.135 = (bf16[32,4,4,1024]{3,2,1,0:T(4,128)(2,1)}, bf16[6,4,36,1024]{3,2,1,0:T(8,128)(2,1)}) custom-call(bf16[24,4096]{1,0:T(8,128)(2,1)} %reshape.381.src_ref, bf16[128,128]{1,0:T(8,128)(2,1)} %fusion.145.perm_ref, bf16[3,32,36]{2,1,0:T(8,128)(2,1)} %bitcast.181, f32[32,1]{1,0:T(8,128)} %copy.90.b_ref), custom_call_target="tpu_custom_call" | custom-call | tf_op jit(solution)/shard_map/pallas_call | solution.py:214
  22.0 4.0 %fusion.9 = f32[32,4,1024]{2,1,0:T(4,128)S(1)} fusion(bf16[32,4,4,1024]{3,2,1,0:T(4,128)(2,1)} %get-tuple-element.82), kind=kLoop, calls=%fused_computation.12 | loop fusion | flops 3014656 | bytes 1572864 | tf_op jit(solution)/shard_map/reduce_sum | solution.py:152
  26.3 1.3 collective-permute-start.3
  27.6 4.2 %collective-permute-start.2 = (bf16[32,1,1,1024]{3,0,2,1:T(8,128)(2,1)S(1)}, bf16[32,1,1,1024]{3,0,2,1:T(8,128)(2,1)S(1)}, u32[]{:S(2)}, u32[]{:S(2)}) collective-permute-start(bf16[32,1,1,1024]{3,0,2,1:T(8,128)(2,1)S(1)} %get-tuple-element.191), channel_id=1, source_target_pairs={{0,1},{1,2},{2,3},{3,4},{4,5},{5,6},{6,7},{8,9},{9,10},{10,11},{11... | collective-permute-start | bytes 196616 | tf_op jit(solution)/shard_map/ppermute | solution.py:21
  31.8 1.3 collective-permute-done.2
  35.9 1.6 multiply_reduce_fusion
  38.6 1.3 collective-permute-start.5
  39.9 4.3 %collective-permute-start.4 = (bf16[64,1,1,256]{0,3,2,1:T(8,128)(2,1)S(1)}, bf16[64,1,1,256]{0,3,2,1:T(8,128)(2,1)S(1)}, u32[]{:S(2)}, u32[]{:S(2)}) collective-permute-start(bf16[64,1,1,256]{0,3,2,1:T(8,128)(2,1)S(1)} %fusion.142), channel_id=1, source_target_pairs={{0,1},{1,2},{2,3},{3,4},{4,5},{5,6},{6,7},{8,9},{9,10},{10,11},{11... | collective-permute-start | bytes 98312 | tf_op jit(solution)/shard_map/ppermute | solution.py:21
  44.2 2.0 %fusion.165 = (bf16[4,4,36,1024]{3,2,1,0:T(8,128)(2,1)}, bf16[4,4,36,1024]{3,2,1,0:T(8,128)(2,1)}, bf16[4,4,36,1024]{3,2,1,0:T(8,128)(2,1)}) fusion(bf16[6,4,36,1024]{3,2,1,0:T(8,128)(2,1)S(1)} %copy-done), kind=kLoop, calls=%fused_computation.358 | loop fusion | bytes 7077888 | tf_op jit(solution)/shard_map/slice | solution.py:228
  47.2 3.6 %concatenate.71 = bf16[1728,1,1,256]{0,3,2,1:T(8,128)(2,1)S(1)} concatenate(bf16[64,1,1,256]{0,3,2,1:T(8,128)(2,1)S(1)} %get-tuple-element.180, bf16[64,1,1,256]{0,3,2,1:T(8,128)(2,1)} %get-tuple-element.186, bf16[64,1,1,256]{0,3,2,1:T(8,128)(2,1)S(1)} %get-tuple-element.171, bf16[64,1,1,256]{0,3,2,1:T(8,128)(2,1)S(1)} %get-tuple-element.179, ...), dimensions={0} | concatenate | bytes 1769472 | tf_op jit(solution)/shard_map/while/body/eval_jaxpr/concatenate | solution.py:57
  50.8 1.9 %convert_reduce_fusion.2 = (f32[128]{0:T(128)S(1)}, bf16[128,1,1,256]{0,3,2,1:T(8,128)(2,1)S(1)}, f32[128,256]{0,1:T(8,128)}) fusion(bf16[128,1,1,256]{0,3,2,1:T(8,128)(2,1)} %copy.94, f32[128]{0:T(128)S(1)} %copy-done.11, bf16[1728,128]{1,0:T(8,128)(2,1)S(1)} %bitcast.176, bf16[1728,1,1,256]{0,3,2,1:T(8,128)(2,1)S(1)} %concatenate.71), kind=kOutput, calls=%fused_computation.253 | convolution fusion | flops 113737600 | bytes 1590272 | tf_op jit(solution)/shard_map/while/body/eval_jaxpr/ko,kgzp->ogzp/dot_general | solution.py:62
  52.7 1.3 collective-permute-start.7
  54.0 5.4 %collective-permute-start.6 = (bf16[128,1,1,256]{0,3,2,1:T(8,128)(2,1)S(1)}, bf16[128,1,1,256]{0,3,2,1:T(8,128)(2,1)S(1)}, u32[]{:S(2)}, u32[]{:S(2)}) collective-permute-start(bf16[128,1,1,256]{0,3,2,1:T(8,128)(2,1)S(1)} %get-tuple-element.147), channel_id=1, source_target_pairs={{0,1},{1,2},{2,3},{3,4},{4,5},{5,6},{6,7},{8,9},{9,10},{10,11},{11... | collective-permute-start | bytes 196616 | tf_op jit(solution)/shard_map/ppermute | solution.py:21
  64.6 1.3 collective-permute-start.9
  65.9 5.2 %collective-permute-start.8 = (bf16[64,1,1,1024]{3,0,2,1:T(8,128)(2,1)S(1)}, bf16[64,1,1,1024]{3,0,2,1:T(8,128)(2,1)S(1)}, u32[]{:S(2)}, u32[]{:S(2)}) collective-permute-start(bf16[64,1,1,1024]{3,0,2,1:T(8,128)(2,1)S(1)} %get-tuple-element.161), channel_id=1, source_target_pairs={{0,1},{1,2},{2,3},{3,4},{4,5},{5,6},{6,7},{8,9},{9,10},{10,11},{11... | collective-permute-start | bytes 393224 | tf_op jit(solution)/shard_map/ppermute | solution.py:21
  71.1 3.1 %fusion.25 = f32[864,64]{1,0:T(8,128)S(1)} fusion(bf16[64,2,1024]{2,0,1:T(8,128)(2,1)S(1)} %get-tuple-element.145, bf16[864,1,2,1024]{3,0,2,1:T(8,128)(2,1)} %copy-done.9), kind=kOutput, calls=%fused_computation.33 | convolution fusion | flops 226492416 | bytes 4022272 | tf_op jit(solution)/shard_map/while/body/eval_jaxpr/kgzp,ogzp->ko/dot_general | solution.py:66
  78.8 1.3 fusion.47
  81.1 2.3 %convert_reduce_fusion = (f32[32]{0:T(128)S(1)}, bf16[32,4,4,1024]{3,2,1,0:T(4,128)(2,1)S(1)}) fusion(bf16[32,4,4,1024]{3,2,1,0:T(4,128)(2,1)S(1)} %copy-done.1, f32[32,4,1024]{2,1,0:T(4,128)S(1)} %mul.1113), kind=kLoop, calls=%fused_computation.17 | loop fusion | flops 6291424 | bytes 2621568 | tf_op jit(solution)/shard_map/reduce_sum | solution.py:280
  83.5 2.9 %fusion.71 = f32[1,36,32]{1,2,0:T(8,128)S(1)} fusion(bf16[4,4,36,1024]{3,2,1,0:T(8,128)(2,1)} %get-tuple-element.149, bf16[32,4,4,1024]{3,2,1,0:T(4,128)(2,1)S(1)} %get-tuple-element.143), kind=kOutput, calls=%fused_computation.52 | convolution fusion | flops 37748736 | bytes 2232832 | tf_op jit(solution)/shard_map/zpkq,ozpq->ko/dot_general | solution.py:227
  86.4 1.5 fusion.68
  87.9 1.5 fusion.65
  90.2 4.4 %collective-permute-start.10 = (f32[1152,128]{1,0:T(8,128)S(1)}, f32[1152,128]{1,0:T(8,128)S(1)}, u32[]{:S(2)}, u32[]{:S(2)}) collective-permute-start(f32[1152,128]{1,0:T(8,128)S(1)} %constant_dynamic-slice_fusion.4), channel_id=1, source_target_pairs={{0,8},{8,0},{16,24},{24,16},{32,40},{40,32},{48,56},{56,48},{64,72... | collective-permute-start | bytes 1769480 | tf_op jit(solution)/shard_map/ppermute | solution.py:327
  94.6 1.6 collective-permute-done.10
  97.3 7.4 %collective-permute-done.11 = f32[576,128]{1,0:T(8,128)S(1)} collective-permute-done((f32[576,128]{1,0:T(8,128)S(1)}, f32[576,128]{1,0:T(8,128)S(1)}, u32[]{:S(2)}, u32[]{:S(2)}) %collective-permute-start.11) | collective-permute-done | bytes 294944 | tf_op jit(solution)/shard_map/ppermute | solution.py:327
  104.8 2.5 %collective-permute-start.12 = (f32[288,128]{1,0:T(8,128)S(1)}, f32[288,128]{1,0:T(8,128)S(1)}, u32[]{:S(2)}, u32[]{:S(2)}) collective-permute-start(f32[288,128]{1,0:T(8,128)S(1)} %constant_dynamic-slice_fusion.2), channel_id=1, source_target_pairs={{0,32},{8,40},{16,48},{24,56},{32,0},{40,8},{48,16},{56,24},{64,96... | collective-permute-start | bytes 442376 | tf_op jit(solution)/shard_map/ppermute | solution.py:327
  107.3 3.1 %collective-permute-done.12 = f32[288,128]{1,0:T(8,128)S(1)} collective-permute-done((f32[288,128]{1,0:T(8,128)S(1)}, f32[288,128]{1,0:T(8,128)S(1)}, u32[]{:S(2)}, u32[]{:S(2)}) %collective-permute-start.12) | collective-permute-done | bytes 147488 | tf_op jit(solution)/shard_map/ppermute | solution.py:327
  111.2 2.5 %collective-permute-done.13 = f32[144,128]{1,0:T(8,128)S(1)} collective-permute-done((f32[144,128]{1,0:T(8,128)S(1)}, f32[144,128]{1,0:T(8,128)S(1)}, u32[]{:S(2)}, u32[]{:S(2)}) %collective-permute-start.13) | collective-permute-done | bytes 73760 | tf_op jit(solution)/shard_map/ppermute | solution.py:327
  113.7 2.3 %collective-permute-start.14 = (f32[72,128]{1,0:T(8,128)S(1)}, f32[72,128]{1,0:T(8,128)S(1)}, u32[]{:S(2)}, u32[]{:S(2)}) collective-permute-start(f32[72,128]{1,0:T(8,128)S(1)} %constant_dynamic-slice_fusion), channel_id=1, source_target_pairs={{0,128},{8,136},{16,144},{24,152},{32,160},{40,168},{48,176},{56,1... | collective-permute-start | bytes 110600 | tf_op jit(solution)/shard_map/ppermute | solution.py:327
  116.1 2.5 %collective-permute-done.14 = f32[72,128]{1,0:T(8,128)S(1)} collective-permute-done((f32[72,128]{1,0:T(8,128)S(1)}, f32[72,128]{1,0:T(8,128)S(1)}, u32[]{:S(2)}, u32[]{:S(2)}) %collective-permute-start.14) | collective-permute-done | bytes 36896 | tf_op jit(solution)/shard_map/ppermute | solution.py:327
  118.5 2.6 %collective-permute-start.15 = (f32[72,128]{1,0:T(8,128)S(1)}, f32[72,128]{1,0:T(8,128)S(1)}, u32[]{:S(2)}, u32[]{:S(2)}) collective-permute-start(f32[72,128]{1,0:T(8,128)S(1)} %dynamic-slice_add_fusion.4), channel_id=1, source_target_pairs={{0,1},{1,0},{2,3},{3,2},{4,5},{5,4},{6,7},{7,6},{8,9},{9,8},{10,11... | collective-permute-start | bytes 110600 | tf_op jit(solution)/shard_map/ppermute | solution.py:330
  121.2 1.3 collective-permute-done.15
  122.5 6.1 %collective-permute-start.16 = (f32[72,128]{1,0:T(8,128)S(1)}, f32[72,128]{1,0:T(8,128)S(1)}, u32[]{:S(2)}, u32[]{:S(2)}) collective-permute-start(f32[72,128]{1,0:T(8,128)S(1)} %add.526), channel_id=1, source_target_pairs={{0,2},{1,3},{2,0},{3,1},{4,6},{5,7},{6,4},{7,5},{8,10},{9,11},{10,... | collective-permute-start | bytes 110600 | tf_op jit(solution)/shard_map/ppermute | solution.py:330
  128.7 1.3 collective-permute-done.16
  130.0 5.9 %collective-permute-start.17 = (f32[72,128]{1,0:T(8,128)S(1)}, f32[72,128]{1,0:T(8,128)S(1)}, u32[]{:S(2)}, u32[]{:S(2)}) collective-permute-start(f32[72,128]{1,0:T(8,128)S(1)} %add.527), channel_id=1, source_target_pairs={{0,4},{1,5},{2,6},{3,7},{4,0},{5,1},{6,2},{7,3},{8,12},{9,13},{10,... | collective-permute-start | bytes 110600 | tf_op jit(solution)/shard_map/ppermute | solution.py:330
  135.9 1.4 collective-permute-done.17
  137.4 2.2 %collective-permute-start.18 = (f32[72,128]{1,0:T(8,128)S(1)}, f32[72,128]{1,0:T(8,128)S(1)}, u32[]{:S(2)}, u32[]{:S(2)}) collective-permute-start(f32[72,128]{1,0:T(8,128)S(1)} %add.528), channel_id=1, source_target_pairs={{0,128},{8,136},{16,144},{24,152},{32,160},{40,168},{48,176},{56,1... | collective-permute-start | bytes 110600 | tf_op jit(solution)/shard_map/ppermute | solution.py:332
  139.6 2.1 %collective-permute-done.18 = f32[72,128]{1,0:T(8,128)S(1)} collective-permute-done((f32[72,128]{1,0:T(8,128)S(1)}, f32[72,128]{1,0:T(8,128)S(1)}, u32[]{:S(2)}, u32[]{:S(2)}) %collective-permute-start.18) | collective-permute-done | bytes 36896 | tf_op jit(solution)/shard_map/ppermute | solution.py:332
  142.5 2.6 %collective-permute-done.19 = f32[144,128]{1,0:T(8,128)S(1)} collective-permute-done((f32[144,128]{1,0:T(8,128)S(1)}, f32[144,128]{1,0:T(8,128)S(1)}, u32[]{:S(2)}, u32[]{:S(2)}) %collective-permute-start.19) | collective-permute-done | bytes 73760 | tf_op jit(solution)/shard_map/ppermute | solution.py:332
  145.1 3.0 %collective-permute-start.20 = (f32[288,128]{1,0:T(8,128)S(1)}, f32[288,128]{1,0:T(8,128)S(1)}, u32[]{:S(2)}, u32[]{:S(2)}) collective-permute-start(f32[288,128]{1,0:T(8,128)S(1)} %get-tuple-element.187), channel_id=1, source_target_pairs={{0,32},{8,40},{16,48},{24,56},{32,0},{40,8},{48,16},{56,24},{64,96... | collective-permute-start | bytes 442376 | tf_op jit(solution)/shard_map/ppermute | solution.py:332
  148.1 2.6 %collective-permute-done.20 = f32[288,128]{1,0:T(8,128)S(1)} collective-permute-done((f32[288,128]{1,0:T(8,128)S(1)}, f32[288,128]{1,0:T(8,128)S(1)}, u32[]{:S(2)}, u32[]{:S(2)}) %collective-permute-start.20) | collective-permute-done | bytes 147488 | tf_op jit(solution)/shard_map/ppermute | solution.py:332
  150.8 1.4 collective-permute-start.21
  152.2 4.3 %collective-permute-done.21 = f32[576,128]{1,0:T(8,128)S(1)} collective-permute-done((f32[576,128]{1,0:T(8,128)S(1)}, f32[576,128]{1,0:T(8,128)S(1)}, u32[]{:S(2)}, u32[]{:S(2)}) %collective-permute-start.21) | collective-permute-done | bytes 294944 | tf_op jit(solution)/shard_map/ppermute | solution.py:332
  156.7 11.9 %collective-permute-start.22 = (f32[1152,128]{1,0:T(8,128)S(1)}, f32[1152,128]{1,0:T(8,128)S(1)}, u32[]{:S(2)}, u32[]{:S(2)}) collective-permute-start(f32[1152,128]{1,0:T(8,128)S(1)} %get-tuple-element.153), channel_id=1, source_target_pairs={{0,8},{8,0},{16,24},{24,16},{32,40},{40,32},{48,56},{56,48},{64,72... | collective-permute-start | bytes 1769480 | tf_op jit(solution)/shard_map/ppermute | solution.py:332
  (193 shorter events, 31.4 us)
Async XLA Ops:
  1.7 13.8 %collective-permute-start.1 = (bf16[4,1,1,4096]{3,2,1,0:T(2,128)(2,1)S(1)}, bf16[4,1,1,4096]{3,2,1,0:T(2,128)(2,1)S(1)}, u32[]{:S(2)}, u32[]{:S(2)}) collective-permute-start(bf16[4,1,1,4096]{3,2,1,0:T(2,128)(2,1)S(1)} %get-tuple-element.194), channel_id=1, source_target_pairs={{1,0},{2,1},{3,2},{4,3},{5,4},{6,5},{7,6},{9,8},{10,9},{11,10},{12... | collective-permute-start | bytes 98312 | tf_op jit(solution)/shard_map/ppermute | solution.py:22
  3.0 12.5 %collective-permute-start = (bf16[4,1,1,4096]{3,2,1,0:T(2,128)(2,1)S(1)}, bf16[4,1,1,4096]{3,2,1,0:T(2,128)(2,1)S(1)}, u32[]{:S(2)}, u32[]{:S(2)}) collective-permute-start(bf16[4,1,1,4096]{3,2,1,0:T(2,128)(2,1)S(1)} %get-tuple-element.193), channel_id=1, source_target_pairs={{0,1},{1,2},{2,3},{3,4},{4,5},{5,6},{6,7},{8,9},{9,10},{10,11},{11... | collective-permute-start | bytes 98312 | tf_op jit(solution)/shard_map/ppermute | solution.py:21
  26.3 5.5 %collective-permute-start.3 = (bf16[32,1,1,1024]{3,0,2,1:T(8,128)(2,1)S(1)}, bf16[32,1,1,1024]{3,0,2,1:T(8,128)(2,1)S(1)}, u32[]{:S(2)}, u32[]{:S(2)}) collective-permute-start(bf16[32,1,1,1024]{3,0,2,1:T(8,128)(2,1)S(1)} %get-tuple-element.192), channel_id=1, source_target_pairs={{1,0},{2,1},{3,2},{4,3},{5,4},{6,5},{7,6},{9,8},{10,9},{11,10},{12... | collective-permute-start | bytes 196616 | tf_op jit(solution)/shard_map/ppermute | solution.py:22
  27.6 5.5 %collective-permute-start.2 = (bf16[32,1,1,1024]{3,0,2,1:T(8,128)(2,1)S(1)}, bf16[32,1,1,1024]{3,0,2,1:T(8,128)(2,1)S(1)}, u32[]{:S(2)}, u32[]{:S(2)}) collective-permute-start(bf16[32,1,1,1024]{3,0,2,1:T(8,128)(2,1)S(1)} %get-tuple-element.191), channel_id=1, source_target_pairs={{0,1},{1,2},{2,3},{3,4},{4,5},{5,6},{6,7},{8,9},{9,10},{10,11},{11... | collective-permute-start | bytes 196616 | tf_op jit(solution)/shard_map/ppermute | solution.py:21
  33.3 2.5 %copy-start.7 = (bf16[27,32,64]{2,1,0:T(8,128)(2,1)S(1)}, bf16[27,32,64]{2,1,0:T(8,128)(2,1)}, u32[]{:S(2)}) copy-start(bf16[27,32,64]{2,1,0:T(8,128)(2,1)} %param.12) | copy-start | bytes 331780
  33.3 2.5 %copy-start.10 = (f32[64]{0:T(128)S(1)}, f32[64]{0:T(128)}, u32[]{:S(2)}) copy-start(f32[64]{0:T(128)} %param.13) | copy-start | bytes 772
  35.8 2.1 %copy-start.9 = (bf16[864,1,2,1024]{3,0,2,1:T(8,128)(2,1)}, bf16[864,1,2,1024]{3,0,2,1:T(8,128)(2,1)S(1)}, u32[]{:S(2)}) copy-start(bf16[864,1,2,1024]{3,0,2,1:T(8,128)(2,1)S(1)} %constant_dynamic-update-slice_fusion) | copy-start | bytes 10616836
  35.9 8.3 %copy-start = (bf16[6,4,36,1024]{3,2,1,0:T(8,128)(2,1)S(1)}, bf16[6,4,36,1024]{3,2,1,0:T(8,128)(2,1)}, u32[]{:S(2)}) copy-start(bf16[6,4,36,1024]{3,2,1,0:T(8,128)(2,1)} %get-tuple-element.83) | copy-start | bytes 5308420
  38.6 7.6 %collective-permute-start.5 = (bf16[64,1,1,256]{0,3,2,1:T(8,128)(2,1)S(1)}, bf16[64,1,1,256]{0,3,2,1:T(8,128)(2,1)S(1)}, u32[]{:S(2)}, u32[]{:S(2)}) collective-permute-start(bf16[64,1,1,256]{0,3,2,1:T(8,128)(2,1)S(1)} %fusion.142), channel_id=1, source_target_pairs={{1,0},{2,1},{3,2},{4,3},{5,4},{6,5},{7,6},{9,8},{10,9},{11,10},{12... | collective-permute-start | bytes 98312 | tf_op jit(solution)/shard_map/ppermute | solution.py:22
  39.9 6.3 %collective-permute-start.4 = (bf16[64,1,1,256]{0,3,2,1:T(8,128)(2,1)S(1)}, bf16[64,1,1,256]{0,3,2,1:T(8,128)(2,1)S(1)}, u32[]{:S(2)}, u32[]{:S(2)}) collective-permute-start(bf16[64,1,1,256]{0,3,2,1:T(8,128)(2,1)S(1)} %fusion.142), channel_id=1, source_target_pairs={{0,1},{1,2},{2,3},{3,4},{4,5},{5,6},{6,7},{8,9},{9,10},{10,11},{11... | collective-permute-start | bytes 98312 | tf_op jit(solution)/shard_map/ppermute | solution.py:21
  46.2 4.6 %copy-start.6 = (bf16[27,64,128]{2,1,0:T(8,128)(2,1)S(1)}, bf16[27,64,128]{2,1,0:T(8,128)(2,1)}, u32[]{:S(2)}) copy-start(bf16[27,64,128]{2,1,0:T(8,128)(2,1)} %param.14) | copy-start | bytes 1327108
  46.2 4.6 %copy-start.11 = (f32[128]{0:T(128)S(1)}, f32[128]{0:T(128)}, u32[]{:S(2)}) copy-start(f32[128]{0:T(128)} %param.15) | copy-start | bytes 1540
  52.7 7.2 %collective-permute-start.7 = (bf16[128,1,1,256]{0,3,2,1:T(8,128)(2,1)S(1)}, bf16[128,1,1,256]{0,3,2,1:T(8,128)(2,1)S(1)}, u32[]{:S(2)}, u32[]{:S(2)}) collective-permute-start(bf16[128,1,1,256]{0,3,2,1:T(8,128)(2,1)S(1)} %get-tuple-element.147), channel_id=1, source_target_pairs={{1,0},{2,1},{3,2},{4,3},{5,4},{6,5},{7,6},{9,8},{10,9},{11,10},{12... | collective-permute-start | bytes 196616 | tf_op jit(solution)/shard_map/ppermute | solution.py:22
  54.0 6.6 %collective-permute-start.6 = (bf16[128,1,1,256]{0,3,2,1:T(8,128)(2,1)S(1)}, bf16[128,1,1,256]{0,3,2,1:T(8,128)(2,1)S(1)}, u32[]{:S(2)}, u32[]{:S(2)}) collective-permute-start(bf16[128,1,1,256]{0,3,2,1:T(8,128)(2,1)S(1)} %get-tuple-element.147), channel_id=1, source_target_pairs={{0,1},{1,2},{2,3},{3,4},{4,5},{5,6},{6,7},{8,9},{9,10},{10,11},{11... | collective-permute-start | bytes 196616 | tf_op jit(solution)/shard_map/ppermute | solution.py:21
  60.9 3.4 %copy-start.5 = (f32[64,2,1024]{2,0,1:T(8,128)S(1)}, f32[64,2,1024]{2,0,1:T(8,128)}, u32[]{:S(2)}) copy-start(f32[64,2,1024]{2,0,1:T(8,128)} %get-tuple-element.200) | copy-start | bytes 1572868
  64.6 10.4 %collective-permute-start.9 = (bf16[64,1,1,1024]{3,0,2,1:T(8,128)(2,1)S(1)}, bf16[64,1,1,1024]{3,0,2,1:T(8,128)(2,1)S(1)}, u32[]{:S(2)}, u32[]{:S(2)}) collective-permute-start(bf16[64,1,1,1024]{3,0,2,1:T(8,128)(2,1)S(1)} %get-tuple-element.162), channel_id=1, source_target_pairs={{1,0},{2,1},{3,2},{4,3},{5,4},{6,5},{7,6},{9,8},{10,9},{11,10},{12... | collective-permute-start | bytes 393224 | tf_op jit(solution)/shard_map/ppermute | solution.py:22
  65.9 9.1 %collective-permute-start.8 = (bf16[64,1,1,1024]{3,0,2,1:T(8,128)(2,1)S(1)}, bf16[64,1,1,1024]{3,0,2,1:T(8,128)(2,1)S(1)}, u32[]{:S(2)}, u32[]{:S(2)}) collective-permute-start(bf16[64,1,1,1024]{3,0,2,1:T(8,128)(2,1)S(1)} %get-tuple-element.161), channel_id=1, source_target_pairs={{0,1},{1,2},{2,3},{3,4},{4,5},{5,6},{6,7},{8,9},{9,10},{10,11},{11... | collective-permute-start | bytes 393224 | tf_op jit(solution)/shard_map/ppermute | solution.py:21
  78.8 2.4 %copy-start.1 = (bf16[32,4,4,1024]{3,2,1,0:T(4,128)(2,1)S(1)}, bf16[32,4,4,1024]{3,2,1,0:T(4,128)(2,1)}, u32[]{:S(2)}) copy-start(bf16[32,4,4,1024]{3,2,1,0:T(4,128)(2,1)} %get-tuple-element.82) | copy-start | bytes 3145732
  81.1 5.3 %copy-start.3 = (bf16[4,4,36,1024]{3,2,1,0:T(8,128)(2,1)S(1)}, bf16[4,4,36,1024]{3,2,1,0:T(8,128)(2,1)}, u32[]{:S(2)}) copy-start(bf16[4,4,36,1024]{3,2,1,0:T(8,128)(2,1)} %get-tuple-element.150) | copy-start | bytes 3538948
  83.5 4.5 %copy-start.2 = (bf16[4,4,36,1024]{3,2,1,0:T(8,128)(2,1)S(1)}, bf16[4,4,36,1024]{3,2,1,0:T(8,128)(2,1)}, u32[]{:S(2)}) copy-start(bf16[4,4,36,1024]{3,2,1,0:T(8,128)(2,1)} %get-tuple-element.148) | copy-start | bytes 3538948
  86.4 3.3 %copy-start.4 = (f32[432,128]{1,0:T(8,128)S(1)}, f32[432,128]{1,0:T(8,128)}, u32[]{:S(2)}) copy-start(f32[432,128]{1,0:T(8,128)} %reshape.391) | copy-start | bytes 663556
  90.2 6.0 %collective-permute-start.10 = (f32[1152,128]{1,0:T(8,128)S(1)}, f32[1152,128]{1,0:T(8,128)S(1)}, u32[]{:S(2)}, u32[]{:S(2)}) collective-permute-start(f32[1152,128]{1,0:T(8,128)S(1)} %constant_dynamic-slice_fusion.4), channel_id=1, source_target_pairs={{0,8},{8,0},{16,24},{24,16},{32,40},{40,32},{48,56},{56,48},{64,72... | collective-permute-start | bytes 1769480 | tf_op jit(solution)/shard_map/ppermute | solution.py:327
  96.4 8.3 %collective-permute-start.11 = (f32[576,128]{1,0:T(8,128)S(1)}, f32[576,128]{1,0:T(8,128)S(1)}, u32[]{:S(2)}, u32[]{:S(2)}) collective-permute-start(f32[576,128]{1,0:T(8,128)S(1)} %constant_dynamic-slice_fusion.3), channel_id=1, source_target_pairs={{0,16},{8,24},{16,0},{24,8},{32,48},{40,56},{48,32},{56,40},{64,80... | collective-permute-start | bytes 884744 | tf_op jit(solution)/shard_map/ppermute | solution.py:327
  104.8 5.6 %collective-permute-start.12 = (f32[288,128]{1,0:T(8,128)S(1)}, f32[288,128]{1,0:T(8,128)S(1)}, u32[]{:S(2)}, u32[]{:S(2)}) collective-permute-start(f32[288,128]{1,0:T(8,128)S(1)} %constant_dynamic-slice_fusion.2), channel_id=1, source_target_pairs={{0,32},{8,40},{16,48},{24,56},{32,0},{40,8},{48,16},{56,24},{64,96... | collective-permute-start | bytes 442376 | tf_op jit(solution)/shard_map/ppermute | solution.py:327
  107.3 61.3 %copy-start.8 = (f32[128,256]{0,1:T(8,128)S(1)}, f32[128,256]{0,1:T(8,128)}, u32[]{:S(2)}) copy-start(f32[128,256]{0,1:T(8,128)} %get-tuple-element.201) | copy-start | bytes 393220
  110.4 3.3 %collective-permute-start.13 = (f32[144,128]{1,0:T(8,128)S(1)}, f32[144,128]{1,0:T(8,128)S(1)}, u32[]{:S(2)}, u32[]{:S(2)}) collective-permute-start(f32[144,128]{1,0:T(8,128)S(1)} %constant_dynamic-slice_fusion.1), channel_id=1, source_target_pairs={{0,64},{8,72},{16,80},{24,88},{32,96},{40,104},{48,112},{56,120},{... | collective-permute-start | bytes 221192 | tf_op jit(solution)/shard_map/ppermute | solution.py:327
  113.7 4.8 %collective-permute-start.14 = (f32[72,128]{1,0:T(8,128)S(1)}, f32[72,128]{1,0:T(8,128)S(1)}, u32[]{:S(2)}, u32[]{:S(2)}) collective-permute-start(f32[72,128]{1,0:T(8,128)S(1)} %constant_dynamic-slice_fusion), channel_id=1, source_target_pairs={{0,128},{8,136},{16,144},{24,152},{32,160},{40,168},{48,176},{56,1... | collective-permute-start | bytes 110600 | tf_op jit(solution)/shard_map/ppermute | solution.py:327
  118.5 4.0 %collective-permute-start.15 = (f32[72,128]{1,0:T(8,128)S(1)}, f32[72,128]{1,0:T(8,128)S(1)}, u32[]{:S(2)}, u32[]{:S(2)}) collective-permute-start(f32[72,128]{1,0:T(8,128)S(1)} %dynamic-slice_add_fusion.4), channel_id=1, source_target_pairs={{0,1},{1,0},{2,3},{3,2},{4,5},{5,4},{6,7},{7,6},{8,9},{9,8},{10,11... | collective-permute-start | bytes 110600 | tf_op jit(solution)/shard_map/ppermute | solution.py:330
  122.5 7.5 %collective-permute-start.16 = (f32[72,128]{1,0:T(8,128)S(1)}, f32[72,128]{1,0:T(8,128)S(1)}, u32[]{:S(2)}, u32[]{:S(2)}) collective-permute-start(f32[72,128]{1,0:T(8,128)S(1)} %add.526), channel_id=1, source_target_pairs={{0,2},{1,3},{2,0},{3,1},{4,6},{5,7},{6,4},{7,5},{8,10},{9,11},{10,... | collective-permute-start | bytes 110600 | tf_op jit(solution)/shard_map/ppermute | solution.py:330
  130.0 7.4 %collective-permute-start.17 = (f32[72,128]{1,0:T(8,128)S(1)}, f32[72,128]{1,0:T(8,128)S(1)}, u32[]{:S(2)}, u32[]{:S(2)}) collective-permute-start(f32[72,128]{1,0:T(8,128)S(1)} %add.527), channel_id=1, source_target_pairs={{0,4},{1,5},{2,6},{3,7},{4,0},{5,1},{6,2},{7,3},{8,12},{9,13},{10,... | collective-permute-start | bytes 110600 | tf_op jit(solution)/shard_map/ppermute | solution.py:330
  137.4 4.3 %collective-permute-start.18 = (f32[72,128]{1,0:T(8,128)S(1)}, f32[72,128]{1,0:T(8,128)S(1)}, u32[]{:S(2)}, u32[]{:S(2)}) collective-permute-start(f32[72,128]{1,0:T(8,128)S(1)} %add.528), channel_id=1, source_target_pairs={{0,128},{8,136},{16,144},{24,152},{32,160},{40,168},{48,176},{56,1... | collective-permute-start | bytes 110600 | tf_op jit(solution)/shard_map/ppermute | solution.py:332
  141.8 3.3 %collective-permute-start.19 = (f32[144,128]{1,0:T(8,128)S(1)}, f32[144,128]{1,0:T(8,128)S(1)}, u32[]{:S(2)}, u32[]{:S(2)}) collective-permute-start(f32[144,128]{1,0:T(8,128)S(1)} %get-tuple-element.195), channel_id=1, source_target_pairs={{0,64},{8,72},{16,80},{24,88},{32,96},{40,104},{48,112},{56,120},{... | collective-permute-start | bytes 221192 | tf_op jit(solution)/shard_map/ppermute | solution.py:332
  145.1 5.6 %collective-permute-start.20 = (f32[288,128]{1,0:T(8,128)S(1)}, f32[288,128]{1,0:T(8,128)S(1)}, u32[]{:S(2)}, u32[]{:S(2)}) collective-permute-start(f32[288,128]{1,0:T(8,128)S(1)} %get-tuple-element.187), channel_id=1, source_target_pairs={{0,32},{8,40},{16,48},{24,56},{32,0},{40,8},{48,16},{56,24},{64,96... | collective-permute-start | bytes 442376 | tf_op jit(solution)/shard_map/ppermute | solution.py:332
  150.8 5.7 %collective-permute-start.21 = (f32[576,128]{1,0:T(8,128)S(1)}, f32[576,128]{1,0:T(8,128)S(1)}, u32[]{:S(2)}, u32[]{:S(2)}) collective-permute-start(f32[576,128]{1,0:T(8,128)S(1)} %get-tuple-element.157), channel_id=1, source_target_pairs={{0,16},{8,24},{16,0},{24,8},{32,48},{40,56},{48,32},{56,40},{64,80... | collective-permute-start | bytes 884744 | tf_op jit(solution)/shard_map/ppermute | solution.py:332
  156.7 13.6 %collective-permute-start.22 = (f32[1152,128]{1,0:T(8,128)S(1)}, f32[1152,128]{1,0:T(8,128)S(1)}, u32[]{:S(2)}, u32[]{:S(2)}) collective-permute-start(f32[1152,128]{1,0:T(8,128)S(1)} %get-tuple-element.153), channel_id=1, source_target_pairs={{0,8},{8,0},{16,24},{24,16},{32,40},{40,32},{48,56},{56,48},{64,72... | collective-permute-start | bytes 1769480 | tf_op jit(solution)/shard_map/ppermute | solution.py:332

commit v7 on v6

--- a/solution.py
+++ b/solution.py
@@ -297,7 +297,7 @@
     return [(i, i ^ mask) for i in range(lax.axis_size(axis))]
 
 
-def all_reduce_rows(grads, halving_steps=5, lanes=128):
+def all_reduce_rows(grads, halving_steps=4, lanes=128):
     steps = []
     for axis in ("sample", "slab"):
         mask = 1

time: 175 us -> 174 us (level)
    ppermute x3 -> x4, waiting for transfers between devices: 4.14 us -> 8.28 us  [all_reduce_rows(): buffer = buffer + lax.ppermute(buffer, axis, xor_pairs(axis, mask))]
    ppermute x3 -> x4, starting transfers between devices: 14.7 us -> 18 us  [all_reduce_rows(): buffer = buffer + lax.ppermute(buffer, axis, xor_pairs(axis, mask))]
    ppermute x5 -> x4, starting transfers between devices: 10.9 us -> 8.5 us  [all_reduce_rows(): buffer = keep + lax.ppermute(send, axis, xor_pairs(axis, mask))]
    ppermute x5 -> x4, waiting for transfers between devices: 17.1 us -> 14.7 us  [all_reduce_rows(): buffer = keep + lax.ppermute(send, axis, xor_pairs(axis, mask))]
    ppermute x5 -> x4, waiting for transfers between devices: 12.4 us -> 10.2 us  [all_reduce_rows(): other = lax.ppermute(buffer, axis, xor_pairs(axis, mask))]
    ppermute x5 -> x4, starting transfers between devices: 19.2 us -> 17.4 us  [all_reduce_rows(): other = lax.ppermute(buffer, axis, xor_pairs(axis, mask))]
  transfers between devices with their start and end apart: 23 -> 22, of which waited for: 15 -> 14; matrix products, arithmetic and copies ran while one was open for 8% -> 8% of each run, Pallas kernels for 0% -> 0%
where the time goes in v7:
time: 174 us; the launch traced here: 173 us
  starting transfers between devices  74.5 us (43%)
  waiting for transfers between devices  35.2 us (20%)
  local copies, waits for them, and re-layouts  23.6 us (14%)
  other arithmetic  18.7 us (11%)
  matrix products  15 us (9%)
  Pallas kernels  4.45 us (3%)
  between operations  1.88 us (1%)
    ppermute x5, starting transfers between devices, with_halo(): before = lax.ppermute(last, axis, up)  24.1 us
    ppermute x4, starting transfers between devices, all_reduce_rows(): buffer = buffer + lax.ppermute(buffer, axis, xor_pairs(axis, mask))  18 us
    ppermute x4, starting transfers between devices, all_reduce_rows(): other = lax.ppermute(buffer, axis, xor_pairs(axis, mask))  17.4 us
    ppermute x4, waiting for transfers between devices, all_reduce_rows(): buffer = keep + lax.ppermute(send, axis, xor_pairs(axis, mask))  14.7 us
    ppermute x4, waiting for transfers between devices, all_reduce_rows(): other = lax.ppermute(buffer, axis, xor_pairs(axis, mask))  10.2 us
    ppermute x4, starting transfers between devices, all_reduce_rows(): buffer = keep + lax.ppermute(send, axis, xor_pairs(axis, mask))  8.5 us
    ppermute x4, waiting for transfers between devices, all_reduce_rows(): buffer = buffer + lax.ppermute(buffer, axis, xor_pairs(axis, mask))  8.28 us
    ppermute x5, starting transfers between devices, with_halo(): after = lax.ppermute(first, axis, down)  6.45 us
  transfers between devices with their start and end apart: 22, of which 14 were waited for; matrix products, arithmetic and copies ran while one was open for 8% of the time, Pallas kernels for 0%

profile of v7, /device:TPU:1, one launch (start us, length us, event | category | flops | bytes accessed | tf_op | source)
XLA Modules:
  0.0 173.2 jit_solution(5409614568244775476)
XLA Ops:
  0.6 1.1 fusion.163
  1.7 1.3 collective-permute-start.1
  3.0 5.0 %collective-permute-start = (bf16[4,1,1,4096]{3,2,1,0:T(2,128)(2,1)S(1)}, bf16[4,1,1,4096]{3,2,1,0:T(2,128)(2,1)S(1)}, u32[]{:S(2)}, u32[]{:S(2)}) collective-permute-start(bf16[4,1,1,4096]{3,2,1,0:T(2,128)(2,1)S(1)} %get-tuple-element.193), channel_id=1, source_target_pairs={{0,1},{1,2},{2,3},{3,4},{4,5},{5,6},{6,7},{8,9},{9,10},{10,11},{11... | collective-permute-start | bytes 98312 | tf_op jit(solution)/shard_map/ppermute | solution.py:21
  8.8 1.0 reverse_bitcast_fusion
  10.8 1.6 copy.94
  13.8 1.3 copy.90.b_ref
  15.6 1.1 maximum_bitcast_fusion
  17.6 4.4 %shard_map.135 = (bf16[32,4,4,1024]{3,2,1,0:T(4,128)(2,1)}, bf16[6,4,36,1024]{3,2,1,0:T(8,128)(2,1)}) custom-call(bf16[24,4096]{1,0:T(8,128)(2,1)} %reshape.381.src_ref, bf16[128,128]{1,0:T(8,128)(2,1)} %fusion.145.perm_ref, bf16[3,32,36]{2,1,0:T(8,128)(2,1)} %bitcast.174, f32[32,1]{1,0:T(8,128)} %copy.90.b_ref), custom_call_target="tpu_custom_call" | custom-call | tf_op jit(solution)/shard_map/pallas_call | solution.py:214
  22.0 4.0 %fusion.9 = f32[32,4,1024]{2,1,0:T(4,128)S(1)} fusion(bf16[32,4,4,1024]{3,2,1,0:T(4,128)(2,1)} %get-tuple-element.82), kind=kLoop, calls=%fused_computation.12 | loop fusion | flops 3014656 | bytes 1572864 | tf_op jit(solution)/shard_map/reduce_sum | solution.py:152
  26.3 1.3 collective-permute-start.3
  27.6 4.2 %collective-permute-start.2 = (bf16[32,1,1,1024]{3,0,2,1:T(8,128)(2,1)S(1)}, bf16[32,1,1,1024]{3,0,2,1:T(8,128)(2,1)S(1)}, u32[]{:S(2)}, u32[]{:S(2)}) collective-permute-start(bf16[32,1,1,1024]{3,0,2,1:T(8,128)(2,1)S(1)} %get-tuple-element.191), channel_id=1, source_target_pairs={{0,1},{1,2},{2,3},{3,4},{4,5},{5,6},{6,7},{8,9},{9,10},{10,11},{11... | collective-permute-start | bytes 196616 | tf_op jit(solution)/shard_map/ppermute | solution.py:21
  31.8 1.3 collective-permute-done.2
  35.8 1.6 multiply_reduce_fusion
  38.5 1.3 collective-permute-start.5
  39.8 4.3 %collective-permute-start.4 = (bf16[64,1,1,256]{0,3,2,1:T(8,128)(2,1)S(1)}, bf16[64,1,1,256]{0,3,2,1:T(8,128)(2,1)S(1)}, u32[]{:S(2)}, u32[]{:S(2)}) collective-permute-start(bf16[64,1,1,256]{0,3,2,1:T(8,128)(2,1)S(1)} %fusion.142), channel_id=1, source_target_pairs={{0,1},{1,2},{2,3},{3,4},{4,5},{5,6},{6,7},{8,9},{9,10},{10,11},{11... | collective-permute-start | bytes 98312 | tf_op jit(solution)/shard_map/ppermute | solution.py:21
  44.2 2.0 %fusion.160 = (bf16[4,4,36,1024]{3,2,1,0:T(8,128)(2,1)}, bf16[4,4,36,1024]{3,2,1,0:T(8,128)(2,1)}, bf16[4,4,36,1024]{3,2,1,0:T(8,128)(2,1)}) fusion(bf16[6,4,36,1024]{3,2,1,0:T(8,128)(2,1)S(1)} %copy-done), kind=kLoop, calls=%fused_computation.346 | loop fusion | bytes 7077888 | tf_op jit(solution)/shard_map/slice | solution.py:228
  47.2 3.6 %concatenate.68 = bf16[1728,1,1,256]{0,3,2,1:T(8,128)(2,1)S(1)} concatenate(bf16[64,1,1,256]{0,3,2,1:T(8,128)(2,1)S(1)} %get-tuple-element.180, bf16[64,1,1,256]{0,3,2,1:T(8,128)(2,1)} %get-tuple-element.186, bf16[64,1,1,256]{0,3,2,1:T(8,128)(2,1)S(1)} %get-tuple-element.171, bf16[64,1,1,256]{0,3,2,1:T(8,128)(2,1)S(1)} %get-tuple-element.179, ...), dimensions={0} | concatenate | bytes 1769472 | tf_op jit(solution)/shard_map/while/body/eval_jaxpr/concatenate | solution.py:57
  50.8 1.9 %convert_reduce_fusion.2 = (f32[128]{0:T(128)S(1)}, bf16[128,1,1,256]{0,3,2,1:T(8,128)(2,1)S(1)}, f32[128,256]{0,1:T(8,128)}) fusion(bf16[128,1,1,256]{0,3,2,1:T(8,128)(2,1)} %copy.94, f32[128]{0:T(128)S(1)} %copy-done.11, bf16[1728,128]{1,0:T(8,128)(2,1)S(1)} %bitcast.169, bf16[1728,1,1,256]{0,3,2,1:T(8,128)(2,1)S(1)} %concatenate.68), kind=kOutput, calls=%fused_computation.253 | convolution fusion | flops 113737600 | bytes 1590272 | tf_op jit(solution)/shard_map/while/body/eval_jaxpr/ko,kgzp->ogzp/dot_general | solution.py:62
  52.7 1.3 collective-permute-start.7
  54.0 5.4 %collective-permute-start.6 = (bf16[128,1,1,256]{0,3,2,1:T(8,128)(2,1)S(1)}, bf16[128,1,1,256]{0,3,2,1:T(8,128)(2,1)S(1)}, u32[]{:S(2)}, u32[]{:S(2)}) collective-permute-start(bf16[128,1,1,256]{0,3,2,1:T(8,128)(2,1)S(1)} %get-tuple-element.147), channel_id=1, source_target_pairs={{0,1},{1,2},{2,3},{3,4},{4,5},{5,6},{6,7},{8,9},{9,10},{10,11},{11... | collective-permute-start | bytes 196616 | tf_op jit(solution)/shard_map/ppermute | solution.py:21
  64.6 1.3 collective-permute-start.9
  65.9 5.2 %collective-permute-start.8 = (bf16[64,1,1,1024]{3,0,2,1:T(8,128)(2,1)S(1)}, bf16[64,1,1,1024]{3,0,2,1:T(8,128)(2,1)S(1)}, u32[]{:S(2)}, u32[]{:S(2)}) collective-permute-start(bf16[64,1,1,1024]{3,0,2,1:T(8,128)(2,1)S(1)} %get-tuple-element.161), channel_id=1, source_target_pairs={{0,1},{1,2},{2,3},{3,4},{4,5},{5,6},{6,7},{8,9},{9,10},{10,11},{11... | collective-permute-start | bytes 393224 | tf_op jit(solution)/shard_map/ppermute | solution.py:21
  71.1 3.1 %fusion.25 = f32[864,64]{1,0:T(8,128)S(1)} fusion(bf16[64,2,1024]{2,0,1:T(8,128)(2,1)S(1)} %get-tuple-element.145, bf16[864,1,2,1024]{3,0,2,1:T(8,128)(2,1)} %copy-done.9), kind=kOutput, calls=%fused_computation.33 | convolution fusion | flops 226492416 | bytes 4022272 | tf_op jit(solution)/shard_map/while/body/eval_jaxpr/kgzp,ogzp->ko/dot_general | solution.py:66
  78.7 1.3 fusion.47
  81.1 2.3 %convert_reduce_fusion = (f32[32]{0:T(128)S(1)}, bf16[32,4,4,1024]{3,2,1,0:T(4,128)(2,1)S(1)}) fusion(bf16[32,4,4,1024]{3,2,1,0:T(4,128)(2,1)S(1)} %copy-done.1, f32[32,4,1024]{2,1,0:T(4,128)S(1)} %mul.1107), kind=kLoop, calls=%fused_computation.17 | loop fusion | flops 6291424 | bytes 2621568 | tf_op jit(solution)/shard_map/reduce_sum | solution.py:280
  83.4 2.9 %fusion.71 = f32[1,36,32]{1,2,0:T(8,128)S(1)} fusion(bf16[4,4,36,1024]{3,2,1,0:T(8,128)(2,1)} %get-tuple-element.149, bf16[32,4,4,1024]{3,2,1,0:T(4,128)(2,1)S(1)} %get-tuple-element.143), kind=kOutput, calls=%fused_computation.52 | convolution fusion | flops 37748736 | bytes 2232832 | tf_op jit(solution)/shard_map/zpkq,ozpq->ko/dot_general | solution.py:227
  86.4 1.5 fusion.68
  87.9 1.5 fusion.65
  90.2 4.4 %collective-permute-start.10 = (f32[1152,128]{1,0:T(8,128)S(1)}, f32[1152,128]{1,0:T(8,128)S(1)}, u32[]{:S(2)}, u32[]{:S(2)}) collective-permute-start(f32[1152,128]{1,0:T(8,128)S(1)} %constant_dynamic-slice_fusion.3), channel_id=1, source_target_pairs={{0,8},{8,0},{16,24},{24,16},{32,40},{40,32},{48,56},{56,48},{64,72... | collective-permute-start | bytes 1769480 | tf_op jit(solution)/shard_map/ppermute | solution.py:327
  94.6 1.6 collective-permute-done.10
  97.2 7.5 %collective-permute-done.11 = f32[576,128]{1,0:T(8,128)S(1)} collective-permute-done((f32[576,128]{1,0:T(8,128)S(1)}, f32[576,128]{1,0:T(8,128)S(1)}, u32[]{:S(2)}, u32[]{:S(2)}) %collective-permute-start.11) | collective-permute-done | bytes 294944 | tf_op jit(solution)/shard_map/ppermute | solution.py:327
  104.8 2.5 %collective-permute-start.12 = (f32[288,128]{1,0:T(8,128)S(1)}, f32[288,128]{1,0:T(8,128)S(1)}, u32[]{:S(2)}, u32[]{:S(2)}) collective-permute-start(f32[288,128]{1,0:T(8,128)S(1)} %constant_dynamic-slice_fusion.1), channel_id=1, source_target_pairs={{0,32},{8,40},{16,48},{24,56},{32,0},{40,8},{48,16},{56,24},{64,96... | collective-permute-start | bytes 442376 | tf_op jit(solution)/shard_map/ppermute | solution.py:327
  107.2 3.1 %collective-permute-done.12 = f32[288,128]{1,0:T(8,128)S(1)} collective-permute-done((f32[288,128]{1,0:T(8,128)S(1)}, f32[288,128]{1,0:T(8,128)S(1)}, u32[]{:S(2)}, u32[]{:S(2)}) %collective-permute-start.12) | collective-permute-done | bytes 147488 | tf_op jit(solution)/shard_map/ppermute | solution.py:327
  111.1 2.5 %collective-permute-done.13 = f32[144,128]{1,0:T(8,128)S(1)} collective-permute-done((f32[144,128]{1,0:T(8,128)S(1)}, f32[144,128]{1,0:T(8,128)S(1)}, u32[]{:S(2)}, u32[]{:S(2)}) %collective-permute-start.13) | collective-permute-done | bytes 73760 | tf_op jit(solution)/shard_map/ppermute | solution.py:327
  113.7 2.3 %collective-permute-start.14 = (f32[144,128]{1,0:T(8,128)S(1)}, f32[144,128]{1,0:T(8,128)S(1)}, u32[]{:S(2)}, u32[]{:S(2)}) collective-permute-start(f32[144,128]{1,0:T(8,128)S(1)} %dynamic-slice_add_fusion.3), channel_id=1, source_target_pairs={{0,128},{8,136},{16,144},{24,152},{32,160},{40,168},{48,176},{56,1... | collective-permute-start | bytes 221192 | tf_op jit(solution)/shard_map/ppermute | solution.py:330
  116.0 2.9 %collective-permute-done.14 = f32[144,128]{1,0:T(8,128)S(1)} collective-permute-done((f32[144,128]{1,0:T(8,128)S(1)}, f32[144,128]{1,0:T(8,128)S(1)}, u32[]{:S(2)}, u32[]{:S(2)}) %collective-permute-start.14) | collective-permute-done | bytes 73760 | tf_op jit(solution)/shard_map/ppermute | solution.py:330
  118.9 3.0 %collective-permute-start.15 = (f32[144,128]{1,0:T(8,128)S(1)}, f32[144,128]{1,0:T(8,128)S(1)}, u32[]{:S(2)}, u32[]{:S(2)}) collective-permute-start(f32[144,128]{1,0:T(8,128)S(1)} %add.504), channel_id=1, source_target_pairs={{0,1},{1,0},{2,3},{3,2},{4,5},{5,4},{6,7},{7,6},{8,9},{9,8},{10,11... | collective-permute-start | bytes 221192 | tf_op jit(solution)/shard_map/ppermute | solution.py:330
  121.9 1.7 %collective-permute-done.15 = f32[144,128]{1,0:T(8,128)S(1)} collective-permute-done((f32[144,128]{1,0:T(8,128)S(1)}, f32[144,128]{1,0:T(8,128)S(1)}, u32[]{:S(2)}, u32[]{:S(2)}) %collective-permute-start.15) | collective-permute-done | bytes 73760 | tf_op jit(solution)/shard_map/ppermute | solution.py:330
  123.7 6.3 %collective-permute-start.16 = (f32[144,128]{1,0:T(8,128)S(1)}, f32[144,128]{1,0:T(8,128)S(1)}, u32[]{:S(2)}, u32[]{:S(2)}) collective-permute-start(f32[144,128]{1,0:T(8,128)S(1)} %add.505), channel_id=1, source_target_pairs={{0,2},{1,3},{2,0},{3,1},{4,6},{5,7},{6,4},{7,5},{8,10},{9,11},{10,... | collective-permute-start | bytes 221192 | tf_op jit(solution)/shard_map/ppermute | solution.py:330
  130.0 1.7 %collective-permute-done.16 = f32[144,128]{1,0:T(8,128)S(1)} collective-permute-done((f32[144,128]{1,0:T(8,128)S(1)}, f32[144,128]{1,0:T(8,128)S(1)}, u32[]{:S(2)}, u32[]{:S(2)}) %collective-permute-start.16) | collective-permute-done | bytes 73760 | tf_op jit(solution)/shard_map/ppermute | solution.py:330
  131.7 6.4 %collective-permute-start.17 = (f32[144,128]{1,0:T(8,128)S(1)}, f32[144,128]{1,0:T(8,128)S(1)}, u32[]{:S(2)}, u32[]{:S(2)}) collective-permute-start(f32[144,128]{1,0:T(8,128)S(1)} %add.506), channel_id=1, source_target_pairs={{0,4},{1,5},{2,6},{3,7},{4,0},{5,1},{6,2},{7,3},{8,12},{9,13},{10,... | collective-permute-start | bytes 221192 | tf_op jit(solution)/shard_map/ppermute | solution.py:330
  138.1 1.8 %collective-permute-done.17 = f32[144,128]{1,0:T(8,128)S(1)} collective-permute-done((f32[144,128]{1,0:T(8,128)S(1)}, f32[144,128]{1,0:T(8,128)S(1)}, u32[]{:S(2)}, u32[]{:S(2)}) %collective-permute-start.17) | collective-permute-done | bytes 73760 | tf_op jit(solution)/shard_map/ppermute | solution.py:330
  140.7 2.6 %collective-permute-done.18 = f32[144,128]{1,0:T(8,128)S(1)} collective-permute-done((f32[144,128]{1,0:T(8,128)S(1)}, f32[144,128]{1,0:T(8,128)S(1)}, u32[]{:S(2)}, u32[]{:S(2)}) %collective-permute-start.18) | collective-permute-done | bytes 73760 | tf_op jit(solution)/shard_map/ppermute | solution.py:332
  143.3 3.0 %collective-permute-start.19 = (f32[288,128]{1,0:T(8,128)S(1)}, f32[288,128]{1,0:T(8,128)S(1)}, u32[]{:S(2)}, u32[]{:S(2)}) collective-permute-start(f32[288,128]{1,0:T(8,128)S(1)} %get-tuple-element.187), channel_id=1, source_target_pairs={{0,32},{8,40},{16,48},{24,56},{32,0},{40,8},{48,16},{56,24},{64,96... | collective-permute-start | bytes 442376 | tf_op jit(solution)/shard_map/ppermute | solution.py:332
  146.3 2.6 %collective-permute-done.19 = f32[288,128]{1,0:T(8,128)S(1)} collective-permute-done((f32[288,128]{1,0:T(8,128)S(1)}, f32[288,128]{1,0:T(8,128)S(1)}, u32[]{:S(2)}, u32[]{:S(2)}) %collective-permute-start.19) | collective-permute-done | bytes 147488 | tf_op jit(solution)/shard_map/ppermute | solution.py:332
  149.0 1.4 collective-permute-start.20
  150.4 4.3 %collective-permute-done.20 = f32[576,128]{1,0:T(8,128)S(1)} collective-permute-done((f32[576,128]{1,0:T(8,128)S(1)}, f32[576,128]{1,0:T(8,128)S(1)}, u32[]{:S(2)}, u32[]{:S(2)}) %collective-permute-start.20) | collective-permute-done | bytes 294944 | tf_op jit(solution)/shard_map/ppermute | solution.py:332
  154.9 12.3 %collective-permute-start.21 = (f32[1152,128]{1,0:T(8,128)S(1)}, f32[1152,128]{1,0:T(8,128)S(1)}, u32[]{:S(2)}, u32[]{:S(2)}) collective-permute-start(f32[1152,128]{1,0:T(8,128)S(1)} %get-tuple-element.153), channel_id=1, source_target_pairs={{0,8},{8,0},{16,24},{24,16},{32,40},{40,32},{48,56},{56,48},{64,72... | collective-permute-start | bytes 1769480 | tf_op jit(solution)/shard_map/ppermute | solution.py:332
  (188 shorter events, 29.2 us)
Async XLA Ops:
  1.7 13.8 %collective-permute-start.1 = (bf16[4,1,1,4096]{3,2,1,0:T(2,128)(2,1)S(1)}, bf16[4,1,1,4096]{3,2,1,0:T(2,128)(2,1)S(1)}, u32[]{:S(2)}, u32[]{:S(2)}) collective-permute-start(bf16[4,1,1,4096]{3,2,1,0:T(2,128)(2,1)S(1)} %get-tuple-element.194), channel_id=1, source_target_pairs={{1,0},{2,1},{3,2},{4,3},{5,4},{6,5},{7,6},{9,8},{10,9},{11,10},{12... | collective-permute-start | bytes 98312 | tf_op jit(solution)/shard_map/ppermute | solution.py:22
  3.0 12.5 %collective-permute-start = (bf16[4,1,1,4096]{3,2,1,0:T(2,128)(2,1)S(1)}, bf16[4,1,1,4096]{3,2,1,0:T(2,128)(2,1)S(1)}, u32[]{:S(2)}, u32[]{:S(2)}) collective-permute-start(bf16[4,1,1,4096]{3,2,1,0:T(2,128)(2,1)S(1)} %get-tuple-element.193), channel_id=1, source_target_pairs={{0,1},{1,2},{2,3},{3,4},{4,5},{5,6},{6,7},{8,9},{9,10},{10,11},{11... | collective-permute-start | bytes 98312 | tf_op jit(solution)/shard_map/ppermute | solution.py:21
  26.3 5.5 %collective-permute-start.3 = (bf16[32,1,1,1024]{3,0,2,1:T(8,128)(2,1)S(1)}, bf16[32,1,1,1024]{3,0,2,1:T(8,128)(2,1)S(1)}, u32[]{:S(2)}, u32[]{:S(2)}) collective-permute-start(bf16[32,1,1,1024]{3,0,2,1:T(8,128)(2,1)S(1)} %get-tuple-element.192), channel_id=1, source_target_pairs={{1,0},{2,1},{3,2},{4,3},{5,4},{6,5},{7,6},{9,8},{10,9},{11,10},{12... | collective-permute-start | bytes 196616 | tf_op jit(solution)/shard_map/ppermute | solution.py:22
  27.6 5.5 %collective-permute-start.2 = (bf16[32,1,1,1024]{3,0,2,1:T(8,128)(2,1)S(1)}, bf16[32,1,1,1024]{3,0,2,1:T(8,128)(2,1)S(1)}, u32[]{:S(2)}, u32[]{:S(2)}) collective-permute-start(bf16[32,1,1,1024]{3,0,2,1:T(8,128)(2,1)S(1)} %get-tuple-element.191), channel_id=1, source_target_pairs={{0,1},{1,2},{2,3},{3,4},{4,5},{5,6},{6,7},{8,9},{9,10},{10,11},{11... | collective-permute-start | bytes 196616 | tf_op jit(solution)/shard_map/ppermute | solution.py:21
  33.3 2.5 %copy-start.7 = (bf16[27,32,64]{2,1,0:T(8,128)(2,1)S(1)}, bf16[27,32,64]{2,1,0:T(8,128)(2,1)}, u32[]{:S(2)}) copy-start(bf16[27,32,64]{2,1,0:T(8,128)(2,1)} %param.12) | copy-start | bytes 331780
  33.3 2.5 %copy-start.10 = (f32[64]{0:T(128)S(1)}, f32[64]{0:T(128)}, u32[]{:S(2)}) copy-start(f32[64]{0:T(128)} %param.13) | copy-start | bytes 772
  35.8 2.1 %copy-start.9 = (bf16[864,1,2,1024]{3,0,2,1:T(8,128)(2,1)}, bf16[864,1,2,1024]{3,0,2,1:T(8,128)(2,1)S(1)}, u32[]{:S(2)}) copy-start(bf16[864,1,2,1024]{3,0,2,1:T(8,128)(2,1)S(1)} %constant_dynamic-update-slice_fusion) | copy-start | bytes 10616836
  35.8 8.3 %copy-start = (bf16[6,4,36,1024]{3,2,1,0:T(8,128)(2,1)S(1)}, bf16[6,4,36,1024]{3,2,1,0:T(8,128)(2,1)}, u32[]{:S(2)}) copy-start(bf16[6,4,36,1024]{3,2,1,0:T(8,128)(2,1)} %get-tuple-element.83) | copy-start | bytes 5308420
  38.5 7.6 %collective-permute-start.5 = (bf16[64,1,1,256]{0,3,2,1:T(8,128)(2,1)S(1)}, bf16[64,1,1,256]{0,3,2,1:T(8,128)(2,1)S(1)}, u32[]{:S(2)}, u32[]{:S(2)}) collective-permute-start(bf16[64,1,1,256]{0,3,2,1:T(8,128)(2,1)S(1)} %fusion.142), channel_id=1, source_target_pairs={{1,0},{2,1},{3,2},{4,3},{5,4},{6,5},{7,6},{9,8},{10,9},{11,10},{12... | collective-permute-start | bytes 98312 | tf_op jit(solution)/shard_map/ppermute | solution.py:22
  39.8 6.3 %collective-permute-start.4 = (bf16[64,1,1,256]{0,3,2,1:T(8,128)(2,1)S(1)}, bf16[64,1,1,256]{0,3,2,1:T(8,128)(2,1)S(1)}, u32[]{:S(2)}, u32[]{:S(2)}) collective-permute-start(bf16[64,1,1,256]{0,3,2,1:T(8,128)(2,1)S(1)} %fusion.142), channel_id=1, source_target_pairs={{0,1},{1,2},{2,3},{3,4},{4,5},{5,6},{6,7},{8,9},{9,10},{10,11},{11... | collective-permute-start | bytes 98312 | tf_op jit(solution)/shard_map/ppermute | solution.py:21
  46.1 4.6 %copy-start.6 = (bf16[27,64,128]{2,1,0:T(8,128)(2,1)S(1)}, bf16[27,64,128]{2,1,0:T(8,128)(2,1)}, u32[]{:S(2)}) copy-start(bf16[27,64,128]{2,1,0:T(8,128)(2,1)} %param.14) | copy-start | bytes 1327108
  46.1 4.6 %copy-start.11 = (f32[128]{0:T(128)S(1)}, f32[128]{0:T(128)}, u32[]{:S(2)}) copy-start(f32[128]{0:T(128)} %param.15) | copy-start | bytes 1540
  52.7 7.1 %collective-permute-start.7 = (bf16[128,1,1,256]{0,3,2,1:T(8,128)(2,1)S(1)}, bf16[128,1,1,256]{0,3,2,1:T(8,128)(2,1)S(1)}, u32[]{:S(2)}, u32[]{:S(2)}) collective-permute-start(bf16[128,1,1,256]{0,3,2,1:T(8,128)(2,1)S(1)} %get-tuple-element.147), channel_id=1, source_target_pairs={{1,0},{2,1},{3,2},{4,3},{5,4},{6,5},{7,6},{9,8},{10,9},{11,10},{12... | collective-permute-start | bytes 196616 | tf_op jit(solution)/shard_map/ppermute | solution.py:22
  54.0 6.5 %collective-permute-start.6 = (bf16[128,1,1,256]{0,3,2,1:T(8,128)(2,1)S(1)}, bf16[128,1,1,256]{0,3,2,1:T(8,128)(2,1)S(1)}, u32[]{:S(2)}, u32[]{:S(2)}) collective-permute-start(bf16[128,1,1,256]{0,3,2,1:T(8,128)(2,1)S(1)} %get-tuple-element.147), channel_id=1, source_target_pairs={{0,1},{1,2},{2,3},{3,4},{4,5},{5,6},{6,7},{8,9},{9,10},{10,11},{11... | collective-permute-start | bytes 196616 | tf_op jit(solution)/shard_map/ppermute | solution.py:21
  60.8 3.4 %copy-start.5 = (f32[64,2,1024]{2,0,1:T(8,128)S(1)}, f32[64,2,1024]{2,0,1:T(8,128)}, u32[]{:S(2)}) copy-start(f32[64,2,1024]{2,0,1:T(8,128)} %get-tuple-element.196) | copy-start | bytes 1572868
  64.6 10.4 %collective-permute-start.9 = (bf16[64,1,1,1024]{3,0,2,1:T(8,128)(2,1)S(1)}, bf16[64,1,1,1024]{3,0,2,1:T(8,128)(2,1)S(1)}, u32[]{:S(2)}, u32[]{:S(2)}) collective-permute-start(bf16[64,1,1,1024]{3,0,2,1:T(8,128)(2,1)S(1)} %get-tuple-element.162), channel_id=1, source_target_pairs={{1,0},{2,1},{3,2},{4,3},{5,4},{6,5},{7,6},{9,8},{10,9},{11,10},{12... | collective-permute-start | bytes 393224 | tf_op jit(solution)/shard_map/ppermute | solution.py:22
  65.9 9.1 %collective-permute-start.8 = (bf16[64,1,1,1024]{3,0,2,1:T(8,128)(2,1)S(1)}, bf16[64,1,1,1024]{3,0,2,1:T(8,128)(2,1)S(1)}, u32[]{:S(2)}, u32[]{:S(2)}) collective-permute-start(bf16[64,1,1,1024]{3,0,2,1:T(8,128)(2,1)S(1)} %get-tuple-element.161), channel_id=1, source_target_pairs={{0,1},{1,2},{2,3},{3,4},{4,5},{5,6},{6,7},{8,9},{9,10},{10,11},{11... | collective-permute-start | bytes 393224 | tf_op jit(solution)/shard_map/ppermute | solution.py:21
  78.7 2.4 %copy-start.1 = (bf16[32,4,4,1024]{3,2,1,0:T(4,128)(2,1)S(1)}, bf16[32,4,4,1024]{3,2,1,0:T(4,128)(2,1)}, u32[]{:S(2)}) copy-start(bf16[32,4,4,1024]{3,2,1,0:T(4,128)(2,1)} %get-tuple-element.82) | copy-start | bytes 3145732
  81.1 5.3 %copy-start.3 = (bf16[4,4,36,1024]{3,2,1,0:T(8,128)(2,1)S(1)}, bf16[4,4,36,1024]{3,2,1,0:T(8,128)(2,1)}, u32[]{:S(2)}) copy-start(bf16[4,4,36,1024]{3,2,1,0:T(8,128)(2,1)} %get-tuple-element.150) | copy-start | bytes 3538948
  83.4 4.5 %copy-start.2 = (bf16[4,4,36,1024]{3,2,1,0:T(8,128)(2,1)S(1)}, bf16[4,4,36,1024]{3,2,1,0:T(8,128)(2,1)}, u32[]{:S(2)}) copy-start(bf16[4,4,36,1024]{3,2,1,0:T(8,128)(2,1)} %get-tuple-element.148) | copy-start | bytes 3538948
  86.4 3.3 %copy-start.4 = (f32[432,128]{1,0:T(8,128)S(1)}, f32[432,128]{1,0:T(8,128)}, u32[]{:S(2)}) copy-start(f32[432,128]{1,0:T(8,128)} %reshape.391) | copy-start | bytes 663556
  90.2 6.1 %collective-permute-start.10 = (f32[1152,128]{1,0:T(8,128)S(1)}, f32[1152,128]{1,0:T(8,128)S(1)}, u32[]{:S(2)}, u32[]{:S(2)}) collective-permute-start(f32[1152,128]{1,0:T(8,128)S(1)} %constant_dynamic-slice_fusion.3), channel_id=1, source_target_pairs={{0,8},{8,0},{16,24},{24,16},{32,40},{40,32},{48,56},{56,48},{64,72... | collective-permute-start | bytes 1769480 | tf_op jit(solution)/shard_map/ppermute | solution.py:327
  96.4 8.3 %collective-permute-start.11 = (f32[576,128]{1,0:T(8,128)S(1)}, f32[576,128]{1,0:T(8,128)S(1)}, u32[]{:S(2)}, u32[]{:S(2)}) collective-permute-start(f32[576,128]{1,0:T(8,128)S(1)} %constant_dynamic-slice_fusion.2), channel_id=1, source_target_pairs={{0,16},{8,24},{16,0},{24,8},{32,48},{40,56},{48,32},{56,40},{64,80... | collective-permute-start | bytes 884744 | tf_op jit(solution)/shard_map/ppermute | solution.py:327
  104.7 62.5 %copy-start.8 = (f32[128,256]{0,1:T(8,128)S(1)}, f32[128,256]{0,1:T(8,128)}, u32[]{:S(2)}) copy-start(f32[128,256]{0,1:T(8,128)} %get-tuple-element.197) | copy-start | bytes 393220
  104.8 5.6 %collective-permute-start.12 = (f32[288,128]{1,0:T(8,128)S(1)}, f32[288,128]{1,0:T(8,128)S(1)}, u32[]{:S(2)}, u32[]{:S(2)}) collective-permute-start(f32[288,128]{1,0:T(8,128)S(1)} %constant_dynamic-slice_fusion.1), channel_id=1, source_target_pairs={{0,32},{8,40},{16,48},{24,56},{32,0},{40,8},{48,16},{56,24},{64,96... | collective-permute-start | bytes 442376 | tf_op jit(solution)/shard_map/ppermute | solution.py:327
  110.4 3.3 %collective-permute-start.13 = (f32[144,128]{1,0:T(8,128)S(1)}, f32[144,128]{1,0:T(8,128)S(1)}, u32[]{:S(2)}, u32[]{:S(2)}) collective-permute-start(f32[144,128]{1,0:T(8,128)S(1)} %constant_dynamic-slice_fusion), channel_id=1, source_target_pairs={{0,64},{8,72},{16,80},{24,88},{32,96},{40,104},{48,112},{56,120},{... | collective-permute-start | bytes 221192 | tf_op jit(solution)/shard_map/ppermute | solution.py:327
  113.7 5.2 %collective-permute-start.14 = (f32[144,128]{1,0:T(8,128)S(1)}, f32[144,128]{1,0:T(8,128)S(1)}, u32[]{:S(2)}, u32[]{:S(2)}) collective-permute-start(f32[144,128]{1,0:T(8,128)S(1)} %dynamic-slice_add_fusion.3), channel_id=1, source_target_pairs={{0,128},{8,136},{16,144},{24,152},{32,160},{40,168},{48,176},{56,1... | collective-permute-start | bytes 221192 | tf_op jit(solution)/shard_map/ppermute | solution.py:330
  118.9 4.7 %collective-permute-start.15 = (f32[144,128]{1,0:T(8,128)S(1)}, f32[144,128]{1,0:T(8,128)S(1)}, u32[]{:S(2)}, u32[]{:S(2)}) collective-permute-start(f32[144,128]{1,0:T(8,128)S(1)} %add.504), channel_id=1, source_target_pairs={{0,1},{1,0},{2,3},{3,2},{4,5},{5,4},{6,7},{7,6},{8,9},{9,8},{10,11... | collective-permute-start | bytes 221192 | tf_op jit(solution)/shard_map/ppermute | solution.py:330
  123.7 8.0 %collective-permute-start.16 = (f32[144,128]{1,0:T(8,128)S(1)}, f32[144,128]{1,0:T(8,128)S(1)}, u32[]{:S(2)}, u32[]{:S(2)}) collective-permute-start(f32[144,128]{1,0:T(8,128)S(1)} %add.505), channel_id=1, source_target_pairs={{0,2},{1,3},{2,0},{3,1},{4,6},{5,7},{6,4},{7,5},{8,10},{9,11},{10,... | collective-permute-start | bytes 221192 | tf_op jit(solution)/shard_map/ppermute | solution.py:330
  131.7 8.3 %collective-permute-start.17 = (f32[144,128]{1,0:T(8,128)S(1)}, f32[144,128]{1,0:T(8,128)S(1)}, u32[]{:S(2)}, u32[]{:S(2)}) collective-permute-start(f32[144,128]{1,0:T(8,128)S(1)} %add.506), channel_id=1, source_target_pairs={{0,4},{1,5},{2,6},{3,7},{4,0},{5,1},{6,2},{7,3},{8,12},{9,13},{10,... | collective-permute-start | bytes 221192 | tf_op jit(solution)/shard_map/ppermute | solution.py:330
  140.0 3.3 %collective-permute-start.18 = (f32[144,128]{1,0:T(8,128)S(1)}, f32[144,128]{1,0:T(8,128)S(1)}, u32[]{:S(2)}, u32[]{:S(2)}) collective-permute-start(f32[144,128]{1,0:T(8,128)S(1)} %add.507), channel_id=1, source_target_pairs={{0,64},{8,72},{16,80},{24,88},{32,96},{40,104},{48,112},{56,120},{... | collective-permute-start | bytes 221192 | tf_op jit(solution)/shard_map/ppermute | solution.py:332
  143.3 5.6 %collective-permute-start.19 = (f32[288,128]{1,0:T(8,128)S(1)}, f32[288,128]{1,0:T(8,128)S(1)}, u32[]{:S(2)}, u32[]{:S(2)}) collective-permute-start(f32[288,128]{1,0:T(8,128)S(1)} %get-tuple-element.187), channel_id=1, source_target_pairs={{0,32},{8,40},{16,48},{24,56},{32,0},{40,8},{48,16},{56,24},{64,96... | collective-permute-start | bytes 442376 | tf_op jit(solution)/shard_map/ppermute | solution.py:332
  149.0 5.7 %collective-permute-start.20 = (f32[576,128]{1,0:T(8,128)S(1)}, f32[576,128]{1,0:T(8,128)S(1)}, u32[]{:S(2)}, u32[]{:S(2)}) collective-permute-start(f32[576,128]{1,0:T(8,128)S(1)} %get-tuple-element.157), channel_id=1, source_target_pairs={{0,16},{8,24},{16,0},{24,8},{32,48},{40,56},{48,32},{56,40},{64,80... | collective-permute-start | bytes 884744 | tf_op jit(solution)/shard_map/ppermute | solution.py:332
  154.9 13.9 %collective-permute-start.21 = (f32[1152,128]{1,0:T(8,128)S(1)}, f32[1152,128]{1,0:T(8,128)S(1)}, u32[]{:S(2)}, u32[]{:S(2)}) collective-permute-start(f32[1152,128]{1,0:T(8,128)S(1)} %get-tuple-element.153), channel_id=1, source_target_pairs={{0,8},{8,0},{16,24},{24,16},{32,40},{40,32},{48,56},{56,48},{64,72... | collective-permute-start | bytes 1769480 | tf_op jit(solution)/shard_map/ppermute | solution.py:332

commit v8 on v7

--- a/solution.py
+++ b/solution.py
@@ -304,6 +304,8 @@
         while mask < lax.axis_size(axis):
             steps.append((axis, mask))
             mask *= 2
+    near = {("sample", 1), ("sample", 2), ("sample", 8), ("slab", 1)}
+    steps.sort(key=lambda step: step not in near)
     pieces, offsets = [], []
     rows = 0
     for g in grads:

time: 174 us -> 172 us (0.989)
    ppermute x4, starting transfers between devices: 17.4 us -> 15.5 us  [all_reduce_rows(): other = lax.ppermute(buffer, axis, xor_pairs(axis, mask))]
where the time goes in v8:
time: 172 us; the launch traced here: 171 us
  starting transfers between devices  73.5 us (43%)
  waiting for transfers between devices  34.4 us (20%)
  local copies, waits for them, and re-layouts  23.6 us (14%)
  other arithmetic  18.7 us (11%)
  matrix products  15 us (9%)
  Pallas kernels  4.45 us (3%)
  between operations  1.88 us (1%)
    ppermute x5, starting transfers between devices, with_halo(): before = lax.ppermute(last, axis, up)  24.1 us
    ppermute x4, starting transfers between devices, all_reduce_rows(): buffer = buffer + lax.ppermute(buffer, axis, xor_pairs(axis, mask))  18.5 us
    ppermute x4, starting transfers between devices, all_reduce_rows(): other = lax.ppermute(buffer, axis, xor_pairs(axis, mask))  15.5 us
    ppermute x4, waiting for transfers between devices, all_reduce_rows(): buffer = keep + lax.ppermute(send, axis, xor_pairs(axis, mask))  14.2 us
    ppermute x4, waiting for transfers between devices, all_reduce_rows(): other = lax.ppermute(buffer, axis, xor_pairs(axis, mask))  10.9 us
    ppermute x4, starting transfers between devices, all_reduce_rows(): buffer = keep + lax.ppermute(send, axis, xor_pairs(axis, mask))  8.89 us
    ppermute x4, waiting for transfers between devices, all_reduce_rows(): buffer = buffer + lax.ppermute(buffer, axis, xor_pairs(axis, mask))  7.34 us
    ppermute x5, starting transfers between devices, with_halo(): after = lax.ppermute(first, axis, down)  6.45 us
  transfers between devices with their start and end apart: 22, of which 14 were waited for; matrix products, arithmetic and copies ran while one was open for 8% of the time, Pallas kernels for 0%

profile of v8, /device:TPU:1, one launch (start us, length us, event | category | flops | bytes accessed | tf_op | source)
XLA Modules:
  0.0 171.4 jit_solution(978765367506182463)
XLA Ops:
  0.6 1.1 fusion.163
  1.7 1.3 collective-permute-start.1
  3.0 5.0 %collective-permute-start = (bf16[4,1,1,4096]{3,2,1,0:T(2,128)(2,1)S(1)}, bf16[4,1,1,4096]{3,2,1,0:T(2,128)(2,1)S(1)}, u32[]{:S(2)}, u32[]{:S(2)}) collective-permute-start(bf16[4,1,1,4096]{3,2,1,0:T(2,128)(2,1)S(1)} %get-tuple-element.193), channel_id=1, source_target_pairs={{0,1},{1,2},{2,3},{3,4},{4,5},{5,6},{6,7},{8,9},{9,10},{10,11},{11... | collective-permute-start | bytes 98312 | tf_op jit(solution)/shard_map/ppermute | solution.py:21
  8.8 1.0 reverse_bitcast_fusion
  10.8 1.6 copy.94
  13.8 1.3 copy.90.b_ref
  15.6 1.1 maximum_bitcast_fusion
  17.6 4.4 %shard_map.135 = (bf16[32,4,4,1024]{3,2,1,0:T(4,128)(2,1)}, bf16[6,4,36,1024]{3,2,1,0:T(8,128)(2,1)}) custom-call(bf16[24,4096]{1,0:T(8,128)(2,1)} %reshape.381.src_ref, bf16[128,128]{1,0:T(8,128)(2,1)} %fusion.145.perm_ref, bf16[3,32,36]{2,1,0:T(8,128)(2,1)} %bitcast.174, f32[32,1]{1,0:T(8,128)} %copy.90.b_ref), custom_call_target="tpu_custom_call" | custom-call | tf_op jit(solution)/shard_map/pallas_call | solution.py:214
  22.0 4.0 %fusion.9 = f32[32,4,1024]{2,1,0:T(4,128)S(1)} fusion(bf16[32,4,4,1024]{3,2,1,0:T(4,128)(2,1)} %get-tuple-element.82), kind=kLoop, calls=%fused_computation.12 | loop fusion | flops 3014656 | bytes 1572864 | tf_op jit(solution)/shard_map/reduce_sum | solution.py:152
  26.3 1.3 collective-permute-start.3
  27.6 4.2 %collective-permute-start.2 = (bf16[32,1,1,1024]{3,0,2,1:T(8,128)(2,1)S(1)}, bf16[32,1,1,1024]{3,0,2,1:T(8,128)(2,1)S(1)}, u32[]{:S(2)}, u32[]{:S(2)}) collective-permute-start(bf16[32,1,1,1024]{3,0,2,1:T(8,128)(2,1)S(1)} %get-tuple-element.191), channel_id=1, source_target_pairs={{0,1},{1,2},{2,3},{3,4},{4,5},{5,6},{6,7},{8,9},{9,10},{10,11},{11... | collective-permute-start | bytes 196616 | tf_op jit(solution)/shard_map/ppermute | solution.py:21
  31.8 1.3 collective-permute-done.2
  35.8 1.6 multiply_reduce_fusion
  38.5 1.3 collective-permute-start.5
  39.8 4.3 %collective-permute-start.4 = (bf16[64,1,1,256]{0,3,2,1:T(8,128)(2,1)S(1)}, bf16[64,1,1,256]{0,3,2,1:T(8,128)(2,1)S(1)}, u32[]{:S(2)}, u32[]{:S(2)}) collective-permute-start(bf16[64,1,1,256]{0,3,2,1:T(8,128)(2,1)S(1)} %fusion.142), channel_id=1, source_target_pairs={{0,1},{1,2},{2,3},{3,4},{4,5},{5,6},{6,7},{8,9},{9,10},{10,11},{11... | collective-permute-start | bytes 98312 | tf_op jit(solution)/shard_map/ppermute | solution.py:21
  44.2 2.0 %fusion.160 = (bf16[4,4,36,1024]{3,2,1,0:T(8,128)(2,1)}, bf16[4,4,36,1024]{3,2,1,0:T(8,128)(2,1)}, bf16[4,4,36,1024]{3,2,1,0:T(8,128)(2,1)}) fusion(bf16[6,4,36,1024]{3,2,1,0:T(8,128)(2,1)S(1)} %copy-done), kind=kLoop, calls=%fused_computation.346 | loop fusion | bytes 7077888 | tf_op jit(solution)/shard_map/slice | solution.py:228
  47.2 3.6 %concatenate.68 = bf16[1728,1,1,256]{0,3,2,1:T(8,128)(2,1)S(1)} concatenate(bf16[64,1,1,256]{0,3,2,1:T(8,128)(2,1)S(1)} %get-tuple-element.180, bf16[64,1,1,256]{0,3,2,1:T(8,128)(2,1)} %get-tuple-element.186, bf16[64,1,1,256]{0,3,2,1:T(8,128)(2,1)S(1)} %get-tuple-element.171, bf16[64,1,1,256]{0,3,2,1:T(8,128)(2,1)S(1)} %get-tuple-element.179, ...), dimensions={0} | concatenate | bytes 1769472 | tf_op jit(solution)/shard_map/while/body/eval_jaxpr/concatenate | solution.py:57
  50.8 1.9 %convert_reduce_fusion.2 = (f32[128]{0:T(128)S(1)}, bf16[128,1,1,256]{0,3,2,1:T(8,128)(2,1)S(1)}, f32[128,256]{0,1:T(8,128)}) fusion(bf16[128,1,1,256]{0,3,2,1:T(8,128)(2,1)} %copy.94, f32[128]{0:T(128)S(1)} %copy-done.11, bf16[1728,128]{1,0:T(8,128)(2,1)S(1)} %bitcast.169, bf16[1728,1,1,256]{0,3,2,1:T(8,128)(2,1)S(1)} %concatenate.68), kind=kOutput, calls=%fused_computation.253 | convolution fusion | flops 113737600 | bytes 1590272 | tf_op jit(solution)/shard_map/while/body/eval_jaxpr/ko,kgzp->ogzp/dot_general | solution.py:62
  52.7 1.3 collective-permute-start.7
  54.0 5.4 %collective-permute-start.6 = (bf16[128,1,1,256]{0,3,2,1:T(8,128)(2,1)S(1)}, bf16[128,1,1,256]{0,3,2,1:T(8,128)(2,1)S(1)}, u32[]{:S(2)}, u32[]{:S(2)}) collective-permute-start(bf16[128,1,1,256]{0,3,2,1:T(8,128)(2,1)S(1)} %get-tuple-element.147), channel_id=1, source_target_pairs={{0,1},{1,2},{2,3},{3,4},{4,5},{5,6},{6,7},{8,9},{9,10},{10,11},{11... | collective-permute-start | bytes 196616 | tf_op jit(solution)/shard_map/ppermute | solution.py:21
  64.6 1.3 collective-permute-start.9
  65.9 5.2 %collective-permute-start.8 = (bf16[64,1,1,1024]{3,0,2,1:T(8,128)(2,1)S(1)}, bf16[64,1,1,1024]{3,0,2,1:T(8,128)(2,1)S(1)}, u32[]{:S(2)}, u32[]{:S(2)}) collective-permute-start(bf16[64,1,1,1024]{3,0,2,1:T(8,128)(2,1)S(1)} %get-tuple-element.161), channel_id=1, source_target_pairs={{0,1},{1,2},{2,3},{3,4},{4,5},{5,6},{6,7},{8,9},{9,10},{10,11},{11... | collective-permute-start | bytes 393224 | tf_op jit(solution)/shard_map/ppermute | solution.py:21
  71.1 3.1 %fusion.25 = f32[864,64]{1,0:T(8,128)S(1)} fusion(bf16[64,2,1024]{2,0,1:T(8,128)(2,1)S(1)} %get-tuple-element.145, bf16[864,1,2,1024]{3,0,2,1:T(8,128)(2,1)} %copy-done.9), kind=kOutput, calls=%fused_computation.33 | convolution fusion | flops 226492416 | bytes 4022272 | tf_op jit(solution)/shard_map/while/body/eval_jaxpr/kgzp,ogzp->ko/dot_general | solution.py:66
  78.7 1.3 fusion.47
  81.1 2.3 %convert_reduce_fusion = (f32[32]{0:T(128)S(1)}, bf16[32,4,4,1024]{3,2,1,0:T(4,128)(2,1)S(1)}) fusion(bf16[32,4,4,1024]{3,2,1,0:T(4,128)(2,1)S(1)} %copy-done.1, f32[32,4,1024]{2,1,0:T(4,128)S(1)} %mul.1107), kind=kLoop, calls=%fused_computation.17 | loop fusion | flops 6291424 | bytes 2621568 | tf_op jit(solution)/shard_map/reduce_sum | solution.py:280
  83.4 2.9 %fusion.71 = f32[1,36,32]{1,2,0:T(8,128)S(1)} fusion(bf16[4,4,36,1024]{3,2,1,0:T(8,128)(2,1)} %get-tuple-element.149, bf16[32,4,4,1024]{3,2,1,0:T(4,128)(2,1)S(1)} %get-tuple-element.143), kind=kOutput, calls=%fused_computation.52 | convolution fusion | flops 37748736 | bytes 2232832 | tf_op jit(solution)/shard_map/zpkq,ozpq->ko/dot_general | solution.py:227
  86.4 1.5 fusion.68
  87.9 1.5 fusion.65
  90.2 4.4 %collective-permute-start.10 = (f32[1152,128]{1,0:T(8,128)S(1)}, f32[1152,128]{1,0:T(8,128)S(1)}, u32[]{:S(2)}, u32[]{:S(2)}) collective-permute-start(f32[1152,128]{1,0:T(8,128)S(1)} %constant_dynamic-slice_fusion.3), channel_id=1, source_target_pairs={{0,8},{8,0},{16,24},{24,16},{32,40},{40,32},{48,56},{56,48},{64,72... | collective-permute-start | bytes 1769480 | tf_op jit(solution)/shard_map/ppermute | solution.py:329
  94.6 1.6 collective-permute-done.10
  97.2 7.5 %collective-permute-done.11 = f32[576,128]{1,0:T(8,128)S(1)} collective-permute-done((f32[576,128]{1,0:T(8,128)S(1)}, f32[576,128]{1,0:T(8,128)S(1)}, u32[]{:S(2)}, u32[]{:S(2)}) %collective-permute-start.11) | collective-permute-done | bytes 294944 | tf_op jit(solution)/shard_map/ppermute | solution.py:329
  105.5 3.3 %collective-permute-done.12 = f32[288,128]{1,0:T(8,128)S(1)} collective-permute-done((f32[288,128]{1,0:T(8,128)S(1)}, f32[288,128]{1,0:T(8,128)S(1)}, u32[]{:S(2)}, u32[]{:S(2)}) %collective-permute-start.12) | collective-permute-done | bytes 147488 | tf_op jit(solution)/shard_map/ppermute | solution.py:329
  108.9 2.8 %collective-permute-start.13 = (f32[144,128]{1,0:T(8,128)S(1)}, f32[144,128]{1,0:T(8,128)S(1)}, u32[]{:S(2)}, u32[]{:S(2)}) collective-permute-start(f32[144,128]{1,0:T(8,128)S(1)} %constant_dynamic-slice_fusion), channel_id=1, source_target_pairs={{0,1},{1,0},{2,3},{3,2},{4,5},{5,4},{6,7},{7,6},{8,9},{9,8},{10,11... | collective-permute-start | bytes 221192 | tf_op jit(solution)/shard_map/ppermute | solution.py:329
  111.7 1.7 %collective-permute-done.13 = f32[144,128]{1,0:T(8,128)S(1)} collective-permute-done((f32[144,128]{1,0:T(8,128)S(1)}, f32[144,128]{1,0:T(8,128)S(1)}, u32[]{:S(2)}, u32[]{:S(2)}) %collective-permute-start.13) | collective-permute-done | bytes 73760 | tf_op jit(solution)/shard_map/ppermute | solution.py:329
  113.5 3.0 %collective-permute-start.14 = (f32[144,128]{1,0:T(8,128)S(1)}, f32[144,128]{1,0:T(8,128)S(1)}, u32[]{:S(2)}, u32[]{:S(2)}) collective-permute-start(f32[144,128]{1,0:T(8,128)S(1)} %dynamic-slice_add_fusion.3), channel_id=1, source_target_pairs={{0,32},{8,40},{16,48},{24,56},{32,0},{40,8},{48,16},{56,24},{64,96... | collective-permute-start | bytes 221192 | tf_op jit(solution)/shard_map/ppermute | solution.py:332
  116.5 1.8 %collective-permute-done.14 = f32[144,128]{1,0:T(8,128)S(1)} collective-permute-done((f32[144,128]{1,0:T(8,128)S(1)}, f32[144,128]{1,0:T(8,128)S(1)}, u32[]{:S(2)}, u32[]{:S(2)}) %collective-permute-start.14) | collective-permute-done | bytes 73760 | tf_op jit(solution)/shard_map/ppermute | solution.py:332
  118.3 2.8 %collective-permute-start.15 = (f32[144,128]{1,0:T(8,128)S(1)}, f32[144,128]{1,0:T(8,128)S(1)}, u32[]{:S(2)}, u32[]{:S(2)}) collective-permute-start(f32[144,128]{1,0:T(8,128)S(1)} %add.504), channel_id=1, source_target_pairs={{0,128},{8,136},{16,144},{24,152},{32,160},{40,168},{48,176},{56,1... | collective-permute-start | bytes 221192 | tf_op jit(solution)/shard_map/ppermute | solution.py:332
  121.1 2.0 %collective-permute-done.15 = f32[144,128]{1,0:T(8,128)S(1)} collective-permute-done((f32[144,128]{1,0:T(8,128)S(1)}, f32[144,128]{1,0:T(8,128)S(1)}, u32[]{:S(2)}, u32[]{:S(2)}) %collective-permute-start.15) | collective-permute-done | bytes 73760 | tf_op jit(solution)/shard_map/ppermute | solution.py:332
  123.1 6.3 %collective-permute-start.16 = (f32[144,128]{1,0:T(8,128)S(1)}, f32[144,128]{1,0:T(8,128)S(1)}, u32[]{:S(2)}, u32[]{:S(2)}) collective-permute-start(f32[144,128]{1,0:T(8,128)S(1)} %add.505), channel_id=1, source_target_pairs={{0,2},{1,3},{2,0},{3,1},{4,6},{5,7},{6,4},{7,5},{8,10},{9,11},{10,... | collective-permute-start | bytes 221192 | tf_op jit(solution)/shard_map/ppermute | solution.py:332
  129.4 1.7 %collective-permute-done.16 = f32[144,128]{1,0:T(8,128)S(1)} collective-permute-done((f32[144,128]{1,0:T(8,128)S(1)}, f32[144,128]{1,0:T(8,128)S(1)}, u32[]{:S(2)}, u32[]{:S(2)}) %collective-permute-start.16) | collective-permute-done | bytes 73760 | tf_op jit(solution)/shard_map/ppermute | solution.py:332
  131.1 6.4 %collective-permute-start.17 = (f32[144,128]{1,0:T(8,128)S(1)}, f32[144,128]{1,0:T(8,128)S(1)}, u32[]{:S(2)}, u32[]{:S(2)}) collective-permute-start(f32[144,128]{1,0:T(8,128)S(1)} %add.506), channel_id=1, source_target_pairs={{0,4},{1,5},{2,6},{3,7},{4,0},{5,1},{6,2},{7,3},{8,12},{9,13},{10,... | collective-permute-start | bytes 221192 | tf_op jit(solution)/shard_map/ppermute | solution.py:332
  137.5 1.8 %collective-permute-done.17 = f32[144,128]{1,0:T(8,128)S(1)} collective-permute-done((f32[144,128]{1,0:T(8,128)S(1)}, f32[144,128]{1,0:T(8,128)S(1)}, u32[]{:S(2)}, u32[]{:S(2)}) %collective-permute-start.17) | collective-permute-done | bytes 73760 | tf_op jit(solution)/shard_map/ppermute | solution.py:332
  140.0 2.7 %collective-permute-done.18 = f32[144,128]{1,0:T(8,128)S(1)} collective-permute-done((f32[144,128]{1,0:T(8,128)S(1)}, f32[144,128]{1,0:T(8,128)S(1)}, u32[]{:S(2)}, u32[]{:S(2)}) %collective-permute-start.18) | collective-permute-done | bytes 73760 | tf_op jit(solution)/shard_map/ppermute | solution.py:334
  142.8 1.3 collective-permute-start.19
  144.1 3.1 %collective-permute-done.19 = f32[288,128]{1,0:T(8,128)S(1)} collective-permute-done((f32[288,128]{1,0:T(8,128)S(1)}, f32[288,128]{1,0:T(8,128)S(1)}, u32[]{:S(2)}, u32[]{:S(2)}) %collective-permute-start.19) | collective-permute-done | bytes 147488 | tf_op jit(solution)/shard_map/ppermute | solution.py:334
  147.2 1.4 collective-permute-start.20
  148.6 4.3 %collective-permute-done.20 = f32[576,128]{1,0:T(8,128)S(1)} collective-permute-done((f32[576,128]{1,0:T(8,128)S(1)}, f32[576,128]{1,0:T(8,128)S(1)}, u32[]{:S(2)}, u32[]{:S(2)}) %collective-permute-start.20) | collective-permute-done | bytes 294944 | tf_op jit(solution)/shard_map/ppermute | solution.py:334
  153.1 12.2 %collective-permute-start.21 = (f32[1152,128]{1,0:T(8,128)S(1)}, f32[1152,128]{1,0:T(8,128)S(1)}, u32[]{:S(2)}, u32[]{:S(2)}) collective-permute-start(f32[1152,128]{1,0:T(8,128)S(1)} %get-tuple-element.153), channel_id=1, source_target_pairs={{0,8},{8,0},{16,24},{24,16},{32,40},{40,32},{48,56},{56,48},{64,72... | collective-permute-start | bytes 1769480 | tf_op jit(solution)/shard_map/ppermute | solution.py:334
  (188 shorter events, 29.0 us)
Async XLA Ops:
  1.7 13.8 %collective-permute-start.1 = (bf16[4,1,1,4096]{3,2,1,0:T(2,128)(2,1)S(1)}, bf16[4,1,1,4096]{3,2,1,0:T(2,128)(2,1)S(1)}, u32[]{:S(2)}, u32[]{:S(2)}) collective-permute-start(bf16[4,1,1,4096]{3,2,1,0:T(2,128)(2,1)S(1)} %get-tuple-element.194), channel_id=1, source_target_pairs={{1,0},{2,1},{3,2},{4,3},{5,4},{6,5},{7,6},{9,8},{10,9},{11,10},{12... | collective-permute-start | bytes 98312 | tf_op jit(solution)/shard_map/ppermute | solution.py:22
  3.0 12.5 %collective-permute-start = (bf16[4,1,1,4096]{3,2,1,0:T(2,128)(2,1)S(1)}, bf16[4,1,1,4096]{3,2,1,0:T(2,128)(2,1)S(1)}, u32[]{:S(2)}, u32[]{:S(2)}) collective-permute-start(bf16[4,1,1,4096]{3,2,1,0:T(2,128)(2,1)S(1)} %get-tuple-element.193), channel_id=1, source_target_pairs={{0,1},{1,2},{2,3},{3,4},{4,5},{5,6},{6,7},{8,9},{9,10},{10,11},{11... | collective-permute-start | bytes 98312 | tf_op jit(solution)/shard_map/ppermute | solution.py:21
  26.3 5.5 %collective-permute-start.3 = (bf16[32,1,1,1024]{3,0,2,1:T(8,128)(2,1)S(1)}, bf16[32,1,1,1024]{3,0,2,1:T(8,128)(2,1)S(1)}, u32[]{:S(2)}, u32[]{:S(2)}) collective-permute-start(bf16[32,1,1,1024]{3,0,2,1:T(8,128)(2,1)S(1)} %get-tuple-element.192), channel_id=1, source_target_pairs={{1,0},{2,1},{3,2},{4,3},{5,4},{6,5},{7,6},{9,8},{10,9},{11,10},{12... | collective-permute-start | bytes 196616 | tf_op jit(solution)/shard_map/ppermute | solution.py:22
  27.6 5.5 %collective-permute-start.2 = (bf16[32,1,1,1024]{3,0,2,1:T(8,128)(2,1)S(1)}, bf16[32,1,1,1024]{3,0,2,1:T(8,128)(2,1)S(1)}, u32[]{:S(2)}, u32[]{:S(2)}) collective-permute-start(bf16[32,1,1,1024]{3,0,2,1:T(8,128)(2,1)S(1)} %get-tuple-element.191), channel_id=1, source_target_pairs={{0,1},{1,2},{2,3},{3,4},{4,5},{5,6},{6,7},{8,9},{9,10},{10,11},{11... | collective-permute-start | bytes 196616 | tf_op jit(solution)/shard_map/ppermute | solution.py:21
  33.3 2.5 %copy-start.7 = (bf16[27,32,64]{2,1,0:T(8,128)(2,1)S(1)}, bf16[27,32,64]{2,1,0:T(8,128)(2,1)}, u32[]{:S(2)}) copy-start(bf16[27,32,64]{2,1,0:T(8,128)(2,1)} %param.12) | copy-start | bytes 331780
  33.3 2.5 %copy-start.10 = (f32[64]{0:T(128)S(1)}, f32[64]{0:T(128)}, u32[]{:S(2)}) copy-start(f32[64]{0:T(128)} %param.13) | copy-start | bytes 772
  35.8 2.1 %copy-start.9 = (bf16[864,1,2,1024]{3,0,2,1:T(8,128)(2,1)}, bf16[864,1,2,1024]{3,0,2,1:T(8,128)(2,1)S(1)}, u32[]{:S(2)}) copy-start(bf16[864,1,2,1024]{3,0,2,1:T(8,128)(2,1)S(1)} %constant_dynamic-update-slice_fusion) | copy-start | bytes 10616836
  35.8 8.3 %copy-start = (bf16[6,4,36,1024]{3,2,1,0:T(8,128)(2,1)S(1)}, bf16[6,4,36,1024]{3,2,1,0:T(8,128)(2,1)}, u32[]{:S(2)}) copy-start(bf16[6,4,36,1024]{3,2,1,0:T(8,128)(2,1)} %get-tuple-element.83) | copy-start | bytes 5308420
  38.5 7.6 %collective-permute-start.5 = (bf16[64,1,1,256]{0,3,2,1:T(8,128)(2,1)S(1)}, bf16[64,1,1,256]{0,3,2,1:T(8,128)(2,1)S(1)}, u32[]{:S(2)}, u32[]{:S(2)}) collective-permute-start(bf16[64,1,1,256]{0,3,2,1:T(8,128)(2,1)S(1)} %fusion.142), channel_id=1, source_target_pairs={{1,0},{2,1},{3,2},{4,3},{5,4},{6,5},{7,6},{9,8},{10,9},{11,10},{12... | collective-permute-start | bytes 98312 | tf_op jit(solution)/shard_map/ppermute | solution.py:22
  39.8 6.3 %collective-permute-start.4 = (bf16[64,1,1,256]{0,3,2,1:T(8,128)(2,1)S(1)}, bf16[64,1,1,256]{0,3,2,1:T(8,128)(2,1)S(1)}, u32[]{:S(2)}, u32[]{:S(2)}) collective-permute-start(bf16[64,1,1,256]{0,3,2,1:T(8,128)(2,1)S(1)} %fusion.142), channel_id=1, source_target_pairs={{0,1},{1,2},{2,3},{3,4},{4,5},{5,6},{6,7},{8,9},{9,10},{10,11},{11... | collective-permute-start | bytes 98312 | tf_op jit(solution)/shard_map/ppermute | solution.py:21
  46.1 4.6 %copy-start.6 = (bf16[27,64,128]{2,1,0:T(8,128)(2,1)S(1)}, bf16[27,64,128]{2,1,0:T(8,128)(2,1)}, u32[]{:S(2)}) copy-start(bf16[27,64,128]{2,1,0:T(8,128)(2,1)} %param.14) | copy-start | bytes 1327108
  46.1 4.6 %copy-start.11 = (f32[128]{0:T(128)S(1)}, f32[128]{0:T(128)}, u32[]{:S(2)}) copy-start(f32[128]{0:T(128)} %param.15) | copy-start | bytes 1540
  52.7 7.2 %collective-permute-start.7 = (bf16[128,1,1,256]{0,3,2,1:T(8,128)(2,1)S(1)}, bf16[128,1,1,256]{0,3,2,1:T(8,128)(2,1)S(1)}, u32[]{:S(2)}, u32[]{:S(2)}) collective-permute-start(bf16[128,1,1,256]{0,3,2,1:T(8,128)(2,1)S(1)} %get-tuple-element.147), channel_id=1, source_target_pairs={{1,0},{2,1},{3,2},{4,3},{5,4},{6,5},{7,6},{9,8},{10,9},{11,10},{12... | collective-permute-start | bytes 196616 | tf_op jit(solution)/shard_map/ppermute | solution.py:22
  54.0 6.5 %collective-permute-start.6 = (bf16[128,1,1,256]{0,3,2,1:T(8,128)(2,1)S(1)}, bf16[128,1,1,256]{0,3,2,1:T(8,128)(2,1)S(1)}, u32[]{:S(2)}, u32[]{:S(2)}) collective-permute-start(bf16[128,1,1,256]{0,3,2,1:T(8,128)(2,1)S(1)} %get-tuple-element.147), channel_id=1, source_target_pairs={{0,1},{1,2},{2,3},{3,4},{4,5},{5,6},{6,7},{8,9},{9,10},{10,11},{11... | collective-permute-start | bytes 196616 | tf_op jit(solution)/shard_map/ppermute | solution.py:21
  60.8 3.4 %copy-start.5 = (f32[64,2,1024]{2,0,1:T(8,128)S(1)}, f32[64,2,1024]{2,0,1:T(8,128)}, u32[]{:S(2)}) copy-start(f32[64,2,1024]{2,0,1:T(8,128)} %get-tuple-element.196) | copy-start | bytes 1572868
  64.6 10.4 %collective-permute-start.9 = (bf16[64,1,1,1024]{3,0,2,1:T(8,128)(2,1)S(1)}, bf16[64,1,1,1024]{3,0,2,1:T(8,128)(2,1)S(1)}, u32[]{:S(2)}, u32[]{:S(2)}) collective-permute-start(bf16[64,1,1,1024]{3,0,2,1:T(8,128)(2,1)S(1)} %get-tuple-element.162), channel_id=1, source_target_pairs={{1,0},{2,1},{3,2},{4,3},{5,4},{6,5},{7,6},{9,8},{10,9},{11,10},{12... | collective-permute-start | bytes 393224 | tf_op jit(solution)/shard_map/ppermute | solution.py:22
  65.9 9.1 %collective-permute-start.8 = (bf16[64,1,1,1024]{3,0,2,1:T(8,128)(2,1)S(1)}, bf16[64,1,1,1024]{3,0,2,1:T(8,128)(2,1)S(1)}, u32[]{:S(2)}, u32[]{:S(2)}) collective-permute-start(bf16[64,1,1,1024]{3,0,2,1:T(8,128)(2,1)S(1)} %get-tuple-element.161), channel_id=1, source_target_pairs={{0,1},{1,2},{2,3},{3,4},{4,5},{5,6},{6,7},{8,9},{9,10},{10,11},{11... | collective-permute-start | bytes 393224 | tf_op jit(solution)/shard_map/ppermute | solution.py:21
  78.7 2.4 %copy-start.1 = (bf16[32,4,4,1024]{3,2,1,0:T(4,128)(2,1)S(1)}, bf16[32,4,4,1024]{3,2,1,0:T(4,128)(2,1)}, u32[]{:S(2)}) copy-start(bf16[32,4,4,1024]{3,2,1,0:T(4,128)(2,1)} %get-tuple-element.82) | copy-start | bytes 3145732
  81.1 5.3 %copy-start.3 = (bf16[4,4,36,1024]{3,2,1,0:T(8,128)(2,1)S(1)}, bf16[4,4,36,1024]{3,2,1,0:T(8,128)(2,1)}, u32[]{:S(2)}) copy-start(bf16[4,4,36,1024]{3,2,1,0:T(8,128)(2,1)} %get-tuple-element.150) | copy-start | bytes 3538948
  83.4 4.5 %copy-start.2 = (bf16[4,4,36,1024]{3,2,1,0:T(8,128)(2,1)S(1)}, bf16[4,4,36,1024]{3,2,1,0:T(8,128)(2,1)}, u32[]{:S(2)}) copy-start(bf16[4,4,36,1024]{3,2,1,0:T(8,128)(2,1)} %get-tuple-element.148) | copy-start | bytes 3538948
  86.4 3.3 %copy-start.4 = (f32[432,128]{1,0:T(8,128)S(1)}, f32[432,128]{1,0:T(8,128)}, u32[]{:S(2)}) copy-start(f32[432,128]{1,0:T(8,128)} %reshape.391) | copy-start | bytes 663556
  90.2 6.1 %collective-permute-start.10 = (f32[1152,128]{1,0:T(8,128)S(1)}, f32[1152,128]{1,0:T(8,128)S(1)}, u32[]{:S(2)}, u32[]{:S(2)}) collective-permute-start(f32[1152,128]{1,0:T(8,128)S(1)} %constant_dynamic-slice_fusion.3), channel_id=1, source_target_pairs={{0,8},{8,0},{16,24},{24,16},{32,40},{40,32},{48,56},{56,48},{64,72... | collective-permute-start | bytes 1769480 | tf_op jit(solution)/shard_map/ppermute | solution.py:329
  96.4 8.3 %collective-permute-start.11 = (f32[576,128]{1,0:T(8,128)S(1)}, f32[576,128]{1,0:T(8,128)S(1)}, u32[]{:S(2)}, u32[]{:S(2)}) collective-permute-start(f32[576,128]{1,0:T(8,128)S(1)} %constant_dynamic-slice_fusion.2), channel_id=1, source_target_pairs={{0,16},{8,24},{16,0},{24,8},{32,48},{40,56},{48,32},{56,40},{64,80... | collective-permute-start | bytes 884744 | tf_op jit(solution)/shard_map/ppermute | solution.py:329
  104.8 60.6 %copy-start.8 = (f32[128,256]{0,1:T(8,128)S(1)}, f32[128,256]{0,1:T(8,128)}, u32[]{:S(2)}) copy-start(f32[128,256]{0,1:T(8,128)} %get-tuple-element.197) | copy-start | bytes 393220
  104.8 4.1 %collective-permute-start.12 = (f32[288,128]{1,0:T(8,128)S(1)}, f32[288,128]{1,0:T(8,128)S(1)}, u32[]{:S(2)}, u32[]{:S(2)}) collective-permute-start(f32[288,128]{1,0:T(8,128)S(1)} %constant_dynamic-slice_fusion.1), channel_id=1, source_target_pairs={{0,64},{8,72},{16,80},{24,88},{32,96},{40,104},{48,112},{56,120},{... | collective-permute-start | bytes 442376 | tf_op jit(solution)/shard_map/ppermute | solution.py:329
  108.9 4.6 %collective-permute-start.13 = (f32[144,128]{1,0:T(8,128)S(1)}, f32[144,128]{1,0:T(8,128)S(1)}, u32[]{:S(2)}, u32[]{:S(2)}) collective-permute-start(f32[144,128]{1,0:T(8,128)S(1)} %constant_dynamic-slice_fusion), channel_id=1, source_target_pairs={{0,1},{1,0},{2,3},{3,2},{4,5},{5,4},{6,7},{7,6},{8,9},{9,8},{10,11... | collective-permute-start | bytes 221192 | tf_op jit(solution)/shard_map/ppermute | solution.py:329
  113.5 4.8 %collective-permute-start.14 = (f32[144,128]{1,0:T(8,128)S(1)}, f32[144,128]{1,0:T(8,128)S(1)}, u32[]{:S(2)}, u32[]{:S(2)}) collective-permute-start(f32[144,128]{1,0:T(8,128)S(1)} %dynamic-slice_add_fusion.3), channel_id=1, source_target_pairs={{0,32},{8,40},{16,48},{24,56},{32,0},{40,8},{48,16},{56,24},{64,96... | collective-permute-start | bytes 221192 | tf_op jit(solution)/shard_map/ppermute | solution.py:332
  118.3 4.8 %collective-permute-start.15 = (f32[144,128]{1,0:T(8,128)S(1)}, f32[144,128]{1,0:T(8,128)S(1)}, u32[]{:S(2)}, u32[]{:S(2)}) collective-permute-start(f32[144,128]{1,0:T(8,128)S(1)} %add.504), channel_id=1, source_target_pairs={{0,128},{8,136},{16,144},{24,152},{32,160},{40,168},{48,176},{56,1... | collective-permute-start | bytes 221192 | tf_op jit(solution)/shard_map/ppermute | solution.py:332
  123.1 8.0 %collective-permute-start.16 = (f32[144,128]{1,0:T(8,128)S(1)}, f32[144,128]{1,0:T(8,128)S(1)}, u32[]{:S(2)}, u32[]{:S(2)}) collective-permute-start(f32[144,128]{1,0:T(8,128)S(1)} %add.505), channel_id=1, source_target_pairs={{0,2},{1,3},{2,0},{3,1},{4,6},{5,7},{6,4},{7,5},{8,10},{9,11},{10,... | collective-permute-start | bytes 221192 | tf_op jit(solution)/shard_map/ppermute | solution.py:332
  131.1 8.3 %collective-permute-start.17 = (f32[144,128]{1,0:T(8,128)S(1)}, f32[144,128]{1,0:T(8,128)S(1)}, u32[]{:S(2)}, u32[]{:S(2)}) collective-permute-start(f32[144,128]{1,0:T(8,128)S(1)} %add.506), channel_id=1, source_target_pairs={{0,4},{1,5},{2,6},{3,7},{4,0},{5,1},{6,2},{7,3},{8,12},{9,13},{10,... | collective-permute-start | bytes 221192 | tf_op jit(solution)/shard_map/ppermute | solution.py:332
  139.4 3.3 %collective-permute-start.18 = (f32[144,128]{1,0:T(8,128)S(1)}, f32[144,128]{1,0:T(8,128)S(1)}, u32[]{:S(2)}, u32[]{:S(2)}) collective-permute-start(f32[144,128]{1,0:T(8,128)S(1)} %add.507), channel_id=1, source_target_pairs={{0,1},{1,0},{2,3},{3,2},{4,5},{5,4},{6,7},{7,6},{8,9},{9,8},{10,11... | collective-permute-start | bytes 221192 | tf_op jit(solution)/shard_map/ppermute | solution.py:334
  142.8 4.4 %collective-permute-start.19 = (f32[288,128]{1,0:T(8,128)S(1)}, f32[288,128]{1,0:T(8,128)S(1)}, u32[]{:S(2)}, u32[]{:S(2)}) collective-permute-start(f32[288,128]{1,0:T(8,128)S(1)} %get-tuple-element.187), channel_id=1, source_target_pairs={{0,64},{8,72},{16,80},{24,88},{32,96},{40,104},{48,112},{56,120},{... | collective-permute-start | bytes 442376 | tf_op jit(solution)/shard_map/ppermute | solution.py:334
  147.2 5.7 %collective-permute-start.20 = (f32[576,128]{1,0:T(8,128)S(1)}, f32[576,128]{1,0:T(8,128)S(1)}, u32[]{:S(2)}, u32[]{:S(2)}) collective-permute-start(f32[576,128]{1,0:T(8,128)S(1)} %get-tuple-element.157), channel_id=1, source_target_pairs={{0,16},{8,24},{16,0},{24,8},{32,48},{40,56},{48,32},{56,40},{64,80... | collective-permute-start | bytes 884744 | tf_op jit(solution)/shard_map/ppermute | solution.py:334
  153.1 13.9 %collective-permute-start.21 = (f32[1152,128]{1,0:T(8,128)S(1)}, f32[1152,128]{1,0:T(8,128)S(1)}, u32[]{:S(2)}, u32[]{:S(2)}) collective-permute-start(f32[1152,128]{1,0:T(8,128)S(1)} %get-tuple-element.153), channel_id=1, source_target_pairs={{0,8},{8,0},{16,24},{24,16},{32,40},{40,32},{48,56},{56,48},{64,72... | collective-permute-start | bytes 1769480 | tf_op jit(solution)/shard_map/ppermute | solution.py:334
